TPU v7x, 256 devices: a whole 4x4x8 slice. The times are simulated.
256 devices in a mesh: dp: 8 (over z), seq: 32 (over y, x, core).
Axes of the slice: x: 4, y: 4, z: 8, core: 2. Of those that a mesh axis runs over, the one named last changes fastest.
Arguments:
- queries: bfloat16 [8, 8192, 1024], P('dp', 'seq'), may hold values from -150 to 150
- keys: bfloat16 [8, 8192, 1024], P('dp', 'seq'), may hold values from -5 to 5
- values: bfloat16 [8, 8192, 1024], P('dp', 'seq'), may hold values from -5 to 5
- out_weight: bfloat16 [1024, 1024], replicated, may hold values from -0.1875 to 0.1875
- out_grad: bfloat16 [8, 8192, 1024], P('dp', 'seq'), may hold values from -6 to 6
- pooled: int32 [8, 8192], P('dp', 'seq'), may hold values from 0 to 1, as said below
Outputs:
- query_grad: bfloat16 [8, 8192, 1024], P('dp', 'seq')
- key_grad: bfloat16 [8, 8192, 1024], P('dp', 'seq')
- value_grad: bfloat16 [8, 8192, 1024], P('dp', 'seq')
- weight_grad: float32 [1024, 1024], P('seq')
Inputs may be any that keep to these rules, and one draw needn't show every extreme that they name: Every stream has at least one block of 128 tokens in which no token has pooled = 1.
All inputs are finite; a program needn't handle non-finite values.
Results may differ from a plain program's by a relative error of at most 0.035.
Values may be sent and summed in bfloat16 or wider, within the bound.
No kernel may reach another device: no remote copies, remote signals or barrier semaphores. Data moves between devices by JAX's collectives and lax.ppermute only.
A program may use at most 128 MiB of HBM per device.

v0:
```python
import math

import jax
import jax.numpy as jnp
from jax import lax
from jax.experimental import pallas as pl
from jax.experimental.pallas import tpu as pltpu
from jax.sharding import PartitionSpec as P

HEADS = 16
HEAD_DIM = 64
BLOCK = 128


def padded_2(block, sides, width):
    for axis, dim in sides:
        count = lax.axis_size(axis)
        forward = [(i, i + 1) for i in range(count - 1)]
        backward = [(target, source) for source, target in forward]
        low = lax.ppermute(
            lax.slice_in_dim(block, block.shape[dim] - width, None, axis=dim), axis, forward
        )
        high = lax.ppermute(lax.slice_in_dim(block, 0, width, axis=dim), axis, backward)
        block = jnp.concatenate([low, block, high], axis=dim)
    return block


def from_behind(value, axis, steps):
    count = lax.axis_size(axis)
    leading, last = (max(0, -steps), min(count, count - steps))
    return lax.ppermute(value, axis, [(source, source + steps) for source in range(leading, last)])


def xor_pairs(count, bit):
    return [(source, source ^ (1 << bit)) for source in range(count)]


def own_bit(axis, bit):
    return (lax.axis_index(axis) // (1 << bit)) % 2


def doubling_gather(piece, axis):
    count = lax.axis_size(axis)
    bits = count.bit_length() - 1
    held = piece
    for done, bit in enumerate(reversed(range(bits))):
        other = lax.ppermute(held, axis, xor_pairs(count, bit))
        mine_low = own_bit(axis, bit) == 0
        low = jnp.where(mine_low, held, other)
        high = jnp.where(mine_low, other, held)
        held = jnp.stack([low, high], axis=done)
    return held.reshape((count,) + piece.shape)


def halving_scatter(stack, axis):
    count = lax.axis_size(axis)
    bits = count.bit_length() - 1
    held = stack.reshape((2,) * bits + stack.shape[1:])
    for bit in range(bits):
        dim = bits - 1 - bit
        mine = own_bit(axis, bit)
        keep = lax.dynamic_index_in_dim(held, mine, dim, keepdims=False)
        send = lax.dynamic_index_in_dim(held, 1 - mine, dim, keepdims=False)
        held = keep + lax.ppermute(send, axis, xor_pairs(count, bit))
    return held


def doubling_sum(value, axis):
    count = lax.axis_size(axis)
    for bit in range(count.bit_length() - 1):
        value = value + lax.ppermute(value, axis, xor_pairs(count, bit))
    return value


def forward_kernel(q_ref, k_ref, v_ref, ck_ref, cv_ref, counts_ref, fine_ref, far_ref,
                   att_ref, top_ref, total_ref):
    score_scale = 1.0 / math.sqrt(HEAD_DIM)
    lanes = q_ref.shape[1]
    low_lanes = lax.broadcasted_iota(jnp.int32, (BLOCK, lanes), 1) < HEAD_DIM
    coarse_k = ck_ref[...]
    coarse_v = cv_ref[...]
    counts = counts_ref[...]
    contract_last = (((1,), (1,)), ((), ()))
    for block in range(q_ref.shape[0] // BLOCK):
        query = q_ref[pl.ds(block * BLOCK, BLOCK), :]
        key_win = k_ref[pl.ds(block * BLOCK, 3 * BLOCK), :]
        value_win = v_ref[pl.ds(block * BLOCK, 3 * BLOCK), :]
        fine_ok = fine_ref[pl.ds(block, 1), :] > 0
        far_ok = far_ref[pl.ds(block, 1), :] > 0
        halves = []
        for half in range(2):
            own = low_lanes if half == 0 else jnp.logical_not(low_lanes)
            query_h = jnp.where(own, query, jnp.zeros_like(query))
            fine_s = lax.dot_general(query_h, key_win, contract_last,
                                     preferred_element_type=jnp.float32) * score_scale
            coarse_s = lax.dot_general(query_h, coarse_k, contract_last,
                                       preferred_element_type=jnp.float32) * score_scale
            fine_s = jnp.where(fine_ok, fine_s, -jnp.inf)
            coarse_s = jnp.where(far_ok, coarse_s, -jnp.inf)
            top = jnp.maximum(jnp.max(fine_s, axis=1, keepdims=True),
                              jnp.max(coarse_s, axis=1, keepdims=True))
            fine_e = jnp.exp(fine_s - top)
            coarse_e = counts * jnp.exp(coarse_s - top)
            total = (jnp.sum(fine_e, axis=1, keepdims=True)
                     + jnp.sum(coarse_e, axis=1, keepdims=True))
            fine_w = (fine_e / total).astype(jnp.bfloat16)
            coarse_w = (coarse_e / total).astype(jnp.bfloat16)
            att = (jnp.dot(fine_w, value_win, preferred_element_type=jnp.float32)
                   + jnp.dot(coarse_w, coarse_v, preferred_element_type=jnp.float32))
            halves.append((att, top, total))
        rows = pl.ds(block * BLOCK, BLOCK)
        att_ref[rows, :] = jnp.where(low_lanes, halves[0][0], halves[1][0]).astype(att_ref.dtype)
        top_ref[rows, :] = jnp.where(low_lanes, halves[0][1], halves[1][1])
        total_ref[rows, :] = jnp.where(low_lanes, halves[0][2], halves[1][2])


def attention_forward(query_rows, padded_k, padded_v, coarse_k, coarse_v, counts, fine_ok, far_ok):
    tokens, width = query_rows.shape
    lanes = 2 * HEAD_DIM
    by_pair = lambda rows: pl.BlockSpec((rows, lanes), lambda pair: (0, pair))
    whole = lambda shape: pl.BlockSpec(shape, lambda pair: (0, 0))
    stat = jax.ShapeDtypeStruct((tokens, width), jnp.float32)
    return pl.pallas_call(
        forward_kernel,
        grid=(width // lanes,),
        in_specs=[
            by_pair(tokens),
            by_pair(padded_k.shape[0]),
            by_pair(padded_v.shape[0]),
            by_pair(coarse_k.shape[0]),
            by_pair(coarse_v.shape[0]),
            whole(counts.shape),
            whole(fine_ok.shape),
            whole(far_ok.shape),
        ],
        out_specs=[by_pair(tokens), by_pair(tokens), by_pair(tokens)],
        out_shape=[jax.ShapeDtypeStruct((tokens, width), jnp.bfloat16), stat, stat],
    )(query_rows, padded_k, padded_v, coarse_k, coarse_v, counts, fine_ok, far_ok)


def block_windows(padded, local_blocks):
    return jnp.concatenate(
        [padded[0:local_blocks], padded[1 : local_blocks + 1], padded[2 : local_blocks + 2]], axis=1
    )


def fold_windows(grads, local_blocks):
    parts = grads.reshape((local_blocks, 3, BLOCK) + grads.shape[2:])
    edge_zero = jnp.zeros((1,) + parts.shape[2:], jnp.float32)
    left_part = jnp.concatenate([parts[:, 0], edge_zero, edge_zero], axis=0)
    middle = jnp.concatenate([edge_zero, parts[:, 1], edge_zero], axis=0)
    right_part = jnp.concatenate([edge_zero, edge_zero, parts[:, 2]], axis=0)
    return left_part + middle + right_part


def per_device(queries, keys, values, out_weight, out_grad, pooled):
    query_rows = queries[0]
    key_rows = keys[0]
    value_rows = values[0]
    grad_out = out_grad[0]
    tokens, model_width = query_rows.shape
    local_blocks = tokens // BLOCK
    seq_devices = lax.axis_size("seq")
    seq_index = lax.axis_index("seq")
    all_blocks = local_blocks * seq_devices
    score_scale = 1.0 / math.sqrt(HEAD_DIM)
    pooled_mask = pooled[0].reshape(local_blocks, BLOCK).astype(jnp.float32)
    counts = jnp.sum(pooled_mask, axis=1)
    divisor = jnp.maximum(counts, 1.0)
    pooled_bf = pooled_mask.astype(jnp.bfloat16)
    key_sum = jnp.einsum(
        "nb,nbd->nd",
        pooled_bf,
        key_rows.reshape(local_blocks, BLOCK, model_width),
        preferred_element_type=jnp.float32,
    )
    value_sum = jnp.einsum(
        "nb,nbd->nd",
        pooled_bf,
        value_rows.reshape(local_blocks, BLOCK, model_width),
        preferred_element_type=jnp.float32,
    )
    coarse_keys = (key_sum / divisor[:, None]).astype(jnp.bfloat16)
    coarse_values = (value_sum / divisor[:, None]).astype(jnp.bfloat16)
    count_cols = jnp.broadcast_to(counts.astype(jnp.bfloat16)[:, None], (local_blocks, 128))
    packed = jnp.concatenate([coarse_keys, coarse_values, count_cols], axis=1)
    gathered = doubling_gather(packed, "seq").reshape(all_blocks, packed.shape[1])
    gathered_keys = gathered[:, :model_width]
    gathered_values = gathered[:, model_width : 2 * model_width]
    gathered_counts = gathered[:, 2 * model_width].astype(jnp.float32)
    paired = jnp.stack([key_rows, value_rows])
    extended = padded_2(paired, (("seq", 1),), BLOCK)
    padded_kv = extended.reshape(2, local_blocks + 2, BLOCK, HEADS, HEAD_DIM)
    key_win = block_windows(padded_kv[0], local_blocks)
    value_win = block_windows(padded_kv[1], local_blocks)
    query_blk = query_rows.reshape(local_blocks, BLOCK, HEADS, HEAD_DIM)
    coarse_kh = gathered_keys.reshape(all_blocks, HEADS, HEAD_DIM)
    coarse_vh = gathered_values.reshape(all_blocks, HEADS, HEAD_DIM)
    local_ids = seq_index * local_blocks + jnp.arange(local_blocks)
    offsets = jnp.repeat(jnp.arange(3) - 1, BLOCK)
    key_blocks = local_ids[:, None] + offsets[None, :]
    fine_ok = (key_blocks >= 0) & (key_blocks < all_blocks)
    far_ok = jnp.abs(local_ids[:, None] - jnp.arange(all_blocks)[None, :]) >= 2
    fine_s = (
        jnp.einsum("nqhe,nkhe->nhqk", query_blk, key_win, preferred_element_type=jnp.float32)
        * score_scale
    )
    coarse_s = (
        jnp.einsum("nqhe,che->nhqc", query_blk, coarse_kh, preferred_element_type=jnp.float32)
        * score_scale
    )
    fine_s = jnp.where(fine_ok[:, None, None, :], fine_s, -jnp.inf)
    coarse_s = jnp.where(far_ok[:, None, None, :], coarse_s, -jnp.inf)
    padded_rows = extended.reshape(2, (local_blocks + 2) * BLOCK, model_width)
    attended_rows, top_rows, total_rows = attention_forward(
        query_rows,
        padded_rows[0],
        padded_rows[1],
        gathered_keys,
        gathered_values,
        gathered_counts[None, :],
        fine_ok.astype(jnp.float32),
        far_ok.astype(jnp.float32),
    )
    attended = attended_rows.reshape(local_blocks, BLOCK, HEADS, HEAD_DIM)
    head_stat = lambda rows: rows.reshape(local_blocks, BLOCK, HEADS, HEAD_DIM)[..., 0].transpose(0, 2, 1)[..., None]
    row_top = head_stat(top_rows)
    row_total = head_stat(total_rows)
    fine_w = jnp.exp(fine_s - row_top) / row_total
    coarse_w = gathered_counts * jnp.exp(coarse_s - row_top) / row_total
    fine_wb = fine_w.astype(jnp.bfloat16)
    coarse_wb = coarse_w.astype(jnp.bfloat16)
    attended_grad = jnp.dot(grad_out, out_weight, preferred_element_type=jnp.float32).astype(
        jnp.bfloat16
    )
    grad_norm = 1.0 / math.sqrt(seq_devices * tokens)
    full_term = (
        jnp.einsum("to,ti->oi", grad_out, attended_rows, preferred_element_type=jnp.float32)
        * grad_norm
    )
    seq_part = lax.psum_scatter(
        jnp.pad(full_term, ((0, 0), (0, model_width))), "seq", scatter_dimension=0, tiled=True
    )[:, :model_width]
    full_term, attended_grad = lax.optimization_barrier((full_term, attended_grad))
    grad_blk = attended_grad.reshape(local_blocks, BLOCK, HEADS, HEAD_DIM)
    fine_dot = jnp.einsum(
        "nqhe,nkhe->nhqk", grad_blk, value_win, preferred_element_type=jnp.float32
    )
    coarse_dot = jnp.einsum(
        "nqhe,che->nhqc", grad_blk, coarse_vh, preferred_element_type=jnp.float32
    )
    delta_rows = jnp.einsum(
        "nqhe,nqhe->nhq", grad_blk, attended, preferred_element_type=jnp.float32
    )[..., None]
    fine_ds = (fine_w * (fine_dot - delta_rows)).astype(jnp.bfloat16)
    coarse_ds = (coarse_w * (coarse_dot - delta_rows)).astype(jnp.bfloat16)
    query_grad = (
        jnp.einsum("nhqk,nkhe->nqhe", fine_ds, key_win, preferred_element_type=jnp.float32)
        + jnp.einsum("nhqc,che->nqhe", coarse_ds, coarse_kh, preferred_element_type=jnp.float32)
    ) * score_scale
    query_grad = query_grad.astype(jnp.bfloat16).reshape(1, tokens, model_width)
    key_win_grad = (
        jnp.einsum("nhqk,nqhe->nkhe", fine_ds, query_blk, preferred_element_type=jnp.float32)
        * score_scale
    )
    value_win_grad = jnp.einsum(
        "nhqk,nqhe->nkhe", fine_wb, grad_blk, preferred_element_type=jnp.float32
    )
    key_ext = fold_windows(key_win_grad, local_blocks).reshape(local_blocks + 2, BLOCK, model_width)
    value_ext = fold_windows(value_win_grad, local_blocks).reshape(
        local_blocks + 2, BLOCK, model_width
    )
    edge_first = jnp.stack([key_ext[0], value_ext[0]])
    edge_last = jnp.stack([key_ext[local_blocks + 1], value_ext[local_blocks + 1]])
    from_right = from_behind(edge_first, "seq", -1)
    from_left = from_behind(edge_last, "seq", 1)
    zeros_mid = jnp.zeros((2, local_blocks - 1, BLOCK, model_width), jnp.float32)
    boundary = jnp.concatenate([from_left[:, None], zeros_mid], axis=1) + jnp.concatenate(
        [zeros_mid, from_right[:, None]], axis=1
    )
    coarse_key_all = (
        jnp.einsum("nhqc,nqhe->che", coarse_ds, query_blk, preferred_element_type=jnp.float32)
        * score_scale
    )
    coarse_value_all = jnp.einsum(
        "nhqc,nqhe->che", coarse_wb, grad_blk, preferred_element_type=jnp.float32
    )
    coarse_all = jnp.concatenate(
        [
            coarse_key_all.reshape(all_blocks, model_width),
            coarse_value_all.reshape(all_blocks, model_width),
        ],
        axis=1,
    )
    owned_grads = halving_scatter(
        coarse_all.reshape(seq_devices, local_blocks, 2 * model_width), "seq"
    )
    owned_keys = owned_grads[:, :model_width] / divisor[:, None]
    owned_values = owned_grads[:, model_width:] / divisor[:, None]
    spread_keys = owned_keys[:, None, :] * pooled_mask[:, :, None]
    spread_values = owned_values[:, None, :] * pooled_mask[:, :, None]
    key_grad = (
        (key_ext[1 : local_blocks + 1] + boundary[0] + spread_keys)
        .astype(jnp.bfloat16)
        .reshape(1, tokens, model_width)
    )
    value_grad = (
        (value_ext[1 : local_blocks + 1] + boundary[1] + spread_values)
        .astype(jnp.bfloat16)
        .reshape(1, tokens, model_width)
    )
    seq_part, query_grad, key_grad, value_grad = lax.optimization_barrier(
        (seq_part, query_grad, key_grad, value_grad)
    )
    dp_devices = lax.axis_size("dp")
    dp_rows = halving_scatter(seq_part.reshape(dp_devices, -1, model_width), "dp")
    weight_grad = doubling_gather(dp_rows, "dp").reshape(-1, model_width)
    return (query_grad, key_grad, value_grad, weight_grad)


def solution(mesh):
    placed = (
        P("dp", "seq", None),
        P("dp", "seq", None),
        P("dp", "seq", None),
        P(),
        P("dp", "seq", None),
        P("dp", "seq"),
    )
    return jax.shard_map(
        per_device,
        mesh=mesh,
        in_specs=placed,
        out_specs=(
            P("dp", "seq", None),
            P("dp", "seq", None),
            P("dp", "seq", None),
            P("seq", None),
        ),
        check_vma=False,
    )
```

profile of v0, /device:TPU:8, one launch (start us, length us, event | category | flops | bytes accessed | tf_op | source)
XLA Modules:
  0.0 274.8 jit_solution(3664523684646610527)
XLA Ops:
  10.8 2.4 collective-permute-start.2
  16.4 1.9 collective-permute-start
  18.3 5.8 %collective-permute-start.1 = (bf16[2,128,1024]{2,1,0:T(8,128)(2,1)}, bf16[2,128,1024]{2,1,0:T(8,128)(2,1)}, u32[]{:S(2)}, u32[]{:S(2)}) collective-permute-start(bf16[2,128,1024]{2,1,0:T(8,128)(2,1)} %get-tuple-element.59), channel_id=1, source_target_pairs={{1,0},{2,1},{3,2},{4,3},{5,4},{6,5},{7,6},{8,7},{9,8},{10,9},{11,1... | collective-permute-start | bytes 1572872 | tf_op jit(solution)/shard_map/ppermute | solution.py:23
  24.3 5.2 %collective-permute-done.3 = bf16[2,2,2176]{2,1,0:T(2,128)(2,1)S(1)} collective-permute-done((bf16[2,2,2176]{2,1,0:T(2,128)(2,1)S(1)}, bf16[2,2,2176]{2,1,0:T(2,128)(2,1)S(1)}, u32[]{:S(2)}, u32[]{:S(2)}) %collective-permute-start.3) | collective-permute-done | bytes 17440 | tf_op jit(solution)/shard_map/ppermute | solution.py:47
  29.8 5.4 %collective-permute-done.4 = bf16[2,2,2,2176]{3,2,1,0:T(2,128)(2,1)S(1)} collective-permute-done((bf16[2,2,2,2176]{3,2,1,0:T(2,128)(2,1)S(1)}, bf16[2,2,2,2176]{3,2,1,0:T(2,128)(2,1)S(1)}, u32[]{:S(2)}, u32[]{:S(2)}) %collective-permute-start.4) | collective-permute-done | bytes 34848 | tf_op jit(solution)/shard_map/ppermute | solution.py:47
  36.1 3.6 %collective-permute-done.5 = bf16[2,2,2,2,2176]{4,3,2,1,0:T(2,128)(2,1)S(1)} collective-permute-done((bf16[2,2,2,2,2176]{4,3,2,1,0:T(2,128)(2,1)S(1)}, bf16[2,2,2,2,2176]{4,3,2,1,0:T(2,128)(2,1)S(1)}, u32[]{:S(2)}, u32[]{:S(2)}) %collective-permute-start.5) | collective-permute-done | bytes 69664 | tf_op jit(solution)/shard_map/ppermute | solution.py:47
  48.8 15.6 %shard_map.93 = (bf16[256,1024]{1,0:T(8,128)(2,1)}, f32[256,1024]{1,0:T(8,128)}, f32[256,1024]{1,0:T(8,128)}) custom-call(bf16[256,1024]{1,0:T(8,128)(2,1)} %bitcast.265, bf16[512,1024]{1,0:T(8,128)(2,1)} %get-tuple-element.51.k_ref, bf16[512,1024]{1,0:T(8,128)(2,1)} %get-tuple-element.50.v_ref, bf16[64,1024]{1,0:T(8,128)(2,1)} %get-tuple-element.63.ck_ref, ...), custom_call_target="tpu_custom_call" | custom-call | tf_op jit(solution)/shard_map/pallas_call | solution.py:123
  64.5 3.9 %multiply_bitcast_fusion = f32[1024,1024]{0,1:T(8,128)} fusion(bf16[256,1024]{1,0:T(8,128)(2,1)} %get-tuple-element.12, bf16[1,256,1024]{2,1,0:T(8,128)(2,1)} %param.10), kind=kOutput, calls=%fused_computation.4 | convolution fusion | flops 537919488 | bytes 5242880 | tf_op jit(solution)/shard_map/to,ti->oi/dot_general | solution.py:238
  68.4 5.4 %copy.335 = f32[1024,1024]{1,0:T(8,128)} copy(f32[1024,1024]{0,1:T(8,128)} %multiply_bitcast_fusion) | data formatting | bytes 8388608
  73.8 6.7 %pad.10.clone = f32[1024,2048]{1,0:T(8,128)} pad(f32[1024,1024]{1,0:T(8,128)} %copy.335, f32[]{:T(128)} %constant.227.clone.1), padding=0_0x0_1024 | pad | bytes 12582916 | tf_op jit(solution)/shard_map/jit(_pad)/pad | solution.py:242
  80.6 2.0 copy.242
  82.6 2.5 reshape.272
  85.1 2.5 reshape.275
  87.6 2.0 reshape_squeeze.12
  89.5 2.9 %copy.240 = bf16[2,128,16,64]{1,3,2,0:T(8,128)(2,1)} copy(bf16[2,128,16,64]{3,2,1,0:T(8,128)(2,1)} %reshape.272) | data formatting | bytes 1048576 | tf_op jit(solution)/shard_map/slice | solution.py:143
  92.5 2.8 %copy.253 = bf16[2,128,16,64]{1,3,2,0:T(8,128)(2,1)} copy(bf16[2,128,16,64]{3,2,1,0:T(8,128)(2,1)} %reshape.275) | data formatting | bytes 1048576 | tf_op jit(solution)/shard_map/slice | solution.py:143
  95.3 2.6 convolution_convert_fusion
  104.6 2.4 pad_maximum_fusion.11
  107.1 1.9 reshape.274
  118.3 1.8 reshape.276
  134.4 4.2 %exponential_divide_fusion = f32[2,16,384,128]{3,2,1,0:T(8,128)S(1)} fusion(f32[2,16,128]{2,1,0:T(8,128)S(1)} %get-tuple-element.92, f32[2,16,128]{2,1,0:T(8,128)S(1)} %get-tuple-element.93, pred[2,384]{1,0:T(4,128)(4,1)S(1)} %get-tuple-element.37, bf16[2,128,16,64]{1,3,2,0:T(8,128)(2,1)} %copy.241, bf16[2,128,16,64]{1,3,2,0:T(8,128)(2,1)} %copy.240, ...), kind=kOutput, calls=%fused_computation.3 | convolution fusion | flops 212336640 | bytes 8422144 | tf_op jit(solution)/shard_map/nqhe,nkhe->nhqk/dot_general | solution.py:205
  143.0 3.2 %multiply_bitcast_fusion.1 = f32[2,384,16,64]{1,3,2,0:T(8,128)} fusion(bf16[2,16,128,384]{2,3,1,0:T(8,128)(2,1)S(1)} %fusion, bf16[2,128,16,64]{1,0,3,2:T(2,128)(2,1)S(1)} %copy-done.6), kind=kOutput, calls=%fused_computation.6 | convolution fusion | flops 202113024 | bytes 6815744 | tf_op jit(solution)/shard_map/nhqk,nqhe->nkhe/dot_general | solution.py:263
  146.3 5.8 %reshape.256 = f32[2,3,128,16,64]{2,1,4,3,0:T(4,128)} reshape(f32[2,384,16,64]{1,3,2,0:T(8,128)} %multiply_bitcast_fusion.1) | data formatting | bytes 6291456 | tf_op jit(solution)/shard_map/reshape | solution.py:148
  152.1 6.1 %fusion.6 = f32[2,384,16,64]{1,3,2,0:T(8,128)} fusion(bf16[2,128,16,64]{1,0,3,2:T(2,128)(2,1)S(1)} %reshape.251, f32[2,16,384,128]{3,2,1,0:T(8,128)} %copy-done.2), kind=kOutput, calls=%fused_computation.18 | convolution fusion | flops 201326592 | bytes 9961472 | tf_op jit(solution)/shard_map/nhqk,nqhe->nkhe/dot_general | solution.py:266
  158.2 5.8 %reshape.257 = f32[2,3,128,16,64]{2,1,4,3,0:T(4,128)} reshape(f32[2,384,16,64]{1,3,2,0:T(8,128)} %fusion.6) | data formatting | bytes 6291456 | tf_op jit(solution)/shard_map/reshape | solution.py:148
  163.9 8.3 %fusion.72 = (f32[2,1,128,16,64]{2,1,4,3,0:T(1,128)S(1)}, f32[2,1,128,16,64]{2,1,4,3,0:T(1,128)S(1)}, f32[2,1,128,16,64]{2,1,4,3,0:T(1,128)S(1)}) fusion(f32[2,3,128,16,64]{2,1,4,3,0:T(4,128)} %reshape.256), kind=kLoop, calls=%fused_computation.162 | loop fusion | bytes 6291456 | tf_op jit(solution)/shard_map/slice | solution.py:150
  172.3 3.2 %fusion.71 = (f32[2,1,128,16,64]{2,1,4,3,0:T(1,128)S(1)}, f32[2,1,128,16,64]{2,1,4,3,0:T(1,128)S(1)}, f32[2,1,128,16,64]{2,1,4,3,0:T(1,128)S(1)}) fusion(f32[2,3,128,16,64]{2,1,4,3,0:T(4,128)S(1)} %copy-done.3), kind=kLoop, calls=%fused_computation.161 | loop fusion | bytes 6291456 | tf_op jit(solution)/shard_map/slice | solution.py:150
  180.2 5.6 %collective-permute-done.10 = f32[2,2,2,2,2048]{4,3,2,1,0:T(2,128)S(1)} collective-permute-done((f32[2,2,2,2,2048]{4,3,2,1,0:T(2,128)S(1)}, f32[2,2,2,2,2048]{4,3,2,1,0:T(2,128)S(1)}, u32[]{:S(2)}, u32[]{:S(2)}) %collective-permute-start.10) | collective-permute-done | bytes 131104 | tf_op jit(solution)/shard_map/ppermute | solution.py:64
  187.1 1.9 collective-permute-start.7
  189.0 2.8 %collective-permute-done.11 = f32[2,2,2,2048]{3,2,1,0:T(2,128)S(1)} collective-permute-done((f32[2,2,2,2048]{3,2,1,0:T(2,128)S(1)}, f32[2,2,2,2048]{3,2,1,0:T(2,128)S(1)}, u32[]{:S(2)}, u32[]{:S(2)}) %collective-permute-start.11) | collective-permute-done | bytes 65568 | tf_op jit(solution)/shard_map/ppermute | solution.py:64
  193.1 3.0 %collective-permute-start.8 = (f32[2,128,1024]{1,2,0:T(8,128)}, f32[2,128,1024]{1,2,0:T(8,128)}, u32[]{:S(2)}, u32[]{:S(2)}) collective-permute-start(f32[2,128,1024]{1,2,0:T(8,128)} %pad_maximum_fusion.7), channel_id=1, source_target_pairs={{1,0},{2,1},{3,2},{4,3},{5,4},{6,5},{7,6},{8,7},{9,8},{10,9},{11,1... | collective-permute-start | bytes 3145736 | tf_op jit(solution)/shard_map/ppermute | solution.py:31
  196.0 10.0 %collective-permute-done.12 = f32[2,2,2048]{2,1,0:T(2,128)S(1)} collective-permute-done((f32[2,2,2048]{2,1,0:T(2,128)S(1)}, f32[2,2,2048]{2,1,0:T(2,128)S(1)}, u32[]{:S(2)}, u32[]{:S(2)}) %collective-permute-start.12) | collective-permute-done | bytes 32800 | tf_op jit(solution)/shard_map/ppermute | solution.py:64
  210.3 2.0 copy.284
  216.0 2.2 mul.133
  218.2 1.8 mul.134
  221.0 2.2 mul.129
  223.2 1.8 mul.130
  225.0 1.8 fusion.32
  230.1 2.2 collective-permute-start.14
  232.2 2.2 collective-permute-done.14
  234.5 3.8 %collective-permute-start.15 = (f32[2,4,1024]{2,1,0:T(4,128)S(1)}, f32[2,4,1024]{2,1,0:T(4,128)S(1)}, u32[]{:S(2)}, u32[]{:S(2)}) collective-permute-start(f32[2,4,1024]{2,1,0:T(4,128)S(1)} %dynamic-slice_bitcast_fusion.4), channel_id=1, source_target_pairs={{0,64},{32,96},{64,0},{96,32},{128,192},{160,224},{192,128},{224,1... | collective-permute-start | bytes 98312 | tf_op jit(solution)/shard_map/ppermute | solution.py:64
  238.3 1.9 collective-permute-done.15
  240.2 6.5 %collective-permute-start.16 = (f32[4,1024]{1,0:T(4,128)S(1)}, f32[4,1024]{1,0:T(4,128)S(1)}, u32[]{:S(2)}, u32[]{:S(2)}) collective-permute-start(f32[4,1024]{1,0:T(4,128)S(1)} %dynamic-slice_bitcast_fusion.6), channel_id=1, source_target_pairs={{0,128},{32,160},{64,192},{96,224},{128,0},{160,32},{192,64},{224,... | collective-permute-start | bytes 49160 | tf_op jit(solution)/shard_map/ppermute | solution.py:64
  246.7 1.8 collective-permute-done.16
  248.6 5.9 %collective-permute-start.17 = (f32[4,1024]{1,0:T(4,128)S(1)}, f32[4,1024]{1,0:T(4,128)S(1)}, u32[]{:S(2)}, u32[]{:S(2)}) collective-permute-start(f32[4,1024]{1,0:T(4,128)S(1)} %bitcast_add_fusion.8), channel_id=1, source_target_pairs={{0,128},{32,160},{64,192},{96,224},{128,0},{160,32},{192,64},{224,... | collective-permute-start | bytes 49160 | tf_op jit(solution)/shard_map/ppermute | solution.py:47
  256.3 2.8 %collective-permute-start.18 = (f32[2,4,1024]{2,1,0:T(4,128)S(1)}, f32[2,4,1024]{2,1,0:T(4,128)S(1)}, u32[]{:S(2)}, u32[]{:S(2)}) collective-permute-start(f32[2,4,1024]{2,1,0:T(4,128)S(1)} %pad_maximum_fusion.20), channel_id=1, source_target_pairs={{0,64},{32,96},{64,0},{96,32},{128,192},{160,224},{192,128},{224,1... | collective-permute-start | bytes 98312 | tf_op jit(solution)/shard_map/ppermute | solution.py:47
  259.0 2.1 collective-permute-done.18
  263.7 2.0 copy.291
  (185 shorter events, 77.0 us)
Async XLA Ops:
  7.2 88.1 %copy-start = (bf16[1024,1024]{1,0:T(8,128)(2,1)S(1)}, bf16[1024,1024]{1,0:T(8,128)(2,1)}, u32[]{:S(2)}) copy-start(bf16[1024,1024]{1,0:T(8,128)(2,1)} %param.9) | copy-start | bytes 6291460
  7.2 221.5 %reduce-scatter.4.cloned.1.call-start = ((), (), s32[]{:S(2)}) async-start(), calls=%async_computation.1 | async-start | bytes 8650752
  10.8 13.3 %collective-permute-start.2 = (bf16[2,2176]{1,0:T(2,128)(2,1)S(1)}, bf16[2,2176]{1,0:T(2,128)(2,1)S(1)}, u32[]{:S(2)}, u32[]{:S(2)}) collective-permute-start(bf16[2,2176]{1,0:T(2,128)(2,1)S(1)} %pad_maximum_fusion.22), channel_id=1, source_target_pairs={{0,16},{1,17},{2,18},{3,19},{4,20},{5,21},{6,22},{7,23},{8,24},{9,... | collective-permute-start | bytes 26120 | tf_op jit(solution)/shard_map/ppermute | solution.py:47
  16.4 29.6 %collective-permute-start = (bf16[2,128,1024]{2,1,0:T(8,128)(2,1)}, bf16[2,128,1024]{2,1,0:T(8,128)(2,1)}, u32[]{:S(2)}, u32[]{:S(2)}) collective-permute-start(bf16[2,128,1024]{2,1,0:T(8,128)(2,1)} %get-tuple-element.58), channel_id=1, source_target_pairs={{0,1},{1,2},{2,3},{3,4},{4,5},{5,6},{6,7},{7,8},{8,9},{9,10},{10,1... | collective-permute-start | bytes 1572872 | tf_op jit(solution)/shard_map/ppermute | solution.py:20
  18.3 27.6 %collective-permute-start.1 = (bf16[2,128,1024]{2,1,0:T(8,128)(2,1)}, bf16[2,128,1024]{2,1,0:T(8,128)(2,1)}, u32[]{:S(2)}, u32[]{:S(2)}) collective-permute-start(bf16[2,128,1024]{2,1,0:T(8,128)(2,1)} %get-tuple-element.59), channel_id=1, source_target_pairs={{1,0},{2,1},{3,2},{4,3},{5,4},{6,5},{7,6},{8,7},{9,8},{10,9},{11,1... | collective-permute-start | bytes 1572872 | tf_op jit(solution)/shard_map/ppermute | solution.py:23
  24.2 5.4 %collective-permute-start.3 = (bf16[2,2,2176]{2,1,0:T(2,128)(2,1)S(1)}, bf16[2,2,2176]{2,1,0:T(2,128)(2,1)S(1)}, u32[]{:S(2)}, u32[]{:S(2)}) collective-permute-start(bf16[2,2,2176]{2,1,0:T(2,128)(2,1)S(1)} %pad_maximum_fusion.21), channel_id=1, source_target_pairs={{0,8},{1,9},{2,10},{3,11},{4,12},{5,13},{6,14},{7,15},{8,0},{9,1},... | collective-permute-start | bytes 52232 | tf_op jit(solution)/shard_map/ppermute | solution.py:47
  29.7 5.5 %collective-permute-start.4 = (bf16[2,2,2,2176]{3,2,1,0:T(2,128)(2,1)S(1)}, bf16[2,2,2,2176]{3,2,1,0:T(2,128)(2,1)S(1)}, u32[]{:S(2)}, u32[]{:S(2)}) collective-permute-start(bf16[2,2,2,2176]{3,2,1,0:T(2,128)(2,1)S(1)} %pad_maximum_fusion.19), channel_id=1, source_target_pairs={{0,4},{1,5},{2,6},{3,7},{4,0},{5,1},{6,2},{7,3},{8,12},{9,13},{10,... | collective-permute-start | bytes 104456 | tf_op jit(solution)/shard_map/ppermute | solution.py:47
  35.4 4.4 %collective-permute-start.5 = (bf16[2,2,2,2,2176]{4,3,2,1,0:T(2,128)(2,1)S(1)}, bf16[2,2,2,2,2176]{4,3,2,1,0:T(2,128)(2,1)S(1)}, u32[]{:S(2)}, u32[]{:S(2)}) collective-permute-start(bf16[2,2,2,2,2176]{4,3,2,1,0:T(2,128)(2,1)S(1)} %pad_maximum_fusion.17), channel_id=1, source_target_pairs={{0,2},{1,3},{2,0},{3,1},{4,6},{5,7},{6,4},{7,5},{8,10},{9,11},{10,... | collective-permute-start | bytes 208904 | tf_op jit(solution)/shard_map/ppermute | solution.py:47
  40.1 1.9 collective-permute-start.6
  89.5 8.4 %copy-start.15 = (bf16[64,1024]{1,0:T(8,128)(2,1)S(1)}, bf16[64,1024]{1,0:T(8,128)(2,1)}, u32[]{:S(2)}) copy-start(bf16[64,1024]{1,0:T(8,128)(2,1)} %get-tuple-element.63.ck_ref) | copy-start | bytes 393220
  89.5 8.5 %copy-start.14 = (bf16[64,1024]{1,0:T(8,128)(2,1)S(1)}, bf16[64,1024]{1,0:T(8,128)(2,1)}, u32[]{:S(2)}) copy-start(bf16[64,1024]{1,0:T(8,128)(2,1)} %get-tuple-element.62.cv_ref) | copy-start | bytes 393220
  98.1 2.5 copy-start.18
  109.0 4.7 %slice-start = ((f32[2,128,16,64]{1,0,3,2:T(2,128)}), f32[2,128,16,1]{1,0,3,2:T(2,128)S(1)}, s32[]{:S(2)}) async-start(f32[2,128,16,64]{1,0,3,2:T(2,128)} %reshape.249), calls=%async_computation.2 | async-start | bytes 32768 | tf_op jit(solution)/shard_map/slice | solution.py:226
  116.7 6.5 %copy-start.12 = (bf16[2,128,16,64]{1,0,3,2:T(2,128)(2,1)S(1)}, bf16[2,128,16,64]{1,0,3,2:T(2,128)(2,1)}, u32[]{:S(2)}) copy-start(bf16[2,128,16,64]{1,0,3,2:T(2,128)(2,1)} %reshape.252) | copy-start | bytes 1572868
  118.3 5.6 %copy-start.6 = (bf16[2,128,16,64]{1,0,3,2:T(2,128)(2,1)S(1)}, bf16[2,128,16,64]{1,0,3,2:T(2,128)(2,1)}, u32[]{:S(2)}) copy-start(bf16[2,128,16,64]{1,0,3,2:T(2,128)(2,1)} %reshape_squeeze.12) | copy-start | bytes 1572868
  118.3 5.6 %copy-start.22 = (f32[64]{0:T(128)S(1)}, f32[64]{0:T(128)}, u32[]{:S(2)}) copy-start(f32[64]{0:T(128)} %convert_reduce_fusion) | copy-start | bytes 772
  133.4 1.0 copy-start.16
  134.2 44.4 %collective-permute-start.9 = (f32[2,2,2,2,2,2048]{5,4,3,2,1,0:T(2,128)}, f32[2,2,2,2,2,2048]{5,4,3,2,1,0:T(2,128)}, u32[]{:S(2)}, u32[]{:S(2)}) collective-permute-start(f32[2,2,2,2,2,2048]{5,4,3,2,1,0:T(2,128)} %dynamic-slice_bitcast_fusion), channel_id=1, source_target_pairs={{0,1},{1,0},{2,3},{3,2},{4,5},{5,4},{6,7},{7,6},{8,9},{9,8},{10,11... | collective-permute-start | bytes 786440 | tf_op jit(solution)/shard_map/ppermute | solution.py:64
  134.4 4.2 %copy-start.9 = (bf16[2,128,16,64]{1,3,2,0:T(8,128)(2,1)S(1)}, bf16[2,128,16,64]{1,3,2,0:T(8,128)(2,1)}, u32[]{:S(2)}) copy-start(bf16[2,128,16,64]{1,3,2,0:T(8,128)(2,1)} %copy.253) | copy-start | bytes 1572868
  134.4 4.2 %copy-start.10 = (bf16[2,128,16,64]{1,3,2,0:T(8,128)(2,1)S(1)}, bf16[2,128,16,64]{1,3,2,0:T(8,128)(2,1)}, u32[]{:S(2)}) copy-start(bf16[2,128,16,64]{1,3,2,0:T(8,128)(2,1)} %copy.254) | copy-start | bytes 1572868
  138.6 2.7 copy-start.2
  141.3 1.7 copy-start.4
  163.9 8.3 %copy-start.3 = (f32[2,3,128,16,64]{2,1,4,3,0:T(4,128)S(1)}, f32[2,3,128,16,64]{2,1,4,3,0:T(4,128)}, u32[]{:S(2)}) copy-start(f32[2,3,128,16,64]{2,1,4,3,0:T(4,128)} %reshape.257) | copy-start | bytes 9437188
  175.5 1.9 copy-start.5
  175.5 2.0 copy-start.19
  175.6 2.1 copy-start.20
  175.6 2.3 copy-start.21
  177.9 1.0 copy-start.17
  180.0 5.8 %collective-permute-start.10 = (f32[2,2,2,2,2048]{4,3,2,1,0:T(2,128)S(1)}, f32[2,2,2,2,2048]{4,3,2,1,0:T(2,128)S(1)}, u32[]{:S(2)}, u32[]{:S(2)}) collective-permute-start(f32[2,2,2,2,2048]{4,3,2,1,0:T(2,128)S(1)} %dynamic-slice_bitcast_fusion.1), channel_id=1, source_target_pairs={{0,2},{1,3},{2,0},{3,1},{4,6},{5,7},{6,4},{7,5},{8,10},{9,11},{10,... | collective-permute-start | bytes 393224 | tf_op jit(solution)/shard_map/ppermute | solution.py:64
  185.9 5.9 %collective-permute-start.11 = (f32[2,2,2,2048]{3,2,1,0:T(2,128)S(1)}, f32[2,2,2,2048]{3,2,1,0:T(2,128)S(1)}, u32[]{:S(2)}, u32[]{:S(2)}) collective-permute-start(f32[2,2,2,2048]{3,2,1,0:T(2,128)S(1)} %dynamic-slice_bitcast_fusion.3), channel_id=1, source_target_pairs={{0,4},{1,5},{2,6},{3,7},{4,0},{5,1},{6,2},{7,3},{8,12},{9,13},{10,... | collective-permute-start | bytes 196616 | tf_op jit(solution)/shard_map/ppermute | solution.py:64
  187.1 37.9 %collective-permute-start.7 = (f32[2,128,1024]{1,2,0:T(8,128)}, f32[2,128,1024]{1,2,0:T(8,128)}, u32[]{:S(2)}, u32[]{:S(2)}) collective-permute-start(f32[2,128,1024]{1,2,0:T(8,128)} %pad_maximum_fusion.6), channel_id=1, source_target_pairs={{0,1},{1,2},{2,3},{3,4},{4,5},{5,6},{6,7},{7,8},{8,9},{9,10},{10,1... | collective-permute-start | bytes 3145736 | tf_op jit(solution)/shard_map/ppermute | solution.py:31
  191.8 14.2 %collective-permute-start.12 = (f32[2,2,2048]{2,1,0:T(2,128)S(1)}, f32[2,2,2048]{2,1,0:T(2,128)S(1)}, u32[]{:S(2)}, u32[]{:S(2)}) collective-permute-start(f32[2,2,2048]{2,1,0:T(2,128)S(1)} %dynamic-slice_bitcast_fusion.5), channel_id=1, source_target_pairs={{0,8},{1,9},{2,10},{3,11},{4,12},{5,13},{6,14},{7,15},{8,0},{9,1},... | collective-permute-start | bytes 98312 | tf_op jit(solution)/shard_map/ppermute | solution.py:64
  193.1 32.0 %collective-permute-start.8 = (f32[2,128,1024]{1,2,0:T(8,128)}, f32[2,128,1024]{1,2,0:T(8,128)}, u32[]{:S(2)}, u32[]{:S(2)}) collective-permute-start(f32[2,128,1024]{1,2,0:T(8,128)} %pad_maximum_fusion.7), channel_id=1, source_target_pairs={{1,0},{2,1},{3,2},{4,3},{5,4},{6,5},{7,6},{8,7},{9,8},{10,9},{11,1... | collective-permute-start | bytes 3145736 | tf_op jit(solution)/shard_map/ppermute | solution.py:31
  206.1 8.8 %collective-permute-start.13 = (f32[2,2048]{1,0:T(2,128)S(1)}, f32[2,2048]{1,0:T(2,128)S(1)}, u32[]{:S(2)}, u32[]{:S(2)}) collective-permute-start(f32[2,2048]{1,0:T(2,128)S(1)} %dynamic-slice_bitcast_fusion.7), channel_id=1, source_target_pairs={{0,16},{1,17},{2,18},{3,19},{4,20},{5,21},{6,22},{7,23},{8,24},{9,... | collective-permute-start | bytes 49160 | tf_op jit(solution)/shard_map/ppermute | solution.py:64
  225.0 1.9 copy-start.7
  225.0 2.2 copy-start.8
  228.6 34.0 %copy-start.11 = (bf16[1,256,1024]{1,2,0:T(8,128)(2,1)S(1)}, bf16[1,256,1024]{1,2,0:T(8,128)(2,1)}, u32[]{:S(2)}) copy-start(bf16[1,256,1024]{1,2,0:T(8,128)(2,1)} %reshape.255) | copy-start | bytes 1572868
  229.6 37.9 %copy-start.1 = (bf16[1024,1024]{1,0:T(8,128)(2,1)S(1)}, bf16[1024,1024]{1,0:T(8,128)(2,1)}, u32[]{:S(2)}) copy-start(bf16[1024,1024]{1,0:T(8,128)(2,1)} %param.9) | copy-start | bytes 6291460
  230.0 35.7 %copy-start.13 = (bf16[1,256,1024]{1,2,0:T(8,128)(2,1)S(1)}, bf16[1,256,1024]{1,2,0:T(8,128)(2,1)}, u32[]{:S(2)}) copy-start(bf16[1,256,1024]{1,2,0:T(8,128)(2,1)} %get-tuple-element.34) | copy-start | bytes 1572868
  230.1 4.4 %collective-permute-start.14 = (f32[2,2,4,1024]{3,2,1,0:T(4,128)S(1)}, f32[2,2,4,1024]{3,2,1,0:T(4,128)S(1)}, u32[]{:S(2)}, u32[]{:S(2)}) collective-permute-start(f32[2,2,4,1024]{3,2,1,0:T(4,128)S(1)} %dynamic-slice_bitcast_fusion.2), channel_id=1, source_target_pairs={{0,32},{32,0},{64,96},{96,64},{128,160},{160,128},{192,224},{224,1... | collective-permute-start | bytes 196616 | tf_op jit(solution)/shard_map/ppermute | solution.py:64
  234.5 5.7 %collective-permute-start.15 = (f32[2,4,1024]{2,1,0:T(4,128)S(1)}, f32[2,4,1024]{2,1,0:T(4,128)S(1)}, u32[]{:S(2)}, u32[]{:S(2)}) collective-permute-start(f32[2,4,1024]{2,1,0:T(4,128)S(1)} %dynamic-slice_bitcast_fusion.4), channel_id=1, source_target_pairs={{0,64},{32,96},{64,0},{96,32},{128,192},{160,224},{192,128},{224,1... | collective-permute-start | bytes 98312 | tf_op jit(solution)/shard_map/ppermute | solution.py:64
  240.2 8.4 %collective-permute-start.16 = (f32[4,1024]{1,0:T(4,128)S(1)}, f32[4,1024]{1,0:T(4,128)S(1)}, u32[]{:S(2)}, u32[]{:S(2)}) collective-permute-start(f32[4,1024]{1,0:T(4,128)S(1)} %dynamic-slice_bitcast_fusion.6), channel_id=1, source_target_pairs={{0,128},{32,160},{64,192},{96,224},{128,0},{160,32},{192,64},{224,... | collective-permute-start | bytes 49160 | tf_op jit(solution)/shard_map/ppermute | solution.py:64
  248.6 7.6 %collective-permute-start.17 = (f32[4,1024]{1,0:T(4,128)S(1)}, f32[4,1024]{1,0:T(4,128)S(1)}, u32[]{:S(2)}, u32[]{:S(2)}) collective-permute-start(f32[4,1024]{1,0:T(4,128)S(1)} %bitcast_add_fusion.8), channel_id=1, source_target_pairs={{0,128},{32,160},{64,192},{96,224},{128,0},{160,32},{192,64},{224,... | collective-permute-start | bytes 49160 | tf_op jit(solution)/shard_map/ppermute | solution.py:47
  256.3 4.9 %collective-permute-start.18 = (f32[2,4,1024]{2,1,0:T(4,128)S(1)}, f32[2,4,1024]{2,1,0:T(4,128)S(1)}, u32[]{:S(2)}, u32[]{:S(2)}) collective-permute-start(f32[2,4,1024]{2,1,0:T(4,128)S(1)} %pad_maximum_fusion.20), channel_id=1, source_target_pairs={{0,64},{32,96},{64,0},{96,32},{128,192},{160,224},{192,128},{224,1... | collective-permute-start | bytes 98312 | tf_op jit(solution)/shard_map/ppermute | solution.py:47
  261.2 5.5 %collective-permute-start.19 = (f32[2,2,4,1024]{3,2,1,0:T(4,128)S(1)}, f32[2,2,4,1024]{3,2,1,0:T(4,128)S(1)}, u32[]{:S(2)}, u32[]{:S(2)}) collective-permute-start(f32[2,2,4,1024]{3,2,1,0:T(4,128)S(1)} %pad_maximum_fusion.18), channel_id=1, source_target_pairs={{0,32},{32,0},{64,96},{96,64},{128,160},{160,128},{192,224},{224,1... | collective-permute-start | bytes 196616 | tf_op jit(solution)/shard_map/ppermute | solution.py:47
Sparse Core Ops, SparseCore 0:
  80.6 99.0 reduce-scatter.3
where the time goes:
time: 280 us; the launch traced here: 275 us
  local copies, waits for them, and re-layouts  114 us (41%)
  waiting for transfers between devices  43.3 us (15%)
  starting transfers between devices  39.8 us (14%)
  matrix products  28.9 us (10%)
  other arithmetic  17.7 us (6%)
  Pallas kernels  15.6 us (6%)
  between operations  15.4 us (6%)
    ppermute x8, waiting for transfers between devices, halving_scatter(): held = keep + lax.ppermute(send, axis, xor_pairs(count, bit))  24.4 us
    ppermute x8, waiting for transfers between devices, doubling_gather(): other = lax.ppermute(held, axis, xor_pairs(count, bit))  18.9 us
    unnamed x53, local copies, waits for them, and re-layouts  18.2 us
    pallas_call x1, Pallas kernels, attention_forward(): pl.pallas_call(forward_kernel, grid=(width // lanes,), in_specs=[by_pair(...  15.6 us
    ppermute x8, starting transfers between devices, halving_scatter(): held = keep + lax.ppermute(send, axis, xor_pairs(count, bit))  14 us
    ppermute x8, starting transfers between devices, doubling_gather(): other = lax.ppermute(held, axis, xor_pairs(count, bit))  13.3 us
    reshape x2, local copies, waits for them, and re-layouts, fold_windows(): parts = grads.reshape((local_blocks, 3, BLOCK) + grads.shape[2:])  11.6 us
    slice x2, local copies, waits for them, and re-layouts, fold_windows(): left_part = jnp.concatenate([parts[:, 0], edge_zero, edge_zero], axis=0)  11.5 us
  transfers between devices with their start and end apart: 21, of which 12 were waited for; matrix products, arithmetic and copies ran while one was open for 48% of the time, Pallas kernels for 0%

commit v1 on v0

--- a/solution.py
+++ b/solution.py
@@ -138,6 +138,123 @@
     )(query_rows, padded_k, padded_v, coarse_k, coarse_v, counts, fine_ok, far_ok)
 
 
+def backward_kernel(q_ref, k_ref, v_ref, ck_ref, cv_ref, counts_ref, fine_ref, far_ref,
+                    g_ref, att_ref, qg_ref, kg_ref, vg_ref, ckg_ref, cvg_ref):
+    score_scale = 1.0 / math.sqrt(HEAD_DIM)
+    lanes = q_ref.shape[1]
+    low_lanes = lax.broadcasted_iota(jnp.int32, (BLOCK, lanes), 1) < HEAD_DIM
+    coarse_k = ck_ref[...]
+    coarse_v = cv_ref[...]
+    counts = counts_ref[...]
+    contract_last = (((1,), (1,)), ((), ()))
+    kg_ref[...] = jnp.zeros_like(kg_ref)
+    vg_ref[...] = jnp.zeros_like(vg_ref)
+    coarse_kg = jnp.zeros(ckg_ref.shape, jnp.float32)
+    coarse_vg = jnp.zeros(cvg_ref.shape, jnp.float32)
+    for block in range(q_ref.shape[0] // BLOCK):
+        rows = pl.ds(block * BLOCK, BLOCK)
+        window = pl.ds(block * BLOCK, 3 * BLOCK)
+        query = q_ref[rows, :]
+        grad = g_ref[rows, :]
+        att = att_ref[rows, :].astype(jnp.float32)
+        key_win = k_ref[window, :]
+        value_win = v_ref[window, :]
+        fine_ok = fine_ref[pl.ds(block, 1), :] > 0
+        far_ok = far_ref[pl.ds(block, 1), :] > 0
+        query_grads = []
+        key_grad = jnp.zeros((3 * BLOCK, lanes), jnp.float32)
+        value_grad = jnp.zeros((3 * BLOCK, lanes), jnp.float32)
+        for half in range(2):
+            own = low_lanes if half == 0 else jnp.logical_not(low_lanes)
+            query_h = jnp.where(own, query, jnp.zeros_like(query))
+            grad_h = jnp.where(own, grad, jnp.zeros_like(grad))
+            fine_s = lax.dot_general(query_h, key_win, contract_last,
+                                     preferred_element_type=jnp.float32) * score_scale
+            coarse_s = lax.dot_general(query_h, coarse_k, contract_last,
+                                       preferred_element_type=jnp.float32) * score_scale
+            fine_s = jnp.where(fine_ok, fine_s, -jnp.inf)
+            coarse_s = jnp.where(far_ok, coarse_s, -jnp.inf)
+            top = jnp.maximum(jnp.max(fine_s, axis=1, keepdims=True),
+                              jnp.max(coarse_s, axis=1, keepdims=True))
+            fine_e = jnp.exp(fine_s - top)
+            coarse_e = counts * jnp.exp(coarse_s - top)
+            total = (jnp.sum(fine_e, axis=1, keepdims=True)
+                     + jnp.sum(coarse_e, axis=1, keepdims=True))
+            fine_w = fine_e / total
+            coarse_w = coarse_e / total
+            fine_dot = lax.dot_general(grad_h, value_win, contract_last,
+                                       preferred_element_type=jnp.float32)
+            coarse_dot = lax.dot_general(grad_h, coarse_v, contract_last,
+                                         preferred_element_type=jnp.float32)
+            delta = jnp.sum(jnp.where(own, grad.astype(jnp.float32) * att, 0.0),
+                            axis=1, keepdims=True)
+            fine_ds = fine_w * (fine_dot - delta)
+            coarse_ds = coarse_w * (coarse_dot - delta)
+            fine_ds_b = fine_ds.astype(jnp.bfloat16)
+            coarse_ds_b = coarse_ds.astype(jnp.bfloat16)
+            query_grads.append(
+                (jnp.dot(fine_ds_b, key_win, preferred_element_type=jnp.float32)
+                 + jnp.dot(coarse_ds_b, coarse_k, preferred_element_type=jnp.float32))
+                * score_scale)
+            fine_ds_t = fine_ds.T.astype(jnp.bfloat16)
+            coarse_ds_t = coarse_ds.T.astype(jnp.bfloat16)
+            fine_w_t = fine_w.T.astype(jnp.bfloat16)
+            coarse_w_t = coarse_w.T.astype(jnp.bfloat16)
+            key_grad = key_grad + jnp.dot(fine_ds_t, query_h,
+                                          preferred_element_type=jnp.float32) * score_scale
+            value_grad = value_grad + jnp.dot(fine_w_t, grad_h,
+                                              preferred_element_type=jnp.float32)
+            coarse_kg = coarse_kg + jnp.dot(coarse_ds_t, query_h,
+                                            preferred_element_type=jnp.float32) * score_scale
+            coarse_vg = coarse_vg + jnp.dot(coarse_w_t, grad_h,
+                                            preferred_element_type=jnp.float32)
+        qg_ref[rows, :] = jnp.where(low_lanes, query_grads[0], query_grads[1]).astype(qg_ref.dtype)
+        kg_ref[window, :] += key_grad
+        vg_ref[window, :] += value_grad
+    ckg_ref[...] = coarse_kg
+    cvg_ref[...] = coarse_vg
+
+
+def attention_backward(query_rows, padded_k, padded_v, coarse_k, coarse_v, counts, fine_ok,
+                       far_ok, grad_rows, attended_rows):
+    tokens, width = query_rows.shape
+    lanes = 2 * HEAD_DIM
+    by_pair = lambda rows: pl.BlockSpec((rows, lanes), lambda pair: (0, pair))
+    whole = lambda shape: pl.BlockSpec(shape, lambda pair: (0, 0))
+    wide = lambda rows: jax.ShapeDtypeStruct((rows, width), jnp.float32)
+    return pl.pallas_call(
+        backward_kernel,
+        grid=(width // lanes,),
+        in_specs=[
+            by_pair(tokens),
+            by_pair(padded_k.shape[0]),
+            by_pair(padded_v.shape[0]),
+            by_pair(coarse_k.shape[0]),
+            by_pair(coarse_v.shape[0]),
+            whole(counts.shape),
+            whole(fine_ok.shape),
+            whole(far_ok.shape),
+            by_pair(tokens),
+            by_pair(tokens),
+        ],
+        out_specs=[
+            by_pair(tokens),
+            by_pair(padded_k.shape[0]),
+            by_pair(padded_v.shape[0]),
+            by_pair(coarse_k.shape[0]),
+            by_pair(coarse_v.shape[0]),
+        ],
+        out_shape=[
+            jax.ShapeDtypeStruct((tokens, width), jnp.bfloat16),
+            wide(padded_k.shape[0]),
+            wide(padded_v.shape[0]),
+            wide(coarse_k.shape[0]),
+            wide(coarse_v.shape[0]),
+        ],
+    )(query_rows, padded_k, padded_v, coarse_k, coarse_v, counts, fine_ok, far_ok, grad_rows,
+      attended_rows)
+
+
 def block_windows(padded, local_blocks):
     return jnp.concatenate(
         [padded[0:local_blocks], padded[1 : local_blocks + 1], padded[2 : local_blocks + 2]], axis=1
@@ -242,34 +359,21 @@
         jnp.pad(full_term, ((0, 0), (0, model_width))), "seq", scatter_dimension=0, tiled=True
     )[:, :model_width]
     full_term, attended_grad = lax.optimization_barrier((full_term, attended_grad))
-    grad_blk = attended_grad.reshape(local_blocks, BLOCK, HEADS, HEAD_DIM)
-    fine_dot = jnp.einsum(
-        "nqhe,nkhe->nhqk", grad_blk, value_win, preferred_element_type=jnp.float32
-    )
-    coarse_dot = jnp.einsum(
-        "nqhe,che->nhqc", grad_blk, coarse_vh, preferred_element_type=jnp.float32
-    )
-    delta_rows = jnp.einsum(
-        "nqhe,nqhe->nhq", grad_blk, attended, preferred_element_type=jnp.float32
-    )[..., None]
-    fine_ds = (fine_w * (fine_dot - delta_rows)).astype(jnp.bfloat16)
-    coarse_ds = (coarse_w * (coarse_dot - delta_rows)).astype(jnp.bfloat16)
-    query_grad = (
-        jnp.einsum("nhqk,nkhe->nqhe", fine_ds, key_win, preferred_element_type=jnp.float32)
-        + jnp.einsum("nhqc,che->nqhe", coarse_ds, coarse_kh, preferred_element_type=jnp.float32)
-    ) * score_scale
-    query_grad = query_grad.astype(jnp.bfloat16).reshape(1, tokens, model_width)
-    key_win_grad = (
-        jnp.einsum("nhqk,nqhe->nkhe", fine_ds, query_blk, preferred_element_type=jnp.float32)
-        * score_scale
-    )
-    value_win_grad = jnp.einsum(
-        "nhqk,nqhe->nkhe", fine_wb, grad_blk, preferred_element_type=jnp.float32
-    )
-    key_ext = fold_windows(key_win_grad, local_blocks).reshape(local_blocks + 2, BLOCK, model_width)
-    value_ext = fold_windows(value_win_grad, local_blocks).reshape(
-        local_blocks + 2, BLOCK, model_width
-    )
+    query_grad, key_pad, value_pad, coarse_key_all, coarse_value_all = attention_backward(
+        query_rows,
+        padded_rows[0],
+        padded_rows[1],
+        gathered_keys,
+        gathered_values,
+        gathered_counts[None, :],
+        fine_ok.astype(jnp.float32),
+        far_ok.astype(jnp.float32),
+        attended_grad,
+        attended_rows,
+    )
+    query_grad = query_grad.reshape(1, tokens, model_width)
+    key_ext = key_pad.reshape(local_blocks + 2, BLOCK, model_width)
+    value_ext = value_pad.reshape(local_blocks + 2, BLOCK, model_width)
     edge_first = jnp.stack([key_ext[0], value_ext[0]])
     edge_last = jnp.stack([key_ext[local_blocks + 1], value_ext[local_blocks + 1]])
     from_right = from_behind(edge_first, "seq", -1)
@@ -277,13 +381,6 @@
     zeros_mid = jnp.zeros((2, local_blocks - 1, BLOCK, model_width), jnp.float32)
     boundary = jnp.concatenate([from_left[:, None], zeros_mid], axis=1) + jnp.concatenate(
         [zeros_mid, from_right[:, None]], axis=1
-    )
-    coarse_key_all = (
-        jnp.einsum("nhqc,nqhe->che", coarse_ds, query_blk, preferred_element_type=jnp.float32)
-        * score_scale
-    )
-    coarse_value_all = jnp.einsum(
-        "nhqc,nqhe->che", coarse_wb, grad_blk, preferred_element_type=jnp.float32
     )
     coarse_all = jnp.concatenate(
         [

time: 280 us -> 224 us (0.80); the launches traced: 275 us -> 224 us
  local copies, waits for them, and re-layouts: 114 us -> 23.1 us
  waiting for transfers between devices: 43.3 us -> 91.3 us
  matrix products: 28.9 us -> 7.73 us
  Pallas kernels: 15.6 us -> 36.1 us
  other arithmetic: 17.7 us -> 12.9 us
    unnamed x2, waiting for transfers between devices: 0.02 us -> 41 us
    slice x23 -> x0, local copies, waits for them, and re-layouts: 39.4 us -> none  [the longest x2 11.5 us: fold_windows(): left_part = jnp.concatenate([parts[:, 0], edge_zero, edge_zero], axis=0)]
    pallas_call x0 -> x1, Pallas kernels: none -> 20.4 us  [attention_backward(): pl.pallas_call(backward_kernel, grid=(width // lanes,), in_specs=[by_pair...]
    dot_general x10 -> x0, matrix products: 19.9 us -> none  [the longest x1 6.09 us: per_device(): jnp.einsum('nhqk,nqhe->nkhe', fine_wb, grad_blk, preferred_element_type=j...]
    reshape x10 -> x0, local copies, waits for them, and re-layouts: 18.2 us -> none  [the longest x2 11.6 us: fold_windows(): parts = grads.reshape((local_blocks, 3, BLOCK) + grads.shape[2:])]
    unnamed x53 -> x12, local copies, waits for them, and re-layouts: 18.2 us -> 7.72 us
    mul x5 -> x0, local copies, waits for them, and re-layouts: 8.29 us -> none  [the longest x2 4 us: per_device(): spread_keys = owned_keys[:, None, :] * pooled_mask[:, :, None]]
    ppermute x8, waiting for transfers between devices: 24.4 us -> 29.1 us  [halving_scatter(): held = keep + lax.ppermute(send, axis, xor_pairs(count, bit))]
  transfers between devices with their start and end apart: 21 -> 21, of which waited for: 12 -> 16; matrix products, arithmetic and copies ran while one was open for 48% -> 8% of each run, Pallas kernels for 0% -> 9%
where the time goes in v1:
time: 224 us
  waiting for transfers between devices  91.3 us (41%)
  starting transfers between devices  37.9 us (17%)
  Pallas kernels  36.1 us (16%)
  local copies, waits for them, and re-layouts  23.1 us (10%)
  between operations  14.6 us (7%)
  other arithmetic  12.9 us (6%)
  matrix products  7.73 us (3%)
    unnamed x2, waiting for transfers between devices  41 us
    ppermute x8, waiting for transfers between devices, halving_scatter(): held = keep + lax.ppermute(send, axis, xor_pairs(count, bit))  29.1 us
    ppermute x8, waiting for transfers between devices, doubling_gather(): other = lax.ppermute(held, axis, xor_pairs(count, bit))  21.2 us
    pallas_call x1, Pallas kernels, attention_backward(): pl.pallas_call(backward_kernel, grid=(width // lanes,), in_specs=[by_pair...  20.4 us
    pallas_call x1, Pallas kernels, attention_forward(): pl.pallas_call(forward_kernel, grid=(width // lanes,), in_specs=[by_pair(...  15.7 us
    ppermute x8, starting transfers between devices, doubling_gather(): other = lax.ppermute(held, axis, xor_pairs(count, bit))  13.4 us
    ppermute x8, starting transfers between devices, halving_scatter(): held = keep + lax.ppermute(send, axis, xor_pairs(count, bit))  12.9 us
    unnamed x12, local copies, waits for them, and re-layouts  7.72 us
  transfers between devices with their start and end apart: 21, of which 16 were waited for; matrix products, arithmetic and copies ran while one was open for 8% of the time, Pallas kernels for 9%

profile of v1, /device:TPU:8, one launch (start us, length us, event | category | flops | bytes accessed | tf_op | source)
XLA Modules:
  0.0 223.5 jit_solution(9516435098902615550)
XLA Ops:
  7.2 0.8 convert_element_type.73
  8.2 1.2 fusion.19
  9.4 1.2 fusion.21
  10.8 2.4 %collective-permute-start.2 = (bf16[2,2176]{1,0:T(2,128)(2,1)S(1)}, bf16[2,2176]{1,0:T(2,128)(2,1)S(1)}, u32[]{:S(2)}, u32[]{:S(2)}) collective-permute-start(bf16[2,2176]{1,0:T(2,128)(2,1)S(1)} %pad_maximum_fusion.12), channel_id=1, source_target_pairs={{0,16},{1,17},{2,18},{3,19},{4,20},{5,21},{6,22},{7,23},{8,24},{9,... | collective-permute-start | bytes 26120 | tf_op jit(solution)/shard_map/ppermute | solution.py:47
  13.2 1.1 constant_dynamic-update-slice_fusion.1
  14.3 1.0 fusion.23
  15.4 1.9 collective-permute-start
  17.3 5.8 %collective-permute-start.1 = (bf16[2,128,1024]{2,1,0:T(8,128)(2,1)}, bf16[2,128,1024]{2,1,0:T(8,128)(2,1)}, u32[]{:S(2)}, u32[]{:S(2)}) collective-permute-start(bf16[2,128,1024]{2,1,0:T(8,128)(2,1)} %get-tuple-element.35), channel_id=1, source_target_pairs={{1,0},{2,1},{3,2},{4,3},{5,4},{6,5},{7,6},{8,7},{9,8},{10,9},{11,1... | collective-permute-start | bytes 1572872 | tf_op jit(solution)/shard_map/ppermute | solution.py:23
  23.3 5.2 %collective-permute-done.3 = bf16[2,2,2176]{2,1,0:T(2,128)(2,1)S(1)} collective-permute-done((bf16[2,2,2176]{2,1,0:T(2,128)(2,1)S(1)}, bf16[2,2,2176]{2,1,0:T(2,128)(2,1)S(1)}, u32[]{:S(2)}, u32[]{:S(2)}) %collective-permute-start.3) | collective-permute-done | bytes 17440 | tf_op jit(solution)/shard_map/ppermute | solution.py:47
  28.8 5.4 %collective-permute-done.4 = bf16[2,2,2,2176]{3,2,1,0:T(2,128)(2,1)S(1)} collective-permute-done((bf16[2,2,2,2176]{3,2,1,0:T(2,128)(2,1)S(1)}, bf16[2,2,2,2176]{3,2,1,0:T(2,128)(2,1)S(1)}, u32[]{:S(2)}, u32[]{:S(2)}) %collective-permute-start.4) | collective-permute-done | bytes 34848 | tf_op jit(solution)/shard_map/ppermute | solution.py:47
  35.1 3.6 %collective-permute-done.5 = bf16[2,2,2,2,2176]{4,3,2,1,0:T(2,128)(2,1)S(1)} collective-permute-done((bf16[2,2,2,2,2176]{4,3,2,1,0:T(2,128)(2,1)S(1)}, bf16[2,2,2,2,2176]{4,3,2,1,0:T(2,128)(2,1)S(1)}, u32[]{:S(2)}, u32[]{:S(2)}) %collective-permute-start.5) | collective-permute-done | bytes 69664 | tf_op jit(solution)/shard_map/ppermute | solution.py:47
  40.9 1.1 pad_maximum_fusion.4
  42.0 1.1 reshape_reshape.12
  44.5 1.4 pad_maximum_fusion
  45.8 1.5 slice_bitcast_fusion
  47.3 15.7 %shard_map.93 = (bf16[256,1024]{1,0:T(8,128)(2,1)}, f32[256,1024]{1,0:T(8,128)}, f32[256,1024]{1,0:T(8,128)}) custom-call(bf16[256,1024]{1,0:T(8,128)(2,1)} %bitcast.142, bf16[512,1024]{1,0:T(8,128)(2,1)} %get-tuple-element.33.k_ref, bf16[512,1024]{1,0:T(8,128)(2,1)} %get-tuple-element.32.v_ref, bf16[64,1024]{1,0:T(8,128)(2,1)} %get-tuple-element.39.ck_ref, ...), custom_call_target="tpu_custom_call" | custom-call | tf_op jit(solution)/shard_map/pallas_call | solution.py:123
  63.0 3.8 %multiply_bitcast_fusion = f32[1024,1024]{0,1:T(8,128)} fusion(bf16[256,1024]{1,0:T(8,128)(2,1)} %get-tuple-element.15.att_ref, bf16[1,256,1024]{2,1,0:T(8,128)(2,1)S(1)} %copy-done.4), kind=kOutput, calls=%fused_computation | convolution fusion | flops 537919488 | bytes 5242880 | tf_op jit(solution)/shard_map/to,ti->oi/dot_general | solution.py:355
  66.8 5.4 %copy.56 = f32[1024,1024]{1,0:T(8,128)} copy(f32[1024,1024]{0,1:T(8,128)} %multiply_bitcast_fusion) | data formatting | bytes 8388608
  72.2 6.6 %pad.6.clone = f32[1024,2048]{1,0:T(8,128)} pad(f32[1024,1024]{1,0:T(8,128)} %copy.56, f32[]{:T(128)} %constant.219.clone.1), padding=0_0x0_1024 | pad | bytes 12582916 | tf_op jit(solution)/shard_map/jit(_pad)/pad | solution.py:359
  78.9 1.5 convolution_convert_fusion.g_ref
  80.4 20.4 %shard_map.94 = (bf16[256,1024]{1,0:T(8,128)(2,1)}, f32[512,1024]{1,0:T(8,128)}, f32[512,1024]{1,0:T(8,128)}, f32[64,1024]{1,0:T(8,128)}, f32[64,1024]{1,0:T(8,128)}) custom-call(bf16[256,1024]{1,0:T(8,128)(2,1)} %bitcast.143, bf16[512,1024]{1,0:T(8,128)(2,1)} %get-tuple-element.33.k_ref, bf16[512,1024]{1,0:T(8,128)(2,1)} %get-tuple-element.32.v_ref, ...), custom_call_target="tpu_custom_call" | custom-call | tf_op jit(solution)/shard_map/pallas_call | solution.py:225
  100.7 1.1 pad_maximum_fusion.3
  102.5 1.4 collective-permute-done.9
  104.3 1.7 slice_bitcast_fusion.2
  106.1 3.8 %collective-permute-done.10 = f32[2,2,2,2,2048]{4,3,2,1,0:T(2,128)S(1)} collective-permute-done((f32[2,2,2,2,2048]{4,3,2,1,0:T(2,128)S(1)}, f32[2,2,2,2,2048]{4,3,2,1,0:T(2,128)S(1)}, u32[]{:S(2)}, u32[]{:S(2)}) %collective-permute-start.10) | collective-permute-done | bytes 131104 | tf_op jit(solution)/shard_map/ppermute | solution.py:64
  110.1 1.9 collective-permute-start.7
  112.1 3.7 %collective-permute-done.11 = f32[2,2,2,2048]{3,2,1,0:T(2,128)S(1)} collective-permute-done((f32[2,2,2,2048]{3,2,1,0:T(2,128)S(1)}, f32[2,2,2,2048]{3,2,1,0:T(2,128)S(1)}, u32[]{:S(2)}, u32[]{:S(2)}) %collective-permute-start.11) | collective-permute-done | bytes 65568 | tf_op jit(solution)/shard_map/ppermute | solution.py:64
  116.0 1.1 pad_maximum_fusion.2
  117.0 2.0 collective-permute-start.8
  119.1 9.8 %collective-permute-done.12 = f32[2,2,2048]{2,1,0:T(2,128)S(1)} collective-permute-done((f32[2,2,2048]{2,1,0:T(2,128)S(1)}, f32[2,2,2048]{2,1,0:T(2,128)S(1)}, u32[]{:S(2)}, u32[]{:S(2)}) %collective-permute-start.12) | collective-permute-done | bytes 32800 | tf_op jit(solution)/shard_map/ppermute | solution.py:64
  128.9 1.4 collective-permute-start.13
  130.3 3.9 %collective-permute-done.13 = f32[2,2048]{1,0:T(2,128)S(1)} collective-permute-done((f32[2,2048]{1,0:T(2,128)S(1)}, f32[2,2048]{1,0:T(2,128)S(1)}, u32[]{:S(2)}, u32[]{:S(2)}) %collective-permute-start.13) | collective-permute-done | bytes 16416 | tf_op jit(solution)/shard_map/ppermute | solution.py:64
  134.4 2.4 %pad_add_fusion = (f32[1,2,128,1024]{3,2,0,1:T(8,128)S(1)}, f32[1,2,128,1024]{3,2,0,1:T(8,128)S(1)}) fusion(f32[2,1,128,1024]{3,2,0,1:T(8,128)} %bitcast.32, f32[2,1,128,1024]{3,2,0,1:T(8,128)} %bitcast.29), kind=kLoop, calls=%fused_computation.6 | loop fusion | flops 524288 | bytes 4194304 | tf_op jit(solution)/shard_map/add | solution.py:382
  138.0 1.3 fusion.2
  139.3 41.0 %reduce-scatter.4.cloned.1.call-done = f32[32,2048]{1,0:T(8,128)} async-done(((f32[1024,2048]{1,0:T(8,128)}), f32[32,2048]{1,0:T(8,128)}) %reduce-scatter.4.cloned.1.call-update) | async-done | bytes 262160
  180.2 0.9 slice.99
  181.6 1.7 collective-permute-start.14
  183.3 2.7 %collective-permute-done.14 = f32[2,2,4,1024]{3,2,1,0:T(4,128)S(1)} collective-permute-done((f32[2,2,4,1024]{3,2,1,0:T(4,128)S(1)}, f32[2,2,4,1024]{3,2,1,0:T(4,128)S(1)}, u32[]{:S(2)}, u32[]{:S(2)}) %collective-permute-start.14) | collective-permute-done | bytes 65568 | tf_op jit(solution)/shard_map/ppermute | solution.py:64
  186.0 2.9 %collective-permute-start.15 = (f32[2,4,1024]{2,1,0:T(4,128)S(1)}, f32[2,4,1024]{2,1,0:T(4,128)S(1)}, u32[]{:S(2)}, u32[]{:S(2)}) collective-permute-start(f32[2,4,1024]{2,1,0:T(4,128)S(1)} %dynamic-slice_bitcast_fusion.3), channel_id=1, source_target_pairs={{0,64},{32,96},{64,0},{96,32},{128,192},{160,224},{192,128},{224,1... | collective-permute-start | bytes 98312 | tf_op jit(solution)/shard_map/ppermute | solution.py:64
  188.9 2.0 collective-permute-done.15
  190.9 6.2 %collective-permute-start.16 = (f32[4,1024]{1,0:T(4,128)S(1)}, f32[4,1024]{1,0:T(4,128)S(1)}, u32[]{:S(2)}, u32[]{:S(2)}) collective-permute-start(f32[4,1024]{1,0:T(4,128)S(1)} %dynamic-slice_bitcast_fusion.5), channel_id=1, source_target_pairs={{0,128},{32,160},{64,192},{96,224},{128,0},{160,32},{192,64},{224,... | collective-permute-start | bytes 49160 | tf_op jit(solution)/shard_map/ppermute | solution.py:64
  197.1 1.7 collective-permute-done.16
  198.9 5.9 %collective-permute-start.17 = (f32[4,1024]{1,0:T(4,128)S(1)}, f32[4,1024]{1,0:T(4,128)S(1)}, u32[]{:S(2)}, u32[]{:S(2)}) collective-permute-start(f32[4,1024]{1,0:T(4,128)S(1)} %bitcast_add_fusion.8), channel_id=1, source_target_pairs={{0,128},{32,160},{64,192},{96,224},{128,0},{160,32},{192,64},{224,... | collective-permute-start | bytes 49160 | tf_op jit(solution)/shard_map/ppermute | solution.py:47
  204.8 1.7 collective-permute-done.17
  206.5 3.1 %collective-permute-start.18 = (f32[2,4,1024]{2,1,0:T(4,128)S(1)}, f32[2,4,1024]{2,1,0:T(4,128)S(1)}, u32[]{:S(2)}, u32[]{:S(2)}) collective-permute-start(f32[2,4,1024]{2,1,0:T(4,128)S(1)} %pad_maximum_fusion.10), channel_id=1, source_target_pairs={{0,64},{32,96},{64,0},{96,32},{128,192},{160,224},{192,128},{224,1... | collective-permute-start | bytes 98312 | tf_op jit(solution)/shard_map/ppermute | solution.py:47
  209.6 1.9 collective-permute-done.18
  211.5 1.6 collective-permute-start.19
  213.2 2.7 %collective-permute-done.19 = f32[2,2,4,1024]{3,2,1,0:T(4,128)S(1)} collective-permute-done((f32[2,2,4,1024]{3,2,1,0:T(4,128)S(1)}, f32[2,2,4,1024]{3,2,1,0:T(4,128)S(1)}, u32[]{:S(2)}, u32[]{:S(2)}) %collective-permute-start.19) | collective-permute-done | bytes 65568 | tf_op jit(solution)/shard_map/ppermute | solution.py:47
  (79 shorter events, 9.4 us)
Async XLA Ops:
  7.2 71.7 %copy-start = (bf16[1024,1024]{1,0:T(8,128)(2,1)S(1)}, bf16[1024,1024]{1,0:T(8,128)(2,1)}, u32[]{:S(2)}) copy-start(bf16[1024,1024]{1,0:T(8,128)(2,1)} %param.9) | copy-start | bytes 6291460
  7.2 173.1 %reduce-scatter.4.cloned.1.call-start = ((), (), s32[]{:S(2)}) async-start(), calls=%async_computation.1 | async-start | bytes 8650752
  7.2 7.0 %copy-start.1 = (bf16[1,256,1024]{2,1,0:T(8,128)(2,1)S(1)}, bf16[1,256,1024]{2,1,0:T(8,128)(2,1)}, u32[]{:S(2)}) copy-start(bf16[1,256,1024]{2,1,0:T(8,128)(2,1)} %param.8) | copy-start | bytes 1572868
  10.8 12.3 %collective-permute-start.2 = (bf16[2,2176]{1,0:T(2,128)(2,1)S(1)}, bf16[2,2176]{1,0:T(2,128)(2,1)S(1)}, u32[]{:S(2)}, u32[]{:S(2)}) collective-permute-start(bf16[2,2176]{1,0:T(2,128)(2,1)S(1)} %pad_maximum_fusion.12), channel_id=1, source_target_pairs={{0,16},{1,17},{2,18},{3,19},{4,20},{5,21},{6,22},{7,23},{8,24},{9,... | collective-permute-start | bytes 26120 | tf_op jit(solution)/shard_map/ppermute | solution.py:47
  15.4 29.1 %collective-permute-start = (bf16[2,128,1024]{2,1,0:T(8,128)(2,1)}, bf16[2,128,1024]{2,1,0:T(8,128)(2,1)}, u32[]{:S(2)}, u32[]{:S(2)}) collective-permute-start(bf16[2,128,1024]{2,1,0:T(8,128)(2,1)} %get-tuple-element.34), channel_id=1, source_target_pairs={{0,1},{1,2},{2,3},{3,4},{4,5},{5,6},{6,7},{7,8},{8,9},{9,10},{10,1... | collective-permute-start | bytes 1572872 | tf_op jit(solution)/shard_map/ppermute | solution.py:20
  17.3 27.2 %collective-permute-start.1 = (bf16[2,128,1024]{2,1,0:T(8,128)(2,1)}, bf16[2,128,1024]{2,1,0:T(8,128)(2,1)}, u32[]{:S(2)}, u32[]{:S(2)}) collective-permute-start(bf16[2,128,1024]{2,1,0:T(8,128)(2,1)} %get-tuple-element.35), channel_id=1, source_target_pairs={{1,0},{2,1},{3,2},{4,3},{5,4},{6,5},{7,6},{8,7},{9,8},{10,9},{11,1... | collective-permute-start | bytes 1572872 | tf_op jit(solution)/shard_map/ppermute | solution.py:23
  23.2 5.4 %collective-permute-start.3 = (bf16[2,2,2176]{2,1,0:T(2,128)(2,1)S(1)}, bf16[2,2,2176]{2,1,0:T(2,128)(2,1)S(1)}, u32[]{:S(2)}, u32[]{:S(2)}) collective-permute-start(bf16[2,2,2176]{2,1,0:T(2,128)(2,1)S(1)} %pad_maximum_fusion.11), channel_id=1, source_target_pairs={{0,8},{1,9},{2,10},{3,11},{4,12},{5,13},{6,14},{7,15},{8,0},{9,1},... | collective-permute-start | bytes 52232 | tf_op jit(solution)/shard_map/ppermute | solution.py:47
  28.7 5.5 %collective-permute-start.4 = (bf16[2,2,2,2176]{3,2,1,0:T(2,128)(2,1)S(1)}, bf16[2,2,2,2176]{3,2,1,0:T(2,128)(2,1)S(1)}, u32[]{:S(2)}, u32[]{:S(2)}) collective-permute-start(bf16[2,2,2,2176]{3,2,1,0:T(2,128)(2,1)S(1)} %pad_maximum_fusion.9), channel_id=1, source_target_pairs={{0,4},{1,5},{2,6},{3,7},{4,0},{5,1},{6,2},{7,3},{8,12},{9,13},{10,... | collective-permute-start | bytes 104456 | tf_op jit(solution)/shard_map/ppermute | solution.py:47
  34.4 4.4 %collective-permute-start.5 = (bf16[2,2,2,2,2176]{4,3,2,1,0:T(2,128)(2,1)S(1)}, bf16[2,2,2,2,2176]{4,3,2,1,0:T(2,128)(2,1)S(1)}, u32[]{:S(2)}, u32[]{:S(2)}) collective-permute-start(bf16[2,2,2,2,2176]{4,3,2,1,0:T(2,128)(2,1)S(1)} %pad_maximum_fusion.7), channel_id=1, source_target_pairs={{0,2},{1,3},{2,0},{3,1},{4,6},{5,7},{6,4},{7,5},{8,10},{9,11},{10,... | collective-permute-start | bytes 208904 | tf_op jit(solution)/shard_map/ppermute | solution.py:47
  39.1 1.4 collective-permute-start.6
  47.3 15.7 %copy-start.4 = (bf16[1,256,1024]{2,1,0:T(8,128)(2,1)S(1)}, bf16[1,256,1024]{2,1,0:T(8,128)(2,1)}, u32[]{:S(2)}) copy-start(bf16[1,256,1024]{2,1,0:T(8,128)(2,1)} %param.10) | copy-start | bytes 1572868
  102.2 1.6 collective-permute-start.9
  104.0 5.8 %collective-permute-start.10 = (f32[2,2,2,2,2048]{4,3,2,1,0:T(2,128)S(1)}, f32[2,2,2,2,2048]{4,3,2,1,0:T(2,128)S(1)}, u32[]{:S(2)}, u32[]{:S(2)}) collective-permute-start(f32[2,2,2,2,2048]{4,3,2,1,0:T(2,128)S(1)} %dynamic-slice_bitcast_fusion), channel_id=1, source_target_pairs={{0,2},{1,3},{2,0},{3,1},{4,6},{5,7},{6,4},{7,5},{8,10},{9,11},{10,... | collective-permute-start | bytes 393224 | tf_op jit(solution)/shard_map/ppermute | solution.py:64
  109.9 5.9 %collective-permute-start.11 = (f32[2,2,2,2048]{3,2,1,0:T(2,128)S(1)}, f32[2,2,2,2048]{3,2,1,0:T(2,128)S(1)}, u32[]{:S(2)}, u32[]{:S(2)}) collective-permute-start(f32[2,2,2,2048]{3,2,1,0:T(2,128)S(1)} %dynamic-slice_bitcast_fusion.2), channel_id=1, source_target_pairs={{0,4},{1,5},{2,6},{3,7},{4,0},{5,1},{6,2},{7,3},{8,12},{9,13},{10,... | collective-permute-start | bytes 196616 | tf_op jit(solution)/shard_map/ppermute | solution.py:64
  110.1 24.2 %collective-permute-start.7 = (f32[2,128,1024]{2,1,0:T(8,128)S(1)}, f32[2,128,1024]{2,1,0:T(8,128)}, u32[]{:S(2)}, u32[]{:S(2)}) collective-permute-start(f32[2,128,1024]{2,1,0:T(8,128)S(1)} %pad_maximum_fusion.1), channel_id=1, source_target_pairs={{0,1},{1,2},{2,3},{3,4},{4,5},{5,6},{6,7},{7,8},{8,9},{9,10},{10,1... | collective-permute-start | bytes 3145736 | tf_op jit(solution)/shard_map/ppermute | solution.py:31
  115.9 13.0 %collective-permute-start.12 = (f32[2,2,2048]{2,1,0:T(2,128)S(1)}, f32[2,2,2048]{2,1,0:T(2,128)S(1)}, u32[]{:S(2)}, u32[]{:S(2)}) collective-permute-start(f32[2,2,2048]{2,1,0:T(2,128)S(1)} %dynamic-slice_bitcast_fusion.4), channel_id=1, source_target_pairs={{0,8},{1,9},{2,10},{3,11},{4,12},{5,13},{6,14},{7,15},{8,0},{9,1},... | collective-permute-start | bytes 98312 | tf_op jit(solution)/shard_map/ppermute | solution.py:64
  117.0 17.3 %collective-permute-start.8 = (f32[2,128,1024]{2,1,0:T(8,128)}, f32[2,128,1024]{2,1,0:T(8,128)}, u32[]{:S(2)}, u32[]{:S(2)}) collective-permute-start(f32[2,128,1024]{2,1,0:T(8,128)} %pad_maximum_fusion.2), channel_id=1, source_target_pairs={{1,0},{2,1},{3,2},{4,3},{5,4},{6,5},{7,6},{8,7},{9,8},{10,9},{11,1... | collective-permute-start | bytes 3145736 | tf_op jit(solution)/shard_map/ppermute | solution.py:31
  128.9 5.3 %collective-permute-start.13 = (f32[2,2048]{1,0:T(2,128)S(1)}, f32[2,2048]{1,0:T(2,128)S(1)}, u32[]{:S(2)}, u32[]{:S(2)}) collective-permute-start(f32[2,2048]{1,0:T(2,128)S(1)} %dynamic-slice_bitcast_fusion.6), channel_id=1, source_target_pairs={{0,16},{1,17},{2,18},{3,19},{4,20},{5,21},{6,22},{7,23},{8,24},{9,... | collective-permute-start | bytes 49160 | tf_op jit(solution)/shard_map/ppermute | solution.py:64
  134.4 3.0 %copy-start.2 = (f32[512,1024]{1,0:T(8,128)S(1)}, f32[512,1024]{1,0:T(8,128)}, u32[]{:S(2)}) copy-start(f32[512,1024]{1,0:T(8,128)} %get-tuple-element.18) | copy-start | bytes 6291460
  134.4 3.6 %copy-start.3 = (f32[512,1024]{1,0:T(8,128)S(1)}, f32[512,1024]{1,0:T(8,128)}, u32[]{:S(2)}) copy-start(f32[512,1024]{1,0:T(8,128)} %get-tuple-element.19) | copy-start | bytes 6291460
  181.6 4.4 %collective-permute-start.14 = (f32[2,2,4,1024]{3,2,1,0:T(4,128)S(1)}, f32[2,2,4,1024]{3,2,1,0:T(4,128)S(1)}, u32[]{:S(2)}, u32[]{:S(2)}) collective-permute-start(f32[2,2,4,1024]{3,2,1,0:T(4,128)S(1)} %dynamic-slice_bitcast_fusion.1), channel_id=1, source_target_pairs={{0,32},{32,0},{64,96},{96,64},{128,160},{160,128},{192,224},{224,1... | collective-permute-start | bytes 196616 | tf_op jit(solution)/shard_map/ppermute | solution.py:64
  186.0 4.9 %collective-permute-start.15 = (f32[2,4,1024]{2,1,0:T(4,128)S(1)}, f32[2,4,1024]{2,1,0:T(4,128)S(1)}, u32[]{:S(2)}, u32[]{:S(2)}) collective-permute-start(f32[2,4,1024]{2,1,0:T(4,128)S(1)} %dynamic-slice_bitcast_fusion.3), channel_id=1, source_target_pairs={{0,64},{32,96},{64,0},{96,32},{128,192},{160,224},{192,128},{224,1... | collective-permute-start | bytes 98312 | tf_op jit(solution)/shard_map/ppermute | solution.py:64
  190.9 7.9 %collective-permute-start.16 = (f32[4,1024]{1,0:T(4,128)S(1)}, f32[4,1024]{1,0:T(4,128)S(1)}, u32[]{:S(2)}, u32[]{:S(2)}) collective-permute-start(f32[4,1024]{1,0:T(4,128)S(1)} %dynamic-slice_bitcast_fusion.5), channel_id=1, source_target_pairs={{0,128},{32,160},{64,192},{96,224},{128,0},{160,32},{192,64},{224,... | collective-permute-start | bytes 49160 | tf_op jit(solution)/shard_map/ppermute | solution.py:64
  198.9 7.6 %collective-permute-start.17 = (f32[4,1024]{1,0:T(4,128)S(1)}, f32[4,1024]{1,0:T(4,128)S(1)}, u32[]{:S(2)}, u32[]{:S(2)}) collective-permute-start(f32[4,1024]{1,0:T(4,128)S(1)} %bitcast_add_fusion.8), channel_id=1, source_target_pairs={{0,128},{32,160},{64,192},{96,224},{128,0},{160,32},{192,64},{224,... | collective-permute-start | bytes 49160 | tf_op jit(solution)/shard_map/ppermute | solution.py:47
  206.5 5.0 %collective-permute-start.18 = (f32[2,4,1024]{2,1,0:T(4,128)S(1)}, f32[2,4,1024]{2,1,0:T(4,128)S(1)}, u32[]{:S(2)}, u32[]{:S(2)}) collective-permute-start(f32[2,4,1024]{2,1,0:T(4,128)S(1)} %pad_maximum_fusion.10), channel_id=1, source_target_pairs={{0,64},{32,96},{64,0},{96,32},{128,192},{160,224},{192,128},{224,1... | collective-permute-start | bytes 98312 | tf_op jit(solution)/shard_map/ppermute | solution.py:47
  211.5 4.4 %collective-permute-start.19 = (f32[2,2,4,1024]{3,2,1,0:T(4,128)S(1)}, f32[2,2,4,1024]{3,2,1,0:T(4,128)S(1)}, u32[]{:S(2)}, u32[]{:S(2)}) collective-permute-start(f32[2,2,4,1024]{3,2,1,0:T(4,128)S(1)} %pad_maximum_fusion.8), channel_id=1, source_target_pairs={{0,32},{32,0},{64,96},{96,64},{128,160},{160,128},{192,224},{224,1... | collective-permute-start | bytes 196616 | tf_op jit(solution)/shard_map/ppermute | solution.py:47
Sparse Core Ops, SparseCore 0:
  79.0 101.2 reduce-scatter.3

commit v2 on v1

--- a/solution.py
+++ b/solution.py
@@ -1,3 +1,4 @@
+import functools
 import math
 
 import jax
@@ -72,8 +73,8 @@
     return value
 
 
-def forward_kernel(q_ref, k_ref, v_ref, ck_ref, cv_ref, counts_ref, fine_ref, far_ref,
-                   att_ref, top_ref, total_ref):
+def forward_kernel(term_scale, q_ref, k_ref, v_ref, ck_ref, cv_ref, counts_ref, fine_ref, far_ref,
+                   grad_t_ref, att_ref, term_ref):
     score_scale = 1.0 / math.sqrt(HEAD_DIM)
     lanes = q_ref.shape[1]
     low_lanes = lax.broadcasted_iota(jnp.int32, (BLOCK, lanes), 1) < HEAD_DIM
@@ -110,18 +111,18 @@
             halves.append((att, top, total))
         rows = pl.ds(block * BLOCK, BLOCK)
         att_ref[rows, :] = jnp.where(low_lanes, halves[0][0], halves[1][0]).astype(att_ref.dtype)
-        top_ref[rows, :] = jnp.where(low_lanes, halves[0][1], halves[1][1])
-        total_ref[rows, :] = jnp.where(low_lanes, halves[0][2], halves[1][2])
-
-
-def attention_forward(query_rows, padded_k, padded_v, coarse_k, coarse_v, counts, fine_ok, far_ok):
+    term_ref[...] = jnp.dot(grad_t_ref[...], att_ref[...],
+                            preferred_element_type=jnp.float32) * term_scale
+
+
+def attention_forward(query_rows, padded_k, padded_v, coarse_k, coarse_v, counts, fine_ok, far_ok,
+                      grad_t, term_scale):
     tokens, width = query_rows.shape
     lanes = 2 * HEAD_DIM
     by_pair = lambda rows: pl.BlockSpec((rows, lanes), lambda pair: (0, pair))
     whole = lambda shape: pl.BlockSpec(shape, lambda pair: (0, 0))
-    stat = jax.ShapeDtypeStruct((tokens, width), jnp.float32)
     return pl.pallas_call(
-        forward_kernel,
+        functools.partial(forward_kernel, term_scale),
         grid=(width // lanes,),
         in_specs=[
             by_pair(tokens),
@@ -132,10 +133,14 @@
             whole(counts.shape),
             whole(fine_ok.shape),
             whole(far_ok.shape),
-        ],
-        out_specs=[by_pair(tokens), by_pair(tokens), by_pair(tokens)],
-        out_shape=[jax.ShapeDtypeStruct((tokens, width), jnp.bfloat16), stat, stat],
-    )(query_rows, padded_k, padded_v, coarse_k, coarse_v, counts, fine_ok, far_ok)
+            whole(grad_t.shape),
+        ],
+        out_specs=[by_pair(tokens), by_pair(grad_t.shape[0])],
+        out_shape=[
+            jax.ShapeDtypeStruct((tokens, width), jnp.bfloat16),
+            jax.ShapeDtypeStruct((grad_t.shape[0], width), jnp.float32),
+        ],
+    )(query_rows, padded_k, padded_v, coarse_k, coarse_v, counts, fine_ok, far_ok, grad_t)
 
 
 def backward_kernel(q_ref, k_ref, v_ref, ck_ref, cv_ref, counts_ref, fine_ref, far_ref,
@@ -308,28 +313,14 @@
     paired = jnp.stack([key_rows, value_rows])
     extended = padded_2(paired, (("seq", 1),), BLOCK)
     padded_kv = extended.reshape(2, local_blocks + 2, BLOCK, HEADS, HEAD_DIM)
-    key_win = block_windows(padded_kv[0], local_blocks)
-    value_win = block_windows(padded_kv[1], local_blocks)
-    query_blk = query_rows.reshape(local_blocks, BLOCK, HEADS, HEAD_DIM)
-    coarse_kh = gathered_keys.reshape(all_blocks, HEADS, HEAD_DIM)
-    coarse_vh = gathered_values.reshape(all_blocks, HEADS, HEAD_DIM)
     local_ids = seq_index * local_blocks + jnp.arange(local_blocks)
     offsets = jnp.repeat(jnp.arange(3) - 1, BLOCK)
     key_blocks = local_ids[:, None] + offsets[None, :]
     fine_ok = (key_blocks >= 0) & (key_blocks < all_blocks)
     far_ok = jnp.abs(local_ids[:, None] - jnp.arange(all_blocks)[None, :]) >= 2
-    fine_s = (
-        jnp.einsum("nqhe,nkhe->nhqk", query_blk, key_win, preferred_element_type=jnp.float32)
-        * score_scale
-    )
-    coarse_s = (
-        jnp.einsum("nqhe,che->nhqc", query_blk, coarse_kh, preferred_element_type=jnp.float32)
-        * score_scale
-    )
-    fine_s = jnp.where(fine_ok[:, None, None, :], fine_s, -jnp.inf)
-    coarse_s = jnp.where(far_ok[:, None, None, :], coarse_s, -jnp.inf)
     padded_rows = extended.reshape(2, (local_blocks + 2) * BLOCK, model_width)
-    attended_rows, top_rows, total_rows = attention_forward(
+    grad_norm = 1.0 / math.sqrt(seq_devices * tokens)
+    attended_rows, full_term = attention_forward(
         query_rows,
         padded_rows[0],
         padded_rows[1],
@@ -338,26 +329,13 @@
         gathered_counts[None, :],
         fine_ok.astype(jnp.float32),
         far_ok.astype(jnp.float32),
-    )
-    attended = attended_rows.reshape(local_blocks, BLOCK, HEADS, HEAD_DIM)
-    head_stat = lambda rows: rows.reshape(local_blocks, BLOCK, HEADS, HEAD_DIM)[..., 0].transpose(0, 2, 1)[..., None]
-    row_top = head_stat(top_rows)
-    row_total = head_stat(total_rows)
-    fine_w = jnp.exp(fine_s - row_top) / row_total
-    coarse_w = gathered_counts * jnp.exp(coarse_s - row_top) / row_total
-    fine_wb = fine_w.astype(jnp.bfloat16)
-    coarse_wb = coarse_w.astype(jnp.bfloat16)
+        grad_out.T,
+        grad_norm,
+    )
     attended_grad = jnp.dot(grad_out, out_weight, preferred_element_type=jnp.float32).astype(
         jnp.bfloat16
     )
-    grad_norm = 1.0 / math.sqrt(seq_devices * tokens)
-    full_term = (
-        jnp.einsum("to,ti->oi", grad_out, attended_rows, preferred_element_type=jnp.float32)
-        * grad_norm
-    )
-    seq_part = lax.psum_scatter(
-        jnp.pad(full_term, ((0, 0), (0, model_width))), "seq", scatter_dimension=0, tiled=True
-    )[:, :model_width]
+    seq_part = lax.psum_scatter(full_term, "seq", scatter_dimension=0, tiled=True)
     full_term, attended_grad = lax.optimization_barrier((full_term, attended_grad))
     query_grad, key_pad, value_pad, coarse_key_all, coarse_value_all = attention_backward(
         query_rows,

time: 224 us -> 201 us (0.90)
  waiting for transfers between devices: 91.3 us -> 78.8 us
  local copies, waits for them, and re-layouts: 23.1 us -> 13.6 us
  matrix products: 7.73 us -> 3.95 us
  Pallas kernels: 36.1 us -> 38.7 us
    unnamed x2 -> x1, waiting for transfers between devices: 41 us -> 0.02 us
    reduce_scatter x0 -> x1, waiting for transfers between devices: none -> 30.1 us  [per_device(): lax.psum_scatter(full_term, 'seq', scatter_dimension=0, tiled=True)]
    pad x1 -> x0, local copies, waits for them, and re-layouts: 6.63 us -> none  [per_device(): jnp.pad(full_term, ((0, 0), (0, model_width)))]
    dot_general x1 -> x0, matrix products: 3.77 us -> none  [per_device(): jnp.einsum('to,ti->oi', grad_out, attended_rows, preferred_element_type=j...]
    pallas_call x1, Pallas kernels: 15.7 us -> 18.3 us  [attention_forward(): pl.pallas_call(functools.partial(forward_kernel, term_scale), grid=(width...]
    unnamed x12, local copies, waits for them, and re-layouts: 7.72 us -> 5.27 us
  transfers between devices with their start and end apart: 21 -> 21, of which waited for: 16 -> 17; matrix products, arithmetic and copies ran while one was open for 8% -> 10% of each run, Pallas kernels for 9% -> 10%
where the time goes in v2:
time: 201 us; the launch traced here: 200 us
  waiting for transfers between devices  78.8 us (39%)
  Pallas kernels  38.7 us (19%)
  starting transfers between devices  37.7 us (19%)
  between operations  14.5 us (7%)
  local copies, waits for them, and re-layouts  13.6 us (7%)
  other arithmetic  12.2 us (6%)
  matrix products  3.95 us (2%)
    reduce_scatter x1, waiting for transfers between devices, per_device(): lax.psum_scatter(full_term, 'seq', scatter_dimension=0, tiled=True)  30.1 us
    ppermute x8, waiting for transfers between devices, halving_scatter(): held = keep + lax.ppermute(send, axis, xor_pairs(count, bit))  28.9 us
    pallas_call x1, Pallas kernels, attention_backward(): pl.pallas_call(backward_kernel, grid=(width // lanes,), in_specs=[by_pair...  20.4 us
    ppermute x8, waiting for transfers between devices, doubling_gather(): other = lax.ppermute(held, axis, xor_pairs(count, bit))  19.5 us
    pallas_call x1, Pallas kernels, attention_forward(): pl.pallas_call(functools.partial(forward_kernel, term_scale), grid=(width...  18.3 us
    ppermute x8, starting transfers between devices, doubling_gather(): other = lax.ppermute(held, axis, xor_pairs(count, bit))  13.2 us
    ppermute x8, starting transfers between devices, halving_scatter(): held = keep + lax.ppermute(send, axis, xor_pairs(count, bit))  12.7 us
    ppermute x1, starting transfers between devices, padded_2(): lax.ppermute(lax.slice_in_dim(block, 0, width, axis=dim), axis, backward)  5.75 us
  transfers between devices with their start and end apart: 21, of which 17 were waited for; matrix products, arithmetic and copies ran while one was open for 10% of the time, Pallas kernels for 10%

profile of v2, /device:TPU:8, one launch (start us, length us, event | category | flops | bytes accessed | tf_op | source)
XLA Modules:
  0.0 199.5 jit_solution(2960855638723759103)
XLA Ops:
  7.2 0.8 convert_element_type.71
  8.2 1.2 fusion.18
  9.4 1.2 fusion.20
  10.8 2.4 %collective-permute-start.2 = (bf16[2,2176]{1,0:T(2,128)(2,1)S(1)}, bf16[2,2176]{1,0:T(2,128)(2,1)S(1)}, u32[]{:S(2)}, u32[]{:S(2)}) collective-permute-start(bf16[2,2176]{1,0:T(2,128)(2,1)S(1)} %pad_maximum_fusion.12), channel_id=1, source_target_pairs={{0,16},{1,17},{2,18},{3,19},{4,20},{5,21},{6,22},{7,23},{8,24},{9,... | collective-permute-start | bytes 26120 | tf_op jit(solution)/shard_map/ppermute | solution.py:48
  13.2 1.1 constant_dynamic-update-slice_fusion.1
  14.3 1.0 fusion.22
  15.4 1.9 collective-permute-start
  17.3 5.8 %collective-permute-start.1 = (bf16[2,128,1024]{2,1,0:T(8,128)(2,1)}, bf16[2,128,1024]{2,1,0:T(8,128)(2,1)}, u32[]{:S(2)}, u32[]{:S(2)}) collective-permute-start(bf16[2,128,1024]{2,1,0:T(8,128)(2,1)} %get-tuple-element.37), channel_id=1, source_target_pairs={{1,0},{2,1},{3,2},{4,3},{5,4},{6,5},{7,6},{8,7},{9,8},{10,9},{11,1... | collective-permute-start | bytes 1572872 | tf_op jit(solution)/shard_map/ppermute | solution.py:24
  23.3 5.2 %collective-permute-done.3 = bf16[2,2,2176]{2,1,0:T(2,128)(2,1)S(1)} collective-permute-done((bf16[2,2,2176]{2,1,0:T(2,128)(2,1)S(1)}, bf16[2,2,2176]{2,1,0:T(2,128)(2,1)S(1)}, u32[]{:S(2)}, u32[]{:S(2)}) %collective-permute-start.3) | collective-permute-done | bytes 17440 | tf_op jit(solution)/shard_map/ppermute | solution.py:48
  28.8 5.4 %collective-permute-done.4 = bf16[2,2,2,2176]{3,2,1,0:T(2,128)(2,1)S(1)} collective-permute-done((bf16[2,2,2,2176]{3,2,1,0:T(2,128)(2,1)S(1)}, bf16[2,2,2,2176]{3,2,1,0:T(2,128)(2,1)S(1)}, u32[]{:S(2)}, u32[]{:S(2)}) %collective-permute-start.4) | collective-permute-done | bytes 34848 | tf_op jit(solution)/shard_map/ppermute | solution.py:48
  35.1 2.0 %copy.21 = bf16[1,256,1024]{1,2,0:T(8,128)(2,1)} copy(bf16[1,256,1024]{2,1,0:T(8,128)(2,1)} %param.10) | data formatting | bytes 1048576 | tf_op args[4]
  37.2 1.6 collective-permute-done.5
  39.8 0.7 collective-permute-done.6
  40.9 1.1 pad_maximum_fusion.4
  42.0 1.1 reshape_reshape.12
  44.4 1.4 pad_maximum_fusion
  45.8 1.5 slice_bitcast_fusion
  47.3 18.3 %shard_map.93 = (bf16[256,1024]{1,0:T(8,128)(2,1)}, f32[1024,1024]{1,0:T(8,128)}) custom-call(bf16[256,1024]{1,0:T(8,128)(2,1)} %bitcast.143, bf16[512,1024]{1,0:T(8,128)(2,1)} %get-tuple-element.35.k_ref, bf16[512,1024]{1,0:T(8,128)(2,1)} %get-tuple-element.34.v_ref, bf16[64,1024]{1,0:T(8,128)(2,1)} %get-tuple-element.41.ck_ref, ...), custom_call_target="tpu_custom_call" | custom-call | tf_op jit(solution)/shard_map/pallas_call | solution.py:124
  65.7 1.0 copy-done.4
  66.6 1.5 convolution_convert_fusion.g_ref
  68.2 20.4 %shard_map.94 = (bf16[256,1024]{1,0:T(8,128)(2,1)}, f32[512,1024]{1,0:T(8,128)}, f32[512,1024]{1,0:T(8,128)}, f32[64,1024]{1,0:T(8,128)}, f32[64,1024]{1,0:T(8,128)}) custom-call(bf16[256,1024]{1,0:T(8,128)(2,1)} %bitcast.144, bf16[512,1024]{1,0:T(8,128)(2,1)} %get-tuple-element.35.k_ref, bf16[512,1024]{1,0:T(8,128)(2,1)} %get-tuple-element.34.v_ref, ...), custom_call_target="tpu_custom_call" | custom-call | tf_op jit(solution)/shard_map/pallas_call | solution.py:230
  88.6 1.1 pad_maximum_fusion.3
  90.3 1.4 collective-permute-done.9
  92.3 1.7 slice_bitcast_fusion.2
  94.0 3.4 %collective-permute-done.10 = f32[2,2,2,2,2048]{4,3,2,1,0:T(2,128)S(1)} collective-permute-done((f32[2,2,2,2,2048]{4,3,2,1,0:T(2,128)S(1)}, f32[2,2,2,2,2048]{4,3,2,1,0:T(2,128)S(1)}, u32[]{:S(2)}, u32[]{:S(2)}) %collective-permute-start.10) | collective-permute-done | bytes 131104 | tf_op jit(solution)/shard_map/ppermute | solution.py:65
  97.8 2.1 %collective-permute-start.7 = (f32[2,128,1024]{2,1,0:T(8,128)S(1)}, f32[2,128,1024]{2,1,0:T(8,128)}, u32[]{:S(2)}, u32[]{:S(2)}) collective-permute-start(f32[2,128,1024]{2,1,0:T(8,128)S(1)} %pad_maximum_fusion.1), channel_id=1, source_target_pairs={{0,1},{1,2},{2,3},{3,4},{4,5},{5,6},{6,7},{7,8},{8,9},{9,10},{10,1... | collective-permute-start | bytes 3145736 | tf_op jit(solution)/shard_map/ppermute | solution.py:32
  99.9 3.5 %collective-permute-done.11 = f32[2,2,2,2048]{3,2,1,0:T(2,128)S(1)} collective-permute-done((f32[2,2,2,2048]{3,2,1,0:T(2,128)S(1)}, f32[2,2,2,2048]{3,2,1,0:T(2,128)S(1)}, u32[]{:S(2)}, u32[]{:S(2)}) %collective-permute-start.11) | collective-permute-done | bytes 65568 | tf_op jit(solution)/shard_map/ppermute | solution.py:65
  103.6 1.1 pad_maximum_fusion.2
  104.6 2.0 %collective-permute-start.8 = (f32[2,128,1024]{2,1,0:T(8,128)}, f32[2,128,1024]{2,1,0:T(8,128)}, u32[]{:S(2)}, u32[]{:S(2)}) collective-permute-start(f32[2,128,1024]{2,1,0:T(8,128)} %pad_maximum_fusion.2), channel_id=1, source_target_pairs={{1,0},{2,1},{3,2},{4,3},{5,4},{6,5},{7,6},{8,7},{9,8},{10,9},{11,1... | collective-permute-start | bytes 3145736 | tf_op jit(solution)/shard_map/ppermute | solution.py:32
  106.7 9.8 %collective-permute-done.12 = f32[2,2,2048]{2,1,0:T(2,128)S(1)} collective-permute-done((f32[2,2,2048]{2,1,0:T(2,128)S(1)}, f32[2,2,2048]{2,1,0:T(2,128)S(1)}, u32[]{:S(2)}, u32[]{:S(2)}) %collective-permute-start.12) | collective-permute-done | bytes 32800 | tf_op jit(solution)/shard_map/ppermute | solution.py:65
  116.6 1.3 collective-permute-start.13
  117.9 4.2 %collective-permute-done.13 = f32[2,2048]{1,0:T(2,128)S(1)} collective-permute-done((f32[2,2048]{1,0:T(2,128)S(1)}, f32[2,2048]{1,0:T(2,128)S(1)}, u32[]{:S(2)}, u32[]{:S(2)}) %collective-permute-start.13) | collective-permute-done | bytes 16416 | tf_op jit(solution)/shard_map/ppermute | solution.py:65
  122.3 1.8 pad_add_fusion
  125.3 1.3 fusion.2
  126.6 30.1 %reduce-scatter.2.cloned.1.call-done = f32[32,1024]{1,0:T(8,128)} async-done(((f32[1024,1024]{1,0:T(8,128)}), f32[32,1024]{1,0:T(8,128)}) %reduce-scatter.2.cloned.1.call-update) | async-done | bytes 131088 | tf_op jit(solution)/shard_map/reduce_scatter | solution.py:338
  156.7 0.9 reshape_reshape.14
  157.7 1.6 collective-permute-start.14
  159.3 2.7 %collective-permute-done.14 = f32[2,2,4,1024]{3,2,1,0:T(4,128)S(1)} collective-permute-done((f32[2,2,4,1024]{3,2,1,0:T(4,128)S(1)}, f32[2,2,4,1024]{3,2,1,0:T(4,128)S(1)}, u32[]{:S(2)}, u32[]{:S(2)}) %collective-permute-start.14) | collective-permute-done | bytes 65568 | tf_op jit(solution)/shard_map/ppermute | solution.py:65
  162.1 3.0 %collective-permute-start.15 = (f32[2,4,1024]{2,1,0:T(4,128)S(1)}, f32[2,4,1024]{2,1,0:T(4,128)S(1)}, u32[]{:S(2)}, u32[]{:S(2)}) collective-permute-start(f32[2,4,1024]{2,1,0:T(4,128)S(1)} %dynamic-slice_bitcast_fusion.3), channel_id=1, source_target_pairs={{0,64},{32,96},{64,0},{96,32},{128,192},{160,224},{192,128},{224,1... | collective-permute-start | bytes 98312 | tf_op jit(solution)/shard_map/ppermute | solution.py:65
  165.0 1.9 collective-permute-done.15
  167.0 5.9 %collective-permute-start.16 = (f32[4,1024]{1,0:T(4,128)S(1)}, f32[4,1024]{1,0:T(4,128)S(1)}, u32[]{:S(2)}, u32[]{:S(2)}) collective-permute-start(f32[4,1024]{1,0:T(4,128)S(1)} %dynamic-slice_bitcast_fusion.5), channel_id=1, source_target_pairs={{0,128},{32,160},{64,192},{96,224},{128,0},{160,32},{192,64},{224,... | collective-permute-start | bytes 49160 | tf_op jit(solution)/shard_map/ppermute | solution.py:65
  172.9 1.9 collective-permute-done.16
  174.8 5.8 %collective-permute-start.17 = (f32[4,1024]{1,0:T(4,128)S(1)}, f32[4,1024]{1,0:T(4,128)S(1)}, u32[]{:S(2)}, u32[]{:S(2)}) collective-permute-start(f32[4,1024]{1,0:T(4,128)S(1)} %bitcast_add_fusion.8), channel_id=1, source_target_pairs={{0,128},{32,160},{64,192},{96,224},{128,0},{160,32},{192,64},{224,... | collective-permute-start | bytes 49160 | tf_op jit(solution)/shard_map/ppermute | solution.py:48
  180.5 2.0 collective-permute-done.17
  182.5 3.1 %collective-permute-start.18 = (f32[2,4,1024]{2,1,0:T(4,128)S(1)}, f32[2,4,1024]{2,1,0:T(4,128)S(1)}, u32[]{:S(2)}, u32[]{:S(2)}) collective-permute-start(f32[2,4,1024]{2,1,0:T(4,128)S(1)} %pad_maximum_fusion.10), channel_id=1, source_target_pairs={{0,64},{32,96},{64,0},{96,32},{128,192},{160,224},{192,128},{224,1... | collective-permute-start | bytes 98312 | tf_op jit(solution)/shard_map/ppermute | solution.py:48
  185.6 1.9 collective-permute-done.18
  187.5 1.6 collective-permute-start.19
  189.1 2.7 %collective-permute-done.19 = f32[2,2,4,1024]{3,2,1,0:T(4,128)S(1)} collective-permute-done((f32[2,2,4,1024]{3,2,1,0:T(4,128)S(1)}, f32[2,2,4,1024]{3,2,1,0:T(4,128)S(1)}, u32[]{:S(2)}, u32[]{:S(2)}) %collective-permute-start.19) | collective-permute-done | bytes 65568 | tf_op jit(solution)/shard_map/ppermute | solution.py:48
  (73 shorter events, 8.4 us)
Async XLA Ops:
  7.2 58.5 %copy-start = (bf16[1024,1024]{1,0:T(8,128)(2,1)S(1)}, bf16[1024,1024]{1,0:T(8,128)(2,1)}, u32[]{:S(2)}) copy-start(bf16[1024,1024]{1,0:T(8,128)(2,1)} %param.9) | copy-start | bytes 6291460
  7.2 149.5 %reduce-scatter.2.cloned.1.call-start = ((), (), s32[]{:S(2)}) async-start(), calls=%async_computation.1 | async-start | bytes 4325376 | tf_op jit(solution)/shard_map/reduce_scatter | solution.py:338
  7.2 7.0 %copy-start.1 = (bf16[1,256,1024]{2,1,0:T(8,128)(2,1)S(1)}, bf16[1,256,1024]{2,1,0:T(8,128)(2,1)}, u32[]{:S(2)}) copy-start(bf16[1,256,1024]{2,1,0:T(8,128)(2,1)} %param.8) | copy-start | bytes 1572868
  10.8 12.3 %collective-permute-start.2 = (bf16[2,2176]{1,0:T(2,128)(2,1)S(1)}, bf16[2,2176]{1,0:T(2,128)(2,1)S(1)}, u32[]{:S(2)}, u32[]{:S(2)}) collective-permute-start(bf16[2,2176]{1,0:T(2,128)(2,1)S(1)} %pad_maximum_fusion.12), channel_id=1, source_target_pairs={{0,16},{1,17},{2,18},{3,19},{4,20},{5,21},{6,22},{7,23},{8,24},{9,... | collective-permute-start | bytes 26120 | tf_op jit(solution)/shard_map/ppermute | solution.py:48
  15.4 29.0 %collective-permute-start = (bf16[2,128,1024]{2,1,0:T(8,128)(2,1)}, bf16[2,128,1024]{2,1,0:T(8,128)(2,1)}, u32[]{:S(2)}, u32[]{:S(2)}) collective-permute-start(bf16[2,128,1024]{2,1,0:T(8,128)(2,1)} %get-tuple-element.36), channel_id=1, source_target_pairs={{0,1},{1,2},{2,3},{3,4},{4,5},{5,6},{6,7},{7,8},{8,9},{9,10},{10,1... | collective-permute-start | bytes 1572872 | tf_op jit(solution)/shard_map/ppermute | solution.py:21
  17.3 27.1 %collective-permute-start.1 = (bf16[2,128,1024]{2,1,0:T(8,128)(2,1)}, bf16[2,128,1024]{2,1,0:T(8,128)(2,1)}, u32[]{:S(2)}, u32[]{:S(2)}) collective-permute-start(bf16[2,128,1024]{2,1,0:T(8,128)(2,1)} %get-tuple-element.37), channel_id=1, source_target_pairs={{1,0},{2,1},{3,2},{4,3},{5,4},{6,5},{7,6},{8,7},{9,8},{10,9},{11,1... | collective-permute-start | bytes 1572872 | tf_op jit(solution)/shard_map/ppermute | solution.py:24
  23.2 5.4 %collective-permute-start.3 = (bf16[2,2,2176]{2,1,0:T(2,128)(2,1)S(1)}, bf16[2,2,2176]{2,1,0:T(2,128)(2,1)S(1)}, u32[]{:S(2)}, u32[]{:S(2)}) collective-permute-start(bf16[2,2,2176]{2,1,0:T(2,128)(2,1)S(1)} %pad_maximum_fusion.11), channel_id=1, source_target_pairs={{0,8},{1,9},{2,10},{3,11},{4,12},{5,13},{6,14},{7,15},{8,0},{9,1},... | collective-permute-start | bytes 52232 | tf_op jit(solution)/shard_map/ppermute | solution.py:48
  28.7 5.5 %collective-permute-start.4 = (bf16[2,2,2,2176]{3,2,1,0:T(2,128)(2,1)S(1)}, bf16[2,2,2,2176]{3,2,1,0:T(2,128)(2,1)S(1)}, u32[]{:S(2)}, u32[]{:S(2)}) collective-permute-start(bf16[2,2,2,2176]{3,2,1,0:T(2,128)(2,1)S(1)} %pad_maximum_fusion.9), channel_id=1, source_target_pairs={{0,4},{1,5},{2,6},{3,7},{4,0},{5,1},{6,2},{7,3},{8,12},{9,13},{10,... | collective-permute-start | bytes 104456 | tf_op jit(solution)/shard_map/ppermute | solution.py:48
  34.4 4.4 %collective-permute-start.5 = (bf16[2,2,2,2,2176]{4,3,2,1,0:T(2,128)(2,1)S(1)}, bf16[2,2,2,2,2176]{4,3,2,1,0:T(2,128)(2,1)S(1)}, u32[]{:S(2)}, u32[]{:S(2)}) collective-permute-start(bf16[2,2,2,2,2176]{4,3,2,1,0:T(2,128)(2,1)S(1)} %pad_maximum_fusion.7), channel_id=1, source_target_pairs={{0,2},{1,3},{2,0},{3,1},{4,6},{5,7},{6,4},{7,5},{8,10},{9,11},{10,... | collective-permute-start | bytes 208904 | tf_op jit(solution)/shard_map/ppermute | solution.py:48
  39.1 1.4 collective-permute-start.6
  65.6 1.0 copy-start.4
  90.0 1.6 collective-permute-start.9
  91.8 5.6 %collective-permute-start.10 = (f32[2,2,2,2,2048]{4,3,2,1,0:T(2,128)S(1)}, f32[2,2,2,2,2048]{4,3,2,1,0:T(2,128)S(1)}, u32[]{:S(2)}, u32[]{:S(2)}) collective-permute-start(f32[2,2,2,2,2048]{4,3,2,1,0:T(2,128)S(1)} %dynamic-slice_bitcast_fusion), channel_id=1, source_target_pairs={{0,2},{1,3},{2,0},{3,1},{4,6},{5,7},{6,4},{7,5},{8,10},{9,11},{10,... | collective-permute-start | bytes 393224 | tf_op jit(solution)/shard_map/ppermute | solution.py:65
  97.5 5.9 %collective-permute-start.11 = (f32[2,2,2,2048]{3,2,1,0:T(2,128)S(1)}, f32[2,2,2,2048]{3,2,1,0:T(2,128)S(1)}, u32[]{:S(2)}, u32[]{:S(2)}) collective-permute-start(f32[2,2,2,2048]{3,2,1,0:T(2,128)S(1)} %dynamic-slice_bitcast_fusion.2), channel_id=1, source_target_pairs={{0,4},{1,5},{2,6},{3,7},{4,0},{5,1},{6,2},{7,3},{8,12},{9,13},{10,... | collective-permute-start | bytes 196616 | tf_op jit(solution)/shard_map/ppermute | solution.py:65
  97.8 24.4 %collective-permute-start.7 = (f32[2,128,1024]{2,1,0:T(8,128)S(1)}, f32[2,128,1024]{2,1,0:T(8,128)}, u32[]{:S(2)}, u32[]{:S(2)}) collective-permute-start(f32[2,128,1024]{2,1,0:T(8,128)S(1)} %pad_maximum_fusion.1), channel_id=1, source_target_pairs={{0,1},{1,2},{2,3},{3,4},{4,5},{5,6},{6,7},{7,8},{8,9},{9,10},{10,1... | collective-permute-start | bytes 3145736 | tf_op jit(solution)/shard_map/ppermute | solution.py:32
  103.5 13.1 %collective-permute-start.12 = (f32[2,2,2048]{2,1,0:T(2,128)S(1)}, f32[2,2,2048]{2,1,0:T(2,128)S(1)}, u32[]{:S(2)}, u32[]{:S(2)}) collective-permute-start(f32[2,2,2048]{2,1,0:T(2,128)S(1)} %dynamic-slice_bitcast_fusion.4), channel_id=1, source_target_pairs={{0,8},{1,9},{2,10},{3,11},{4,12},{5,13},{6,14},{7,15},{8,0},{9,1},... | collective-permute-start | bytes 98312 | tf_op jit(solution)/shard_map/ppermute | solution.py:65
  104.6 17.7 %collective-permute-start.8 = (f32[2,128,1024]{2,1,0:T(8,128)}, f32[2,128,1024]{2,1,0:T(8,128)}, u32[]{:S(2)}, u32[]{:S(2)}) collective-permute-start(f32[2,128,1024]{2,1,0:T(8,128)} %pad_maximum_fusion.2), channel_id=1, source_target_pairs={{1,0},{2,1},{3,2},{4,3},{5,4},{6,5},{7,6},{8,7},{9,8},{10,9},{11,1... | collective-permute-start | bytes 3145736 | tf_op jit(solution)/shard_map/ppermute | solution.py:32
  116.6 5.5 %collective-permute-start.13 = (f32[2,2048]{1,0:T(2,128)S(1)}, f32[2,2048]{1,0:T(2,128)S(1)}, u32[]{:S(2)}, u32[]{:S(2)}) collective-permute-start(f32[2,2048]{1,0:T(2,128)S(1)} %dynamic-slice_bitcast_fusion.6), channel_id=1, source_target_pairs={{0,16},{1,17},{2,18},{3,19},{4,20},{5,21},{6,22},{7,23},{8,24},{9,... | collective-permute-start | bytes 49160 | tf_op jit(solution)/shard_map/ppermute | solution.py:65
  122.3 2.3 %copy-start.2 = (f32[512,1024]{1,0:T(8,128)S(1)}, f32[512,1024]{1,0:T(8,128)}, u32[]{:S(2)}) copy-start(f32[512,1024]{1,0:T(8,128)} %get-tuple-element.20) | copy-start | bytes 6291460
  122.3 3.0 %copy-start.3 = (f32[512,1024]{1,0:T(8,128)S(1)}, f32[512,1024]{1,0:T(8,128)}, u32[]{:S(2)}) copy-start(f32[512,1024]{1,0:T(8,128)} %get-tuple-element.21) | copy-start | bytes 6291460
  157.7 4.4 %collective-permute-start.14 = (f32[2,2,4,1024]{3,2,1,0:T(4,128)S(1)}, f32[2,2,4,1024]{3,2,1,0:T(4,128)S(1)}, u32[]{:S(2)}, u32[]{:S(2)}) collective-permute-start(f32[2,2,4,1024]{3,2,1,0:T(4,128)S(1)} %dynamic-slice_bitcast_fusion.1), channel_id=1, source_target_pairs={{0,32},{32,0},{64,96},{96,64},{128,160},{160,128},{192,224},{224,1... | collective-permute-start | bytes 196616 | tf_op jit(solution)/shard_map/ppermute | solution.py:65
  162.1 4.9 %collective-permute-start.15 = (f32[2,4,1024]{2,1,0:T(4,128)S(1)}, f32[2,4,1024]{2,1,0:T(4,128)S(1)}, u32[]{:S(2)}, u32[]{:S(2)}) collective-permute-start(f32[2,4,1024]{2,1,0:T(4,128)S(1)} %dynamic-slice_bitcast_fusion.3), channel_id=1, source_target_pairs={{0,64},{32,96},{64,0},{96,32},{128,192},{160,224},{192,128},{224,1... | collective-permute-start | bytes 98312 | tf_op jit(solution)/shard_map/ppermute | solution.py:65
  167.0 7.7 %collective-permute-start.16 = (f32[4,1024]{1,0:T(4,128)S(1)}, f32[4,1024]{1,0:T(4,128)S(1)}, u32[]{:S(2)}, u32[]{:S(2)}) collective-permute-start(f32[4,1024]{1,0:T(4,128)S(1)} %dynamic-slice_bitcast_fusion.5), channel_id=1, source_target_pairs={{0,128},{32,160},{64,192},{96,224},{128,0},{160,32},{192,64},{224,... | collective-permute-start | bytes 49160 | tf_op jit(solution)/shard_map/ppermute | solution.py:65
  174.8 7.8 %collective-permute-start.17 = (f32[4,1024]{1,0:T(4,128)S(1)}, f32[4,1024]{1,0:T(4,128)S(1)}, u32[]{:S(2)}, u32[]{:S(2)}) collective-permute-start(f32[4,1024]{1,0:T(4,128)S(1)} %bitcast_add_fusion.8), channel_id=1, source_target_pairs={{0,128},{32,160},{64,192},{96,224},{128,0},{160,32},{192,64},{224,... | collective-permute-start | bytes 49160 | tf_op jit(solution)/shard_map/ppermute | solution.py:48
  182.5 5.0 %collective-permute-start.18 = (f32[2,4,1024]{2,1,0:T(4,128)S(1)}, f32[2,4,1024]{2,1,0:T(4,128)S(1)}, u32[]{:S(2)}, u32[]{:S(2)}) collective-permute-start(f32[2,4,1024]{2,1,0:T(4,128)S(1)} %pad_maximum_fusion.10), channel_id=1, source_target_pairs={{0,64},{32,96},{64,0},{96,32},{128,192},{160,224},{192,128},{224,1... | collective-permute-start | bytes 98312 | tf_op jit(solution)/shard_map/ppermute | solution.py:48
  187.5 4.4 %collective-permute-start.19 = (f32[2,2,4,1024]{3,2,1,0:T(4,128)S(1)}, f32[2,2,4,1024]{3,2,1,0:T(4,128)S(1)}, u32[]{:S(2)}, u32[]{:S(2)}) collective-permute-start(f32[2,2,4,1024]{3,2,1,0:T(4,128)S(1)} %pad_maximum_fusion.8), channel_id=1, source_target_pairs={{0,32},{32,0},{64,96},{96,64},{128,160},{160,128},{192,224},{224,1... | collective-permute-start | bytes 196616 | tf_op jit(solution)/shard_map/ppermute | solution.py:48
Sparse Core Ops, SparseCore 0:
  65.8 90.9 reduce-scatter.1

commit v3 on v2

--- a/solution.py
+++ b/solution.py
@@ -104,8 +104,9 @@
             coarse_e = counts * jnp.exp(coarse_s - top)
             total = (jnp.sum(fine_e, axis=1, keepdims=True)
                      + jnp.sum(coarse_e, axis=1, keepdims=True))
-            fine_w = (fine_e / total).astype(jnp.bfloat16)
-            coarse_w = (coarse_e / total).astype(jnp.bfloat16)
+            inverse = 1.0 / total
+            fine_w = (fine_e * inverse).astype(jnp.bfloat16)
+            coarse_w = (coarse_e * inverse).astype(jnp.bfloat16)
             att = (jnp.dot(fine_w, value_win, preferred_element_type=jnp.float32)
                    + jnp.dot(coarse_w, coarse_v, preferred_element_type=jnp.float32))
             halves.append((att, top, total))
@@ -185,8 +186,9 @@
             coarse_e = counts * jnp.exp(coarse_s - top)
             total = (jnp.sum(fine_e, axis=1, keepdims=True)
                      + jnp.sum(coarse_e, axis=1, keepdims=True))
-            fine_w = fine_e / total
-            coarse_w = coarse_e / total
+            inverse = 1.0 / total
+            fine_w = fine_e * inverse
+            coarse_w = coarse_e * inverse
             fine_dot = lax.dot_general(grad_h, value_win, contract_last,
                                        preferred_element_type=jnp.float32)
             coarse_dot = lax.dot_general(grad_h, coarse_v, contract_last,

time: 201 us -> 201 us (level)
  no operation moved by 1% of the time
where the time goes in v3:
time: 201 us; the launch traced here: 200 us
  waiting for transfers between devices  78.8 us (39%)
  Pallas kernels  38.7 us (19%)
  starting transfers between devices  37.7 us (19%)
  between operations  14.5 us (7%)
  local copies, waits for them, and re-layouts  13.6 us (7%)
  other arithmetic  12.2 us (6%)
  matrix products  3.95 us (2%)
    reduce_scatter x1, waiting for transfers between devices, per_device(): lax.psum_scatter(full_term, 'seq', scatter_dimension=0, tiled=True)  30.1 us
    ppermute x8, waiting for transfers between devices, halving_scatter(): held = keep + lax.ppermute(send, axis, xor_pairs(count, bit))  28.9 us
    pallas_call x1, Pallas kernels, attention_backward(): pl.pallas_call(backward_kernel, grid=(width // lanes,), in_specs=[by_pair...  20.4 us
    ppermute x8, waiting for transfers between devices, doubling_gather(): other = lax.ppermute(held, axis, xor_pairs(count, bit))  19.5 us
    pallas_call x1, Pallas kernels, attention_forward(): pl.pallas_call(functools.partial(forward_kernel, term_scale), grid=(width...  18.3 us
    ppermute x8, starting transfers between devices, doubling_gather(): other = lax.ppermute(held, axis, xor_pairs(count, bit))  13.2 us
    ppermute x8, starting transfers between devices, halving_scatter(): held = keep + lax.ppermute(send, axis, xor_pairs(count, bit))  12.7 us
    ppermute x1, starting transfers between devices, padded_2(): lax.ppermute(lax.slice_in_dim(block, 0, width, axis=dim), axis, backward)  5.75 us
  transfers between devices with their start and end apart: 21, of which 17 were waited for; matrix products, arithmetic and copies ran while one was open for 10% of the time, Pallas kernels for 10%

profile of v3, /device:TPU:8, one launch (start us, length us, event | category | flops | bytes accessed | tf_op | source)
XLA Modules:
  0.0 199.5 jit_solution(2960855638723759103)
XLA Ops:
  7.2 0.8 convert_element_type.71
  8.2 1.2 fusion.18
  9.4 1.2 fusion.20
  10.8 2.4 %collective-permute-start.2 = (bf16[2,2176]{1,0:T(2,128)(2,1)S(1)}, bf16[2,2176]{1,0:T(2,128)(2,1)S(1)}, u32[]{:S(2)}, u32[]{:S(2)}) collective-permute-start(bf16[2,2176]{1,0:T(2,128)(2,1)S(1)} %pad_maximum_fusion.12), channel_id=1, source_target_pairs={{0,16},{1,17},{2,18},{3,19},{4,20},{5,21},{6,22},{7,23},{8,24},{9,... | collective-permute-start | bytes 26120 | tf_op jit(solution)/shard_map/ppermute | solution.py:48
  13.2 1.1 constant_dynamic-update-slice_fusion.1
  14.3 1.0 fusion.22
  15.4 1.9 collective-permute-start
  17.3 5.8 %collective-permute-start.1 = (bf16[2,128,1024]{2,1,0:T(8,128)(2,1)}, bf16[2,128,1024]{2,1,0:T(8,128)(2,1)}, u32[]{:S(2)}, u32[]{:S(2)}) collective-permute-start(bf16[2,128,1024]{2,1,0:T(8,128)(2,1)} %get-tuple-element.37), channel_id=1, source_target_pairs={{1,0},{2,1},{3,2},{4,3},{5,4},{6,5},{7,6},{8,7},{9,8},{10,9},{11,1... | collective-permute-start | bytes 1572872 | tf_op jit(solution)/shard_map/ppermute | solution.py:24
  23.3 5.2 %collective-permute-done.3 = bf16[2,2,2176]{2,1,0:T(2,128)(2,1)S(1)} collective-permute-done((bf16[2,2,2176]{2,1,0:T(2,128)(2,1)S(1)}, bf16[2,2,2176]{2,1,0:T(2,128)(2,1)S(1)}, u32[]{:S(2)}, u32[]{:S(2)}) %collective-permute-start.3) | collective-permute-done | bytes 17440 | tf_op jit(solution)/shard_map/ppermute | solution.py:48
  28.8 5.4 %collective-permute-done.4 = bf16[2,2,2,2176]{3,2,1,0:T(2,128)(2,1)S(1)} collective-permute-done((bf16[2,2,2,2176]{3,2,1,0:T(2,128)(2,1)S(1)}, bf16[2,2,2,2176]{3,2,1,0:T(2,128)(2,1)S(1)}, u32[]{:S(2)}, u32[]{:S(2)}) %collective-permute-start.4) | collective-permute-done | bytes 34848 | tf_op jit(solution)/shard_map/ppermute | solution.py:48
  35.1 2.0 %copy.21 = bf16[1,256,1024]{1,2,0:T(8,128)(2,1)} copy(bf16[1,256,1024]{2,1,0:T(8,128)(2,1)} %param.10) | data formatting | bytes 1048576 | tf_op args[4]
  37.2 1.6 collective-permute-done.5
  39.8 0.7 collective-permute-done.6
  40.9 1.1 pad_maximum_fusion.4
  42.0 1.1 reshape_reshape.12
  44.4 1.4 pad_maximum_fusion
  45.8 1.5 slice_bitcast_fusion
  47.3 18.3 %shard_map.93 = (bf16[256,1024]{1,0:T(8,128)(2,1)}, f32[1024,1024]{1,0:T(8,128)}) custom-call(bf16[256,1024]{1,0:T(8,128)(2,1)} %bitcast.143, bf16[512,1024]{1,0:T(8,128)(2,1)} %get-tuple-element.35.k_ref, bf16[512,1024]{1,0:T(8,128)(2,1)} %get-tuple-element.34.v_ref, bf16[64,1024]{1,0:T(8,128)(2,1)} %get-tuple-element.41.ck_ref, ...), custom_call_target="tpu_custom_call" | custom-call | tf_op jit(solution)/shard_map/pallas_call | solution.py:125
  65.7 1.0 copy-done.4
  66.6 1.5 convolution_convert_fusion.g_ref
  68.2 20.4 %shard_map.94 = (bf16[256,1024]{1,0:T(8,128)(2,1)}, f32[512,1024]{1,0:T(8,128)}, f32[512,1024]{1,0:T(8,128)}, f32[64,1024]{1,0:T(8,128)}, f32[64,1024]{1,0:T(8,128)}) custom-call(bf16[256,1024]{1,0:T(8,128)(2,1)} %bitcast.144, bf16[512,1024]{1,0:T(8,128)(2,1)} %get-tuple-element.35.k_ref, bf16[512,1024]{1,0:T(8,128)(2,1)} %get-tuple-element.34.v_ref, ...), custom_call_target="tpu_custom_call" | custom-call | tf_op jit(solution)/shard_map/pallas_call | solution.py:232
  88.6 1.1 pad_maximum_fusion.3
  90.3 1.4 collective-permute-done.9
  92.3 1.7 slice_bitcast_fusion.2
  94.0 3.4 %collective-permute-done.10 = f32[2,2,2,2,2048]{4,3,2,1,0:T(2,128)S(1)} collective-permute-done((f32[2,2,2,2,2048]{4,3,2,1,0:T(2,128)S(1)}, f32[2,2,2,2,2048]{4,3,2,1,0:T(2,128)S(1)}, u32[]{:S(2)}, u32[]{:S(2)}) %collective-permute-start.10) | collective-permute-done | bytes 131104 | tf_op jit(solution)/shard_map/ppermute | solution.py:65
  97.8 2.1 %collective-permute-start.7 = (f32[2,128,1024]{2,1,0:T(8,128)S(1)}, f32[2,128,1024]{2,1,0:T(8,128)}, u32[]{:S(2)}, u32[]{:S(2)}) collective-permute-start(f32[2,128,1024]{2,1,0:T(8,128)S(1)} %pad_maximum_fusion.1), channel_id=1, source_target_pairs={{0,1},{1,2},{2,3},{3,4},{4,5},{5,6},{6,7},{7,8},{8,9},{9,10},{10,1... | collective-permute-start | bytes 3145736 | tf_op jit(solution)/shard_map/ppermute | solution.py:32
  99.9 3.5 %collective-permute-done.11 = f32[2,2,2,2048]{3,2,1,0:T(2,128)S(1)} collective-permute-done((f32[2,2,2,2048]{3,2,1,0:T(2,128)S(1)}, f32[2,2,2,2048]{3,2,1,0:T(2,128)S(1)}, u32[]{:S(2)}, u32[]{:S(2)}) %collective-permute-start.11) | collective-permute-done | bytes 65568 | tf_op jit(solution)/shard_map/ppermute | solution.py:65
  103.6 1.1 pad_maximum_fusion.2
  104.6 2.0 %collective-permute-start.8 = (f32[2,128,1024]{2,1,0:T(8,128)}, f32[2,128,1024]{2,1,0:T(8,128)}, u32[]{:S(2)}, u32[]{:S(2)}) collective-permute-start(f32[2,128,1024]{2,1,0:T(8,128)} %pad_maximum_fusion.2), channel_id=1, source_target_pairs={{1,0},{2,1},{3,2},{4,3},{5,4},{6,5},{7,6},{8,7},{9,8},{10,9},{11,1... | collective-permute-start | bytes 3145736 | tf_op jit(solution)/shard_map/ppermute | solution.py:32
  106.7 9.8 %collective-permute-done.12 = f32[2,2,2048]{2,1,0:T(2,128)S(1)} collective-permute-done((f32[2,2,2048]{2,1,0:T(2,128)S(1)}, f32[2,2,2048]{2,1,0:T(2,128)S(1)}, u32[]{:S(2)}, u32[]{:S(2)}) %collective-permute-start.12) | collective-permute-done | bytes 32800 | tf_op jit(solution)/shard_map/ppermute | solution.py:65
  116.6 1.3 collective-permute-start.13
  117.9 4.2 %collective-permute-done.13 = f32[2,2048]{1,0:T(2,128)S(1)} collective-permute-done((f32[2,2048]{1,0:T(2,128)S(1)}, f32[2,2048]{1,0:T(2,128)S(1)}, u32[]{:S(2)}, u32[]{:S(2)}) %collective-permute-start.13) | collective-permute-done | bytes 16416 | tf_op jit(solution)/shard_map/ppermute | solution.py:65
  122.3 1.8 pad_add_fusion
  125.3 1.3 fusion.2
  126.6 30.1 %reduce-scatter.2.cloned.1.call-done = f32[32,1024]{1,0:T(8,128)} async-done(((f32[1024,1024]{1,0:T(8,128)}), f32[32,1024]{1,0:T(8,128)}) %reduce-scatter.2.cloned.1.call-update) | async-done | bytes 131088 | tf_op jit(solution)/shard_map/reduce_scatter | solution.py:340
  156.7 0.9 reshape_reshape.14
  157.7 1.6 collective-permute-start.14
  159.3 2.7 %collective-permute-done.14 = f32[2,2,4,1024]{3,2,1,0:T(4,128)S(1)} collective-permute-done((f32[2,2,4,1024]{3,2,1,0:T(4,128)S(1)}, f32[2,2,4,1024]{3,2,1,0:T(4,128)S(1)}, u32[]{:S(2)}, u32[]{:S(2)}) %collective-permute-start.14) | collective-permute-done | bytes 65568 | tf_op jit(solution)/shard_map/ppermute | solution.py:65
  162.1 3.0 %collective-permute-start.15 = (f32[2,4,1024]{2,1,0:T(4,128)S(1)}, f32[2,4,1024]{2,1,0:T(4,128)S(1)}, u32[]{:S(2)}, u32[]{:S(2)}) collective-permute-start(f32[2,4,1024]{2,1,0:T(4,128)S(1)} %dynamic-slice_bitcast_fusion.3), channel_id=1, source_target_pairs={{0,64},{32,96},{64,0},{96,32},{128,192},{160,224},{192,128},{224,1... | collective-permute-start | bytes 98312 | tf_op jit(solution)/shard_map/ppermute | solution.py:65
  165.0 1.9 collective-permute-done.15
  167.0 5.9 %collective-permute-start.16 = (f32[4,1024]{1,0:T(4,128)S(1)}, f32[4,1024]{1,0:T(4,128)S(1)}, u32[]{:S(2)}, u32[]{:S(2)}) collective-permute-start(f32[4,1024]{1,0:T(4,128)S(1)} %dynamic-slice_bitcast_fusion.5), channel_id=1, source_target_pairs={{0,128},{32,160},{64,192},{96,224},{128,0},{160,32},{192,64},{224,... | collective-permute-start | bytes 49160 | tf_op jit(solution)/shard_map/ppermute | solution.py:65
  172.9 1.9 collective-permute-done.16
  174.8 5.8 %collective-permute-start.17 = (f32[4,1024]{1,0:T(4,128)S(1)}, f32[4,1024]{1,0:T(4,128)S(1)}, u32[]{:S(2)}, u32[]{:S(2)}) collective-permute-start(f32[4,1024]{1,0:T(4,128)S(1)} %bitcast_add_fusion.8), channel_id=1, source_target_pairs={{0,128},{32,160},{64,192},{96,224},{128,0},{160,32},{192,64},{224,... | collective-permute-start | bytes 49160 | tf_op jit(solution)/shard_map/ppermute | solution.py:48
  180.5 2.0 collective-permute-done.17
  182.5 3.1 %collective-permute-start.18 = (f32[2,4,1024]{2,1,0:T(4,128)S(1)}, f32[2,4,1024]{2,1,0:T(4,128)S(1)}, u32[]{:S(2)}, u32[]{:S(2)}) collective-permute-start(f32[2,4,1024]{2,1,0:T(4,128)S(1)} %pad_maximum_fusion.10), channel_id=1, source_target_pairs={{0,64},{32,96},{64,0},{96,32},{128,192},{160,224},{192,128},{224,1... | collective-permute-start | bytes 98312 | tf_op jit(solution)/shard_map/ppermute | solution.py:48
  185.6 1.9 collective-permute-done.18
  187.5 1.6 collective-permute-start.19
  189.1 2.7 %collective-permute-done.19 = f32[2,2,4,1024]{3,2,1,0:T(4,128)S(1)} collective-permute-done((f32[2,2,4,1024]{3,2,1,0:T(4,128)S(1)}, f32[2,2,4,1024]{3,2,1,0:T(4,128)S(1)}, u32[]{:S(2)}, u32[]{:S(2)}) %collective-permute-start.19) | collective-permute-done | bytes 65568 | tf_op jit(solution)/shard_map/ppermute | solution.py:48
  (73 shorter events, 8.4 us)
Async XLA Ops:
  7.2 58.5 %copy-start = (bf16[1024,1024]{1,0:T(8,128)(2,1)S(1)}, bf16[1024,1024]{1,0:T(8,128)(2,1)}, u32[]{:S(2)}) copy-start(bf16[1024,1024]{1,0:T(8,128)(2,1)} %param.9) | copy-start | bytes 6291460
  7.2 149.5 %reduce-scatter.2.cloned.1.call-start = ((), (), s32[]{:S(2)}) async-start(), calls=%async_computation.1 | async-start | bytes 4325376 | tf_op jit(solution)/shard_map/reduce_scatter | solution.py:340
  7.2 7.0 %copy-start.1 = (bf16[1,256,1024]{2,1,0:T(8,128)(2,1)S(1)}, bf16[1,256,1024]{2,1,0:T(8,128)(2,1)}, u32[]{:S(2)}) copy-start(bf16[1,256,1024]{2,1,0:T(8,128)(2,1)} %param.8) | copy-start | bytes 1572868
  10.8 12.3 %collective-permute-start.2 = (bf16[2,2176]{1,0:T(2,128)(2,1)S(1)}, bf16[2,2176]{1,0:T(2,128)(2,1)S(1)}, u32[]{:S(2)}, u32[]{:S(2)}) collective-permute-start(bf16[2,2176]{1,0:T(2,128)(2,1)S(1)} %pad_maximum_fusion.12), channel_id=1, source_target_pairs={{0,16},{1,17},{2,18},{3,19},{4,20},{5,21},{6,22},{7,23},{8,24},{9,... | collective-permute-start | bytes 26120 | tf_op jit(solution)/shard_map/ppermute | solution.py:48
  15.4 29.0 %collective-permute-start = (bf16[2,128,1024]{2,1,0:T(8,128)(2,1)}, bf16[2,128,1024]{2,1,0:T(8,128)(2,1)}, u32[]{:S(2)}, u32[]{:S(2)}) collective-permute-start(bf16[2,128,1024]{2,1,0:T(8,128)(2,1)} %get-tuple-element.36), channel_id=1, source_target_pairs={{0,1},{1,2},{2,3},{3,4},{4,5},{5,6},{6,7},{7,8},{8,9},{9,10},{10,1... | collective-permute-start | bytes 1572872 | tf_op jit(solution)/shard_map/ppermute | solution.py:21
  17.3 27.1 %collective-permute-start.1 = (bf16[2,128,1024]{2,1,0:T(8,128)(2,1)}, bf16[2,128,1024]{2,1,0:T(8,128)(2,1)}, u32[]{:S(2)}, u32[]{:S(2)}) collective-permute-start(bf16[2,128,1024]{2,1,0:T(8,128)(2,1)} %get-tuple-element.37), channel_id=1, source_target_pairs={{1,0},{2,1},{3,2},{4,3},{5,4},{6,5},{7,6},{8,7},{9,8},{10,9},{11,1... | collective-permute-start | bytes 1572872 | tf_op jit(solution)/shard_map/ppermute | solution.py:24
  23.2 5.4 %collective-permute-start.3 = (bf16[2,2,2176]{2,1,0:T(2,128)(2,1)S(1)}, bf16[2,2,2176]{2,1,0:T(2,128)(2,1)S(1)}, u32[]{:S(2)}, u32[]{:S(2)}) collective-permute-start(bf16[2,2,2176]{2,1,0:T(2,128)(2,1)S(1)} %pad_maximum_fusion.11), channel_id=1, source_target_pairs={{0,8},{1,9},{2,10},{3,11},{4,12},{5,13},{6,14},{7,15},{8,0},{9,1},... | collective-permute-start | bytes 52232 | tf_op jit(solution)/shard_map/ppermute | solution.py:48
  28.7 5.5 %collective-permute-start.4 = (bf16[2,2,2,2176]{3,2,1,0:T(2,128)(2,1)S(1)}, bf16[2,2,2,2176]{3,2,1,0:T(2,128)(2,1)S(1)}, u32[]{:S(2)}, u32[]{:S(2)}) collective-permute-start(bf16[2,2,2,2176]{3,2,1,0:T(2,128)(2,1)S(1)} %pad_maximum_fusion.9), channel_id=1, source_target_pairs={{0,4},{1,5},{2,6},{3,7},{4,0},{5,1},{6,2},{7,3},{8,12},{9,13},{10,... | collective-permute-start | bytes 104456 | tf_op jit(solution)/shard_map/ppermute | solution.py:48
  34.4 4.4 %collective-permute-start.5 = (bf16[2,2,2,2,2176]{4,3,2,1,0:T(2,128)(2,1)S(1)}, bf16[2,2,2,2,2176]{4,3,2,1,0:T(2,128)(2,1)S(1)}, u32[]{:S(2)}, u32[]{:S(2)}) collective-permute-start(bf16[2,2,2,2,2176]{4,3,2,1,0:T(2,128)(2,1)S(1)} %pad_maximum_fusion.7), channel_id=1, source_target_pairs={{0,2},{1,3},{2,0},{3,1},{4,6},{5,7},{6,4},{7,5},{8,10},{9,11},{10,... | collective-permute-start | bytes 208904 | tf_op jit(solution)/shard_map/ppermute | solution.py:48
  39.1 1.4 collective-permute-start.6
  65.6 1.0 copy-start.4
  90.0 1.6 collective-permute-start.9
  91.8 5.6 %collective-permute-start.10 = (f32[2,2,2,2,2048]{4,3,2,1,0:T(2,128)S(1)}, f32[2,2,2,2,2048]{4,3,2,1,0:T(2,128)S(1)}, u32[]{:S(2)}, u32[]{:S(2)}) collective-permute-start(f32[2,2,2,2,2048]{4,3,2,1,0:T(2,128)S(1)} %dynamic-slice_bitcast_fusion), channel_id=1, source_target_pairs={{0,2},{1,3},{2,0},{3,1},{4,6},{5,7},{6,4},{7,5},{8,10},{9,11},{10,... | collective-permute-start | bytes 393224 | tf_op jit(solution)/shard_map/ppermute | solution.py:65
  97.5 5.9 %collective-permute-start.11 = (f32[2,2,2,2048]{3,2,1,0:T(2,128)S(1)}, f32[2,2,2,2048]{3,2,1,0:T(2,128)S(1)}, u32[]{:S(2)}, u32[]{:S(2)}) collective-permute-start(f32[2,2,2,2048]{3,2,1,0:T(2,128)S(1)} %dynamic-slice_bitcast_fusion.2), channel_id=1, source_target_pairs={{0,4},{1,5},{2,6},{3,7},{4,0},{5,1},{6,2},{7,3},{8,12},{9,13},{10,... | collective-permute-start | bytes 196616 | tf_op jit(solution)/shard_map/ppermute | solution.py:65
  97.8 24.4 %collective-permute-start.7 = (f32[2,128,1024]{2,1,0:T(8,128)S(1)}, f32[2,128,1024]{2,1,0:T(8,128)}, u32[]{:S(2)}, u32[]{:S(2)}) collective-permute-start(f32[2,128,1024]{2,1,0:T(8,128)S(1)} %pad_maximum_fusion.1), channel_id=1, source_target_pairs={{0,1},{1,2},{2,3},{3,4},{4,5},{5,6},{6,7},{7,8},{8,9},{9,10},{10,1... | collective-permute-start | bytes 3145736 | tf_op jit(solution)/shard_map/ppermute | solution.py:32
  103.5 13.1 %collective-permute-start.12 = (f32[2,2,2048]{2,1,0:T(2,128)S(1)}, f32[2,2,2048]{2,1,0:T(2,128)S(1)}, u32[]{:S(2)}, u32[]{:S(2)}) collective-permute-start(f32[2,2,2048]{2,1,0:T(2,128)S(1)} %dynamic-slice_bitcast_fusion.4), channel_id=1, source_target_pairs={{0,8},{1,9},{2,10},{3,11},{4,12},{5,13},{6,14},{7,15},{8,0},{9,1},... | collective-permute-start | bytes 98312 | tf_op jit(solution)/shard_map/ppermute | solution.py:65
  104.6 17.7 %collective-permute-start.8 = (f32[2,128,1024]{2,1,0:T(8,128)}, f32[2,128,1024]{2,1,0:T(8,128)}, u32[]{:S(2)}, u32[]{:S(2)}) collective-permute-start(f32[2,128,1024]{2,1,0:T(8,128)} %pad_maximum_fusion.2), channel_id=1, source_target_pairs={{1,0},{2,1},{3,2},{4,3},{5,4},{6,5},{7,6},{8,7},{9,8},{10,9},{11,1... | collective-permute-start | bytes 3145736 | tf_op jit(solution)/shard_map/ppermute | solution.py:32
  116.6 5.5 %collective-permute-start.13 = (f32[2,2048]{1,0:T(2,128)S(1)}, f32[2,2048]{1,0:T(2,128)S(1)}, u32[]{:S(2)}, u32[]{:S(2)}) collective-permute-start(f32[2,2048]{1,0:T(2,128)S(1)} %dynamic-slice_bitcast_fusion.6), channel_id=1, source_target_pairs={{0,16},{1,17},{2,18},{3,19},{4,20},{5,21},{6,22},{7,23},{8,24},{9,... | collective-permute-start | bytes 49160 | tf_op jit(solution)/shard_map/ppermute | solution.py:65
  122.3 2.3 %copy-start.2 = (f32[512,1024]{1,0:T(8,128)S(1)}, f32[512,1024]{1,0:T(8,128)}, u32[]{:S(2)}) copy-start(f32[512,1024]{1,0:T(8,128)} %get-tuple-element.20) | copy-start | bytes 6291460
  122.3 3.0 %copy-start.3 = (f32[512,1024]{1,0:T(8,128)S(1)}, f32[512,1024]{1,0:T(8,128)}, u32[]{:S(2)}) copy-start(f32[512,1024]{1,0:T(8,128)} %get-tuple-element.21) | copy-start | bytes 6291460
  157.7 4.4 %collective-permute-start.14 = (f32[2,2,4,1024]{3,2,1,0:T(4,128)S(1)}, f32[2,2,4,1024]{3,2,1,0:T(4,128)S(1)}, u32[]{:S(2)}, u32[]{:S(2)}) collective-permute-start(f32[2,2,4,1024]{3,2,1,0:T(4,128)S(1)} %dynamic-slice_bitcast_fusion.1), channel_id=1, source_target_pairs={{0,32},{32,0},{64,96},{96,64},{128,160},{160,128},{192,224},{224,1... | collective-permute-start | bytes 196616 | tf_op jit(solution)/shard_map/ppermute | solution.py:65
  162.1 4.9 %collective-permute-start.15 = (f32[2,4,1024]{2,1,0:T(4,128)S(1)}, f32[2,4,1024]{2,1,0:T(4,128)S(1)}, u32[]{:S(2)}, u32[]{:S(2)}) collective-permute-start(f32[2,4,1024]{2,1,0:T(4,128)S(1)} %dynamic-slice_bitcast_fusion.3), channel_id=1, source_target_pairs={{0,64},{32,96},{64,0},{96,32},{128,192},{160,224},{192,128},{224,1... | collective-permute-start | bytes 98312 | tf_op jit(solution)/shard_map/ppermute | solution.py:65
  167.0 7.7 %collective-permute-start.16 = (f32[4,1024]{1,0:T(4,128)S(1)}, f32[4,1024]{1,0:T(4,128)S(1)}, u32[]{:S(2)}, u32[]{:S(2)}) collective-permute-start(f32[4,1024]{1,0:T(4,128)S(1)} %dynamic-slice_bitcast_fusion.5), channel_id=1, source_target_pairs={{0,128},{32,160},{64,192},{96,224},{128,0},{160,32},{192,64},{224,... | collective-permute-start | bytes 49160 | tf_op jit(solution)/shard_map/ppermute | solution.py:65
  174.8 7.8 %collective-permute-start.17 = (f32[4,1024]{1,0:T(4,128)S(1)}, f32[4,1024]{1,0:T(4,128)S(1)}, u32[]{:S(2)}, u32[]{:S(2)}) collective-permute-start(f32[4,1024]{1,0:T(4,128)S(1)} %bitcast_add_fusion.8), channel_id=1, source_target_pairs={{0,128},{32,160},{64,192},{96,224},{128,0},{160,32},{192,64},{224,... | collective-permute-start | bytes 49160 | tf_op jit(solution)/shard_map/ppermute | solution.py:48
  182.5 5.0 %collective-permute-start.18 = (f32[2,4,1024]{2,1,0:T(4,128)S(1)}, f32[2,4,1024]{2,1,0:T(4,128)S(1)}, u32[]{:S(2)}, u32[]{:S(2)}) collective-permute-start(f32[2,4,1024]{2,1,0:T(4,128)S(1)} %pad_maximum_fusion.10), channel_id=1, source_target_pairs={{0,64},{32,96},{64,0},{96,32},{128,192},{160,224},{192,128},{224,1... | collective-permute-start | bytes 98312 | tf_op jit(solution)/shard_map/ppermute | solution.py:48
  187.5 4.4 %collective-permute-start.19 = (f32[2,2,4,1024]{3,2,1,0:T(4,128)S(1)}, f32[2,2,4,1024]{3,2,1,0:T(4,128)S(1)}, u32[]{:S(2)}, u32[]{:S(2)}) collective-permute-start(f32[2,2,4,1024]{3,2,1,0:T(4,128)S(1)} %pad_maximum_fusion.8), channel_id=1, source_target_pairs={{0,32},{32,0},{64,96},{96,64},{128,160},{160,128},{192,224},{224,1... | collective-permute-start | bytes 196616 | tf_op jit(solution)/shard_map/ppermute | solution.py:48
Sparse Core Ops, SparseCore 0:
  65.8 90.9 reduce-scatter.1

commit v4 on v2

--- a/solution.py
+++ b/solution.py
@@ -32,8 +32,8 @@
     return lax.ppermute(value, axis, [(source, source + steps) for source in range(leading, last)])
 
 
-def xor_pairs(count, bit):
-    return [(source, source ^ (1 << bit)) for source in range(count)]
+def xor_pairs(count, bit, mask=1):
+    return [(source, source ^ (mask << bit)) for source in range(count)]
 
 
 def own_bit(axis, bit):
@@ -260,6 +260,23 @@
       attended_rows)
 
 
+def grouped_gather(piece, axis):
+    count = lax.axis_size(axis)
+    bits = count.bit_length() - 1
+    me = lax.axis_index(axis)
+    groups = [(low, min(2, bits - low)) for low in range(0, bits, 2)][::-1]
+    held = piece
+    for done, (low, width) in enumerate(groups):
+        size = 1 << width
+        arrived = [held] + [
+            lax.ppermute(held, axis, xor_pairs(count, low, mask)) for mask in range(1, size)
+        ]
+        mine = (me // (1 << low)) % size
+        stacked = jnp.stack(arrived, axis=done)
+        held = jnp.take(stacked, jnp.arange(size) ^ mine, axis=done)
+    return held.reshape((count,) + piece.shape)
+
+
 def block_windows(padded, local_blocks):
     return jnp.concatenate(
         [padded[0:local_blocks], padded[1 : local_blocks + 1], padded[2 : local_blocks + 2]], axis=1
@@ -306,7 +323,7 @@
     coarse_values = (value_sum / divisor[:, None]).astype(jnp.bfloat16)
     count_cols = jnp.broadcast_to(counts.astype(jnp.bfloat16)[:, None], (local_blocks, 128))
     packed = jnp.concatenate([coarse_keys, coarse_values, count_cols], axis=1)
-    gathered = doubling_gather(packed, "seq").reshape(all_blocks, packed.shape[1])
+    gathered = grouped_gather(packed, "seq").reshape(all_blocks, packed.shape[1])
     gathered_keys = gathered[:, :model_width]
     gathered_values = gathered[:, model_width : 2 * model_width]
     gathered_counts = gathered[:, 2 * model_width].astype(jnp.float32)

time: 201 us -> 206 us (1.025)
  starting transfers between devices: 37.7 us -> 51.5 us
  waiting for transfers between devices: 78.8 us -> 66.8 us
  local copies, waits for them, and re-layouts: 13.6 us -> 18.4 us
    ppermute x8 -> x3, waiting for transfers between devices: 19.5 us -> 6.71 us  [doubling_gather(): other = lax.ppermute(held, axis, xor_pairs(count, bit))]
    ppermute x0 -> x7, starting transfers between devices: none -> 9.4 us  [grouped_gather(): lax.ppermute(held, axis, xor_pairs(count, low, mask))]
    gather x0 -> x5, local copies, waits for them, and re-layouts: none -> 5.7 us  [grouped_gather(): held = jnp.take(stacked, jnp.arange(size) ^ mine, axis=done)]
    ppermute x0 -> x7, waiting for transfers between devices: none -> 5.66 us  [grouped_gather(): lax.ppermute(held, axis, xor_pairs(count, low, mask))]
    ppermute x8, starting transfers between devices: 12.7 us -> 17.8 us  [halving_scatter(): held = keep + lax.ppermute(send, axis, xor_pairs(count, bit))]
    ppermute x8, waiting for transfers between devices: 28.9 us -> 24.3 us  [halving_scatter(): held = keep + lax.ppermute(send, axis, xor_pairs(count, bit))]
    reduce_scatter x1, waiting for transfers between devices: 30.1 us -> 26 us  [per_device(): lax.psum_scatter(full_term, 'seq', scatter_dimension=0, tiled=True)]
    ppermute x2, waiting for transfers between devices: 0.09 us -> 4.13 us  [from_behind(): lax.ppermute(value, axis, [(source, source + steps) for source in range(l...]
  transfers between devices with their start and end apart: 21 -> 23, of which waited for: 17 -> 16; matrix products, arithmetic and copies ran while one was open for 10% -> 11% of each run, Pallas kernels for 10% -> 10%
where the time goes in v4:
time: 206 us; the launch traced here: 205 us
  waiting for transfers between devices  66.8 us (32%)
  starting transfers between devices  51.5 us (25%)
  Pallas kernels  38.6 us (19%)
  local copies, waits for them, and re-layouts  18.4 us (9%)
  between operations  14.7 us (7%)
  other arithmetic  11.4 us (6%)
  matrix products  3.95 us (2%)
    reduce_scatter x1, waiting for transfers between devices, per_device(): lax.psum_scatter(full_term, 'seq', scatter_dimension=0, tiled=True)  26 us
    ppermute x8, waiting for transfers between devices, halving_scatter(): held = keep + lax.ppermute(send, axis, xor_pairs(count, bit))  24.3 us
    pallas_call x1, Pallas kernels, attention_backward(): pl.pallas_call(backward_kernel, grid=(width // lanes,), in_specs=[by_pair...  20.4 us
    pallas_call x1, Pallas kernels, attention_forward(): pl.pallas_call(functools.partial(forward_kernel, term_scale), grid=(width...  18.3 us
    ppermute x8, starting transfers between devices, halving_scatter(): held = keep + lax.ppermute(send, axis, xor_pairs(count, bit))  17.8 us
    ppermute x3, starting transfers between devices, doubling_gather(): other = lax.ppermute(held, axis, xor_pairs(count, bit))  10.3 us
    ppermute x7, starting transfers between devices, grouped_gather(): lax.ppermute(held, axis, xor_pairs(count, low, mask))  9.4 us
    ppermute x3, waiting for transfers between devices, doubling_gather(): other = lax.ppermute(held, axis, xor_pairs(count, bit))  6.71 us
  transfers between devices with their start and end apart: 23, of which 16 were waited for; matrix products, arithmetic and copies ran while one was open for 11% of the time, Pallas kernels for 10%

profile of v4, /device:TPU:8, one launch (start us, length us, event | category | flops | bytes accessed | tf_op | source)
XLA Modules:
  0.0 205.4 jit_solution(8181910379573816091)
XLA Ops:
  8.2 1.2 fusion.9
  9.4 1.2 fusion.11
  10.8 2.4 %collective-permute-start.2 = (bf16[2,2176]{1,0:T(2,128)(2,1)S(1)}, bf16[2,2176]{1,0:T(2,128)(2,1)S(1)}, u32[]{:S(2)}, u32[]{:S(2)}) collective-permute-start(bf16[2,2176]{1,0:T(2,128)(2,1)S(1)} %pad_maximum_fusion.10), channel_id=1, source_target_pairs={{0,16},{1,17},{2,18},{3,19},{4,20},{5,21},{6,22},{7,23},{8,24},{9,... | collective-permute-start | bytes 26120 | tf_op jit(solution)/shard_map/ppermute | solution.py:272
  15.4 1.9 collective-permute-start
  17.3 5.8 %collective-permute-start.1 = (bf16[2,128,1024]{2,1,0:T(8,128)(2,1)}, bf16[2,128,1024]{2,1,0:T(8,128)(2,1)}, u32[]{:S(2)}, u32[]{:S(2)}) collective-permute-start(bf16[2,128,1024]{2,1,0:T(8,128)(2,1)} %get-tuple-element.37), channel_id=1, source_target_pairs={{1,0},{2,1},{3,2},{4,3},{5,4},{6,5},{7,6},{8,7},{9,8},{10,9},{11,1... | collective-permute-start | bytes 1572872 | tf_op jit(solution)/shard_map/ppermute | solution.py:24
  24.8 2.0 copy.35
  27.6 1.8 collective-permute-start.5
  30.0 2.6 %collective-permute-start.3 = (bf16[2,2,2176]{2,1,0:T(2,128)(2,1)S(1)}, bf16[2,2,2176]{2,1,0:T(2,128)(2,1)S(1)}, u32[]{:S(2)}, u32[]{:S(2)}) collective-permute-start(bf16[2,2,2176]{2,1,0:T(2,128)(2,1)S(1)} %broadcast_select_fusion.3), channel_id=1, source_target_pairs={{0,4},{1,5},{2,6},{3,7},{4,0},{5,1},{6,2},{7,3},{8,12},{9,13},{10,... | collective-permute-start | bytes 52232 | tf_op jit(solution)/shard_map/ppermute | solution.py:272
  33.8 1.5 collective-permute-done.3
  37.0 1.2 collective-permute-start.6
  38.3 1.9 collective-permute-done.8
  40.2 1.3 collective-permute-done.7
  42.1 1.5 gather_fusion.2
  43.5 1.9 copy.34
  48.0 1.4 pad_maximum_fusion
  49.3 1.5 slice_bitcast_fusion
  50.9 18.3 %shard_map.93 = (bf16[256,1024]{1,0:T(8,128)(2,1)}, f32[1024,1024]{1,0:T(8,128)}) custom-call(bf16[256,1024]{1,0:T(8,128)(2,1)} %bitcast.149, bf16[512,1024]{1,0:T(8,128)(2,1)} %get-tuple-element.35.k_ref, bf16[512,1024]{1,0:T(8,128)(2,1)} %get-tuple-element.34.v_ref, bf16[64,1024]{1,0:T(8,128)(2,1)} %get-tuple-element.39.ck_ref, ...), custom_call_target="tpu_custom_call" | custom-call | tf_op jit(solution)/shard_map/pallas_call | solution.py:124
  70.2 1.5 convolution_convert_fusion.g_ref
  71.7 20.4 %shard_map.94 = (bf16[256,1024]{1,0:T(8,128)(2,1)}, f32[512,1024]{1,0:T(8,128)}, f32[512,1024]{1,0:T(8,128)}, f32[64,1024]{1,0:T(8,128)}, f32[64,1024]{1,0:T(8,128)}) custom-call(bf16[256,1024]{1,0:T(8,128)(2,1)} %bitcast.150, bf16[512,1024]{1,0:T(8,128)(2,1)} %get-tuple-element.35.k_ref, bf16[512,1024]{1,0:T(8,128)(2,1)} %get-tuple-element.34.v_ref, ...), custom_call_target="tpu_custom_call" | custom-call | tf_op jit(solution)/shard_map/pallas_call | solution.py:230
  92.1 1.1 pad_maximum_fusion.3
  93.9 1.6 slice_bitcast_fusion.3
  95.7 1.5 collective-permute-start.12
  97.3 4.0 %collective-permute-done.12 = f32[2,2,2,2,2048]{4,3,2,1,0:T(2,128)S(1)} collective-permute-done((f32[2,2,2,2,2048]{4,3,2,1,0:T(2,128)S(1)}, f32[2,2,2,2,2048]{4,3,2,1,0:T(2,128)S(1)}, u32[]{:S(2)}, u32[]{:S(2)}) %collective-permute-start.12) | collective-permute-done | bytes 131104 | tf_op jit(solution)/shard_map/ppermute | solution.py:65
  101.4 2.7 %collective-permute-start.13 = (f32[2,2,2,2048]{3,2,1,0:T(2,128)S(1)}, f32[2,2,2,2048]{3,2,1,0:T(2,128)S(1)}, u32[]{:S(2)}, u32[]{:S(2)}) collective-permute-start(f32[2,2,2,2048]{3,2,1,0:T(2,128)S(1)} %dynamic-slice_bitcast_fusion.3), channel_id=1, source_target_pairs={{0,4},{1,5},{2,6},{3,7},{4,0},{5,1},{6,2},{7,3},{8,12},{9,13},{10,... | collective-permute-start | bytes 196616 | tf_op jit(solution)/shard_map/ppermute | solution.py:65
  104.2 1.9 collective-permute-start.9
  106.1 1.1 collective-permute-done.13
  107.3 1.5 collective-permute-start.14
  108.8 1.1 pad_maximum_fusion.2
  109.9 4.3 %collective-permute-start.10 = (f32[2,128,1024]{2,1,0:T(8,128)}, f32[2,128,1024]{2,1,0:T(8,128)}, u32[]{:S(2)}, u32[]{:S(2)}) collective-permute-start(f32[2,128,1024]{2,1,0:T(8,128)} %pad_maximum_fusion.2), channel_id=1, source_target_pairs={{1,0},{2,1},{3,2},{4,3},{5,4},{6,5},{7,6},{8,7},{9,8},{10,9},{11,1... | collective-permute-start | bytes 3145736 | tf_op jit(solution)/shard_map/ppermute | solution.py:32
  114.2 8.4 %collective-permute-done.14 = f32[2,2,2048]{2,1,0:T(2,128)S(1)} collective-permute-done((f32[2,2,2048]{2,1,0:T(2,128)S(1)}, f32[2,2,2048]{2,1,0:T(2,128)S(1)}, u32[]{:S(2)}, u32[]{:S(2)}) %collective-permute-start.14) | collective-permute-done | bytes 32800 | tf_op jit(solution)/shard_map/ppermute | solution.py:65
  122.6 1.3 collective-permute-start.15
  124.0 4.2 %collective-permute-done.15 = f32[2,2048]{1,0:T(2,128)S(1)} collective-permute-done((f32[2,2048]{1,0:T(2,128)S(1)}, f32[2,2048]{1,0:T(2,128)S(1)}, u32[]{:S(2)}, u32[]{:S(2)}) %collective-permute-start.15) | collective-permute-done | bytes 16416 | tf_op jit(solution)/shard_map/ppermute | solution.py:65
  128.3 4.1 %collective-permute-done.10 = f32[2,128,1024]{2,1,0:T(8,128)} collective-permute-done((f32[2,128,1024]{2,1,0:T(8,128)}, f32[2,128,1024]{2,1,0:T(8,128)}, u32[]{:S(2)}, u32[]{:S(2)}) %collective-permute-start.10) | collective-permute-done | bytes 1048608 | tf_op jit(solution)/shard_map/ppermute | solution.py:32
  132.4 1.8 pad_add_fusion
  135.4 1.3 fusion.2
  136.6 26.0 %reduce-scatter.2.cloned.1.call-done = f32[32,1024]{1,0:T(8,128)} async-done(((f32[1024,1024]{1,0:T(8,128)}), f32[32,1024]{1,0:T(8,128)}) %reduce-scatter.2.cloned.1.call-update) | async-done | bytes 131088 | tf_op jit(solution)/shard_map/reduce_scatter | solution.py:355
  163.6 1.6 collective-permute-start.16
  165.2 2.7 %collective-permute-done.16 = f32[2,2,4,1024]{3,2,1,0:T(4,128)S(1)} collective-permute-done((f32[2,2,4,1024]{3,2,1,0:T(4,128)S(1)}, f32[2,2,4,1024]{3,2,1,0:T(4,128)S(1)}, u32[]{:S(2)}, u32[]{:S(2)}) %collective-permute-start.16) | collective-permute-done | bytes 65568 | tf_op jit(solution)/shard_map/ppermute | solution.py:65
  168.0 3.0 %collective-permute-start.17 = (f32[2,4,1024]{2,1,0:T(4,128)S(1)}, f32[2,4,1024]{2,1,0:T(4,128)S(1)}, u32[]{:S(2)}, u32[]{:S(2)}) collective-permute-start(f32[2,4,1024]{2,1,0:T(4,128)S(1)} %dynamic-slice_bitcast_fusion.4), channel_id=1, source_target_pairs={{0,64},{32,96},{64,0},{96,32},{128,192},{160,224},{192,128},{224,1... | collective-permute-start | bytes 98312 | tf_op jit(solution)/shard_map/ppermute | solution.py:65
  170.9 1.9 collective-permute-done.17
  172.9 5.8 %collective-permute-start.18 = (f32[4,1024]{1,0:T(4,128)S(1)}, f32[4,1024]{1,0:T(4,128)S(1)}, u32[]{:S(2)}, u32[]{:S(2)}) collective-permute-start(f32[4,1024]{1,0:T(4,128)S(1)} %dynamic-slice_bitcast_fusion.6), channel_id=1, source_target_pairs={{0,128},{32,160},{64,192},{96,224},{128,0},{160,32},{192,64},{224,... | collective-permute-start | bytes 49160 | tf_op jit(solution)/shard_map/ppermute | solution.py:65
  178.7 1.9 collective-permute-done.18
  180.6 5.7 %collective-permute-start.19 = (f32[4,1024]{1,0:T(4,128)S(1)}, f32[4,1024]{1,0:T(4,128)S(1)}, u32[]{:S(2)}, u32[]{:S(2)}) collective-permute-start(f32[4,1024]{1,0:T(4,128)S(1)} %bitcast_add_fusion.8), channel_id=1, source_target_pairs={{0,128},{32,160},{64,192},{96,224},{128,0},{160,32},{192,64},{224,... | collective-permute-start | bytes 49160 | tf_op jit(solution)/shard_map/ppermute | solution.py:48
  186.4 2.0 collective-permute-done.19
  188.4 3.1 %collective-permute-start.20 = (f32[2,4,1024]{2,1,0:T(4,128)S(1)}, f32[2,4,1024]{2,1,0:T(4,128)S(1)}, u32[]{:S(2)}, u32[]{:S(2)}) collective-permute-start(f32[2,4,1024]{2,1,0:T(4,128)S(1)} %pad_maximum_fusion.8), channel_id=1, source_target_pairs={{0,64},{32,96},{64,0},{96,32},{128,192},{160,224},{192,128},{224,1... | collective-permute-start | bytes 98312 | tf_op jit(solution)/shard_map/ppermute | solution.py:48
  191.5 1.9 collective-permute-done.20
  193.4 1.6 collective-permute-start.21
  195.0 2.8 %collective-permute-done.21 = f32[2,2,4,1024]{3,2,1,0:T(4,128)S(1)} collective-permute-done((f32[2,2,4,1024]{3,2,1,0:T(4,128)S(1)}, f32[2,2,4,1024]{3,2,1,0:T(4,128)S(1)}, u32[]{:S(2)}, u32[]{:S(2)}) %collective-permute-start.21) | collective-permute-done | bytes 65568 | tf_op jit(solution)/shard_map/ppermute | solution.py:48
  (93 shorter events, 17.6 us)
Async XLA Ops:
  7.2 62.2 %copy-start = (bf16[1024,1024]{1,0:T(8,128)(2,1)S(1)}, bf16[1024,1024]{1,0:T(8,128)(2,1)}, u32[]{:S(2)}) copy-start(bf16[1024,1024]{1,0:T(8,128)(2,1)} %param.9) | copy-start | bytes 6291460
  7.2 155.4 %reduce-scatter.2.cloned.1.call-start = ((), (), s32[]{:S(2)}) async-start(), calls=%async_computation.1 | async-start | bytes 4325376 | tf_op jit(solution)/shard_map/reduce_scatter | solution.py:355
  7.2 7.0 %copy-start.1 = (bf16[1,256,1024]{2,1,0:T(8,128)(2,1)S(1)}, bf16[1,256,1024]{2,1,0:T(8,128)(2,1)}, u32[]{:S(2)}) copy-start(bf16[1,256,1024]{2,1,0:T(8,128)(2,1)} %param.8) | copy-start | bytes 1572868
  10.8 16.1 %collective-permute-start.2 = (bf16[2,2176]{1,0:T(2,128)(2,1)S(1)}, bf16[2,2176]{1,0:T(2,128)(2,1)S(1)}, u32[]{:S(2)}, u32[]{:S(2)}) collective-permute-start(bf16[2,2176]{1,0:T(2,128)(2,1)S(1)} %pad_maximum_fusion.10), channel_id=1, source_target_pairs={{0,16},{1,17},{2,18},{3,19},{4,20},{5,21},{6,22},{7,23},{8,24},{9,... | collective-permute-start | bytes 26120 | tf_op jit(solution)/shard_map/ppermute | solution.py:272
  15.4 32.6 %collective-permute-start = (bf16[2,128,1024]{2,1,0:T(8,128)(2,1)}, bf16[2,128,1024]{2,1,0:T(8,128)(2,1)}, u32[]{:S(2)}, u32[]{:S(2)}) collective-permute-start(bf16[2,128,1024]{2,1,0:T(8,128)(2,1)} %get-tuple-element.36), channel_id=1, source_target_pairs={{0,1},{1,2},{2,3},{3,4},{4,5},{5,6},{6,7},{7,8},{8,9},{9,10},{10,1... | collective-permute-start | bytes 1572872 | tf_op jit(solution)/shard_map/ppermute | solution.py:21
  17.3 30.7 %collective-permute-start.1 = (bf16[2,128,1024]{2,1,0:T(8,128)(2,1)}, bf16[2,128,1024]{2,1,0:T(8,128)(2,1)}, u32[]{:S(2)}, u32[]{:S(2)}) collective-permute-start(bf16[2,128,1024]{2,1,0:T(8,128)(2,1)} %get-tuple-element.37), channel_id=1, source_target_pairs={{1,0},{2,1},{3,2},{4,3},{5,4},{6,5},{7,6},{8,7},{9,8},{10,9},{11,1... | collective-permute-start | bytes 1572872 | tf_op jit(solution)/shard_map/ppermute | solution.py:24
  27.6 6.2 %collective-permute-start.5 = (bf16[2,2,2176]{2,1,0:T(2,128)(2,1)S(1)}, bf16[2,2,2176]{2,1,0:T(2,128)(2,1)S(1)}, u32[]{:S(2)}, u32[]{:S(2)}) collective-permute-start(bf16[2,2,2176]{2,1,0:T(2,128)(2,1)S(1)} %broadcast_select_fusion.3), channel_id=1, source_target_pairs={{0,12},{1,13},{2,14},{3,15},{4,8},{5,9},{6,10},{7,11},{8,4},{9,5},... | collective-permute-start | bytes 52232 | tf_op jit(solution)/shard_map/ppermute | solution.py:272
  29.4 4.5 %collective-permute-start.4 = (bf16[2,2,2176]{2,1,0:T(2,128)(2,1)S(1)}, bf16[2,2,2176]{2,1,0:T(2,128)(2,1)S(1)}, u32[]{:S(2)}, u32[]{:S(2)}) collective-permute-start(bf16[2,2,2176]{2,1,0:T(2,128)(2,1)S(1)} %broadcast_select_fusion.3), channel_id=1, source_target_pairs={{0,8},{1,9},{2,10},{3,11},{4,12},{5,13},{6,14},{7,15},{8,0},{9,1},... | collective-permute-start | bytes 52232 | tf_op jit(solution)/shard_map/ppermute | solution.py:272
  30.0 5.3 %collective-permute-start.3 = (bf16[2,2,2176]{2,1,0:T(2,128)(2,1)S(1)}, bf16[2,2,2176]{2,1,0:T(2,128)(2,1)S(1)}, u32[]{:S(2)}, u32[]{:S(2)}) collective-permute-start(bf16[2,2,2176]{2,1,0:T(2,128)(2,1)S(1)} %broadcast_select_fusion.3), channel_id=1, source_target_pairs={{0,4},{1,5},{2,6},{3,7},{4,0},{5,1},{6,2},{7,3},{8,12},{9,13},{10,... | collective-permute-start | bytes 52232 | tf_op jit(solution)/shard_map/ppermute | solution.py:272
  36.2 3.9 %collective-permute-start.8 = (bf16[2,4,2,2176]{3,2,0,1:T(2,128)(2,1)S(1)}, bf16[2,4,2,2176]{3,2,0,1:T(2,128)(2,1)S(1)}, u32[]{:S(2)}, u32[]{:S(2)}) collective-permute-start(bf16[2,4,2,2176]{3,2,0,1:T(2,128)(2,1)S(1)} %broadcast_select_fusion.1), channel_id=1, source_target_pairs={{0,3},{1,2},{2,1},{3,0},{4,7},{5,6},{6,5},{7,4},{8,11},{9,10},{10,... | collective-permute-start | bytes 208904 | tf_op jit(solution)/shard_map/ppermute | solution.py:272
  36.3 5.1 %collective-permute-start.7 = (bf16[2,4,2,2176]{3,2,0,1:T(2,128)(2,1)S(1)}, bf16[2,4,2,2176]{3,2,0,1:T(2,128)(2,1)S(1)}, u32[]{:S(2)}, u32[]{:S(2)}) collective-permute-start(bf16[2,4,2,2176]{3,2,0,1:T(2,128)(2,1)S(1)} %broadcast_select_fusion.1), channel_id=1, source_target_pairs={{0,2},{1,3},{2,0},{3,1},{4,6},{5,7},{6,4},{7,5},{8,10},{9,11},{10,... | collective-permute-start | bytes 208904 | tf_op jit(solution)/shard_map/ppermute | solution.py:272
  37.0 4.4 %collective-permute-start.6 = (bf16[2,4,2,2176]{3,2,0,1:T(2,128)(2,1)S(1)}, bf16[2,4,2,2176]{3,2,0,1:T(2,128)(2,1)S(1)}, u32[]{:S(2)}, u32[]{:S(2)}) collective-permute-start(bf16[2,4,2,2176]{3,2,0,1:T(2,128)(2,1)S(1)} %broadcast_select_fusion.1), channel_id=1, source_target_pairs={{0,1},{1,0},{2,3},{3,2},{4,5},{5,4},{6,7},{7,6},{8,9},{9,8},{10,11... | collective-permute-start | bytes 208904 | tf_op jit(solution)/shard_map/ppermute | solution.py:272
  69.2 1.0 copy-start.5
  93.5 3.7 %copy-start.3 = (f32[512,1024]{1,0:T(8,128)S(1)}, f32[512,1024]{1,0:T(8,128)}, u32[]{:S(2)}) copy-start(f32[512,1024]{1,0:T(8,128)} %get-tuple-element.21) | copy-start | bytes 6291460
  93.5 2.0 collective-permute-start.11
  95.7 5.6 %collective-permute-start.12 = (f32[2,2,2,2,2048]{4,3,2,1,0:T(2,128)S(1)}, f32[2,2,2,2,2048]{4,3,2,1,0:T(2,128)S(1)}, u32[]{:S(2)}, u32[]{:S(2)}) collective-permute-start(f32[2,2,2,2,2048]{4,3,2,1,0:T(2,128)S(1)} %dynamic-slice_bitcast_fusion.1), channel_id=1, source_target_pairs={{0,2},{1,3},{2,0},{3,1},{4,6},{5,7},{6,4},{7,5},{8,10},{9,11},{10,... | collective-permute-start | bytes 393224 | tf_op jit(solution)/shard_map/ppermute | solution.py:65
  101.4 5.9 %collective-permute-start.13 = (f32[2,2,2,2048]{3,2,1,0:T(2,128)S(1)}, f32[2,2,2,2048]{3,2,1,0:T(2,128)S(1)}, u32[]{:S(2)}, u32[]{:S(2)}) collective-permute-start(f32[2,2,2,2048]{3,2,1,0:T(2,128)S(1)} %dynamic-slice_bitcast_fusion.3), channel_id=1, source_target_pairs={{0,4},{1,5},{2,6},{3,7},{4,0},{5,1},{6,2},{7,3},{8,12},{9,13},{10,... | collective-permute-start | bytes 196616 | tf_op jit(solution)/shard_map/ppermute | solution.py:65
  104.2 24.1 %collective-permute-start.9 = (f32[2,128,1024]{2,1,0:T(8,128)S(1)}, f32[2,128,1024]{2,1,0:T(8,128)}, u32[]{:S(2)}, u32[]{:S(2)}) collective-permute-start(f32[2,128,1024]{2,1,0:T(8,128)S(1)} %pad_maximum_fusion.1), channel_id=1, source_target_pairs={{0,1},{1,2},{2,3},{3,4},{4,5},{5,6},{6,7},{7,8},{8,9},{9,10},{10,1... | collective-permute-start | bytes 3145736 | tf_op jit(solution)/shard_map/ppermute | solution.py:32
  107.3 15.3 %collective-permute-start.14 = (f32[2,2,2048]{2,1,0:T(2,128)S(1)}, f32[2,2,2048]{2,1,0:T(2,128)S(1)}, u32[]{:S(2)}, u32[]{:S(2)}) collective-permute-start(f32[2,2,2048]{2,1,0:T(2,128)S(1)} %dynamic-slice_bitcast_fusion.5), channel_id=1, source_target_pairs={{0,8},{1,9},{2,10},{3,11},{4,12},{5,13},{6,14},{7,15},{8,0},{9,1},... | collective-permute-start | bytes 98312 | tf_op jit(solution)/shard_map/ppermute | solution.py:65
  109.9 22.6 %collective-permute-start.10 = (f32[2,128,1024]{2,1,0:T(8,128)}, f32[2,128,1024]{2,1,0:T(8,128)}, u32[]{:S(2)}, u32[]{:S(2)}) collective-permute-start(f32[2,128,1024]{2,1,0:T(8,128)} %pad_maximum_fusion.2), channel_id=1, source_target_pairs={{1,0},{2,1},{3,2},{4,3},{5,4},{6,5},{7,6},{8,7},{9,8},{10,9},{11,1... | collective-permute-start | bytes 3145736 | tf_op jit(solution)/shard_map/ppermute | solution.py:32
  122.6 5.6 %collective-permute-start.15 = (f32[2,2048]{1,0:T(2,128)S(1)}, f32[2,2048]{1,0:T(2,128)S(1)}, u32[]{:S(2)}, u32[]{:S(2)}) collective-permute-start(f32[2,2048]{1,0:T(2,128)S(1)} %dynamic-slice_bitcast_fusion.7), channel_id=1, source_target_pairs={{0,16},{1,17},{2,18},{3,19},{4,20},{5,21},{6,22},{7,23},{8,24},{9,... | collective-permute-start | bytes 49160 | tf_op jit(solution)/shard_map/ppermute | solution.py:65
  132.4 2.3 %copy-start.2 = (f32[512,1024]{1,0:T(8,128)S(1)}, f32[512,1024]{1,0:T(8,128)}, u32[]{:S(2)}) copy-start(f32[512,1024]{1,0:T(8,128)} %get-tuple-element.20) | copy-start | bytes 6291460
  132.4 3.0 %copy-start.4 = (f32[512,1024]{1,0:T(8,128)S(1)}, f32[512,1024]{1,0:T(8,128)}, u32[]{:S(2)}) copy-start(f32[512,1024]{1,0:T(8,128)} %get-tuple-element.21) | copy-start | bytes 6291460
  163.6 4.4 %collective-permute-start.16 = (f32[2,2,4,1024]{3,2,1,0:T(4,128)S(1)}, f32[2,2,4,1024]{3,2,1,0:T(4,128)S(1)}, u32[]{:S(2)}, u32[]{:S(2)}) collective-permute-start(f32[2,2,4,1024]{3,2,1,0:T(4,128)S(1)} %dynamic-slice_bitcast_fusion.2), channel_id=1, source_target_pairs={{0,32},{32,0},{64,96},{96,64},{128,160},{160,128},{192,224},{224,1... | collective-permute-start | bytes 196616 | tf_op jit(solution)/shard_map/ppermute | solution.py:65
  168.0 4.9 %collective-permute-start.17 = (f32[2,4,1024]{2,1,0:T(4,128)S(1)}, f32[2,4,1024]{2,1,0:T(4,128)S(1)}, u32[]{:S(2)}, u32[]{:S(2)}) collective-permute-start(f32[2,4,1024]{2,1,0:T(4,128)S(1)} %dynamic-slice_bitcast_fusion.4), channel_id=1, source_target_pairs={{0,64},{32,96},{64,0},{96,32},{128,192},{160,224},{192,128},{224,1... | collective-permute-start | bytes 98312 | tf_op jit(solution)/shard_map/ppermute | solution.py:65
  172.9 7.7 %collective-permute-start.18 = (f32[4,1024]{1,0:T(4,128)S(1)}, f32[4,1024]{1,0:T(4,128)S(1)}, u32[]{:S(2)}, u32[]{:S(2)}) collective-permute-start(f32[4,1024]{1,0:T(4,128)S(1)} %dynamic-slice_bitcast_fusion.6), channel_id=1, source_target_pairs={{0,128},{32,160},{64,192},{96,224},{128,0},{160,32},{192,64},{224,... | collective-permute-start | bytes 49160 | tf_op jit(solution)/shard_map/ppermute | solution.py:65
  180.6 7.7 %collective-permute-start.19 = (f32[4,1024]{1,0:T(4,128)S(1)}, f32[4,1024]{1,0:T(4,128)S(1)}, u32[]{:S(2)}, u32[]{:S(2)}) collective-permute-start(f32[4,1024]{1,0:T(4,128)S(1)} %bitcast_add_fusion.8), channel_id=1, source_target_pairs={{0,128},{32,160},{64,192},{96,224},{128,0},{160,32},{192,64},{224,... | collective-permute-start | bytes 49160 | tf_op jit(solution)/shard_map/ppermute | solution.py:48
  188.4 4.9 %collective-permute-start.20 = (f32[2,4,1024]{2,1,0:T(4,128)S(1)}, f32[2,4,1024]{2,1,0:T(4,128)S(1)}, u32[]{:S(2)}, u32[]{:S(2)}) collective-permute-start(f32[2,4,1024]{2,1,0:T(4,128)S(1)} %pad_maximum_fusion.8), channel_id=1, source_target_pairs={{0,64},{32,96},{64,0},{96,32},{128,192},{160,224},{192,128},{224,1... | collective-permute-start | bytes 98312 | tf_op jit(solution)/shard_map/ppermute | solution.py:48
  193.4 4.4 %collective-permute-start.21 = (f32[2,2,4,1024]{3,2,1,0:T(4,128)S(1)}, f32[2,2,4,1024]{3,2,1,0:T(4,128)S(1)}, u32[]{:S(2)}, u32[]{:S(2)}) collective-permute-start(f32[2,2,4,1024]{3,2,1,0:T(4,128)S(1)} %pad_maximum_fusion.7), channel_id=1, source_target_pairs={{0,32},{32,0},{64,96},{96,64},{128,160},{160,128},{192,224},{224,1... | collective-permute-start | bytes 196616 | tf_op jit(solution)/shard_map/ppermute | solution.py:48
Sparse Core Ops, SparseCore 0:
  69.3 93.2 reduce-scatter.1

commit v5 on v2

--- a/solution.py
+++ b/solution.py
@@ -46,11 +46,9 @@
     held = piece
     for done, bit in enumerate(reversed(range(bits))):
         other = lax.ppermute(held, axis, xor_pairs(count, bit))
-        mine_low = own_bit(axis, bit) == 0
-        low = jnp.where(mine_low, held, other)
-        high = jnp.where(mine_low, other, held)
-        held = jnp.stack([low, high], axis=done)
-    return held.reshape((count,) + piece.shape)
+        held = jnp.stack([held, other], axis=done)
+    held = held.reshape((count,) + piece.shape)
+    return jnp.take(held, jnp.arange(count) ^ lax.axis_index(axis), axis=0)
 
 
 def halving_scatter(stack, axis):

time: 201 us -> 207 us (1.030)
  starting transfers between devices: 37.7 us -> 44.7 us
  local copies, waits for them, and re-layouts: 13.6 us -> 15.7 us
  waiting for transfers between devices: 78.8 us -> 76.7 us
    ppermute x8, waiting for transfers between devices: 28.9 us -> 25.4 us  [halving_scatter(): held = keep + lax.ppermute(send, axis, xor_pairs(count, bit))]
    gather x0 -> x4, local copies, waits for them, and re-layouts: none -> 3.53 us  [doubling_gather(): return jnp.take(held, jnp.arange(count) ^ lax.axis_index(axis), axis=0)]
    ppermute x8, starting transfers between devices: 12.7 us -> 16.1 us  [halving_scatter(): held = keep + lax.ppermute(send, axis, xor_pairs(count, bit))]
    ppermute x2, starting transfers between devices: 4.15 us -> 6.82 us  [from_behind(): lax.ppermute(value, axis, [(source, source + steps) for source in range(l...]
where the time goes in v5:
time: 207 us; the launch traced here: 206 us
  waiting for transfers between devices  76.7 us (37%)
  starting transfers between devices  44.7 us (22%)
  Pallas kernels  38.6 us (19%)
  local copies, waits for them, and re-layouts  15.7 us (8%)
  between operations  14.4 us (7%)
  other arithmetic  12.2 us (6%)
  matrix products  3.95 us (2%)
    reduce_scatter x1, waiting for transfers between devices, per_device(): lax.psum_scatter(full_term, 'seq', scatter_dimension=0, tiled=True)  29.3 us
    ppermute x8, waiting for transfers between devices, halving_scatter(): held = keep + lax.ppermute(send, axis, xor_pairs(count, bit))  25.4 us
    pallas_call x1, Pallas kernels, attention_backward(): pl.pallas_call(backward_kernel, grid=(width // lanes,), in_specs=[by_pair...  20.4 us
    ppermute x8, waiting for transfers between devices, doubling_gather(): other = lax.ppermute(held, axis, xor_pairs(count, bit))  20 us
    pallas_call x1, Pallas kernels, attention_forward(): pl.pallas_call(functools.partial(forward_kernel, term_scale), grid=(width...  18.3 us
    ppermute x8, starting transfers between devices, halving_scatter(): held = keep + lax.ppermute(send, axis, xor_pairs(count, bit))  16.1 us
    ppermute x8, starting transfers between devices, doubling_gather(): other = lax.ppermute(held, axis, xor_pairs(count, bit))  14 us
    ppermute x2, starting transfers between devices, from_behind(): lax.ppermute(value, axis, [(source, source + steps) for source in range(l...  6.82 us
  transfers between devices with their start and end apart: 21, of which 17 were waited for; matrix products, arithmetic and copies ran while one was open for 10% of the time, Pallas kernels for 10%

profile of v5, /device:TPU:8, one launch (start us, length us, event | category | flops | bytes accessed | tf_op | source)
XLA Modules:
  0.0 206.3 jit_solution(7389523238535264988)
XLA Ops:
  8.2 1.2 fusion.8
  9.4 1.2 fusion.10
  10.8 2.4 %collective-permute-start.2 = (bf16[2,2176]{1,0:T(2,128)(2,1)S(1)}, bf16[2,2176]{1,0:T(2,128)(2,1)S(1)}, u32[]{:S(2)}, u32[]{:S(2)}) collective-permute-start(bf16[2,2176]{1,0:T(2,128)(2,1)S(1)} %pad_maximum_fusion.12), channel_id=1, source_target_pairs={{0,16},{1,17},{2,18},{3,19},{4,20},{5,21},{6,22},{7,23},{8,24},{9,... | collective-permute-start | bytes 26120 | tf_op jit(solution)/shard_map/ppermute | solution.py:48
  13.2 1.1 constant_dynamic-update-slice_fusion.1
  14.3 1.0 fusion.16
  15.4 1.9 collective-permute-start
  17.3 5.8 %collective-permute-start.1 = (bf16[2,128,1024]{2,1,0:T(8,128)(2,1)}, bf16[2,128,1024]{2,1,0:T(8,128)(2,1)}, u32[]{:S(2)}, u32[]{:S(2)}) collective-permute-start(bf16[2,128,1024]{2,1,0:T(8,128)(2,1)} %get-tuple-element.37), channel_id=1, source_target_pairs={{1,0},{2,1},{3,2},{4,3},{5,4},{6,5},{7,6},{8,7},{9,8},{10,9},{11,1... | collective-permute-start | bytes 1572872 | tf_op jit(solution)/shard_map/ppermute | solution.py:24
  24.7 2.0 copy.31
  26.9 3.7 %collective-permute-done.3 = bf16[2,2,2176]{2,1,0:T(2,128)(2,1)S(1)} collective-permute-done((bf16[2,2,2176]{2,1,0:T(2,128)(2,1)S(1)}, bf16[2,2,2176]{2,1,0:T(2,128)(2,1)S(1)}, u32[]{:S(2)}, u32[]{:S(2)}) %collective-permute-start.3) | collective-permute-done | bytes 17440 | tf_op jit(solution)/shard_map/ppermute | solution.py:48
  31.7 4.5 %collective-permute-done.4 = bf16[2,2,2,2176]{3,2,1,0:T(2,128)(2,1)S(1)} collective-permute-done((bf16[2,2,2,2176]{3,2,1,0:T(2,128)(2,1)S(1)}, bf16[2,2,2,2176]{3,2,1,0:T(2,128)(2,1)S(1)}, u32[]{:S(2)}, u32[]{:S(2)}) %collective-permute-start.4) | collective-permute-done | bytes 34848 | tf_op jit(solution)/shard_map/ppermute | solution.py:48
  36.5 4.2 %collective-permute-done.5 = bf16[2,2,2,2,2176]{4,3,2,1,0:T(2,128)(2,1)S(1)} collective-permute-done((bf16[2,2,2,2,2176]{4,3,2,1,0:T(2,128)(2,1)S(1)}, bf16[2,2,2,2,2176]{4,3,2,1,0:T(2,128)(2,1)S(1)}, u32[]{:S(2)}, u32[]{:S(2)}) %collective-permute-start.5) | collective-permute-done | bytes 69664 | tf_op jit(solution)/shard_map/ppermute | solution.py:48
  41.2 1.2 collective-permute-done.6
  42.7 1.8 gather_fusion
  44.5 1.1 gather.13
  47.1 1.4 pad_maximum_fusion
  48.5 1.5 slice_bitcast_fusion
  50.0 18.3 %shard_map.93 = (bf16[256,1024]{1,0:T(8,128)(2,1)}, f32[1024,1024]{1,0:T(8,128)}) custom-call(bf16[256,1024]{1,0:T(8,128)(2,1)} %bitcast.143, bf16[512,1024]{1,0:T(8,128)(2,1)} %get-tuple-element.35.k_ref, bf16[512,1024]{1,0:T(8,128)(2,1)} %get-tuple-element.34.v_ref, bf16[64,1024]{1,0:T(8,128)(2,1)} %get-tuple-element.39.ck_ref, ...), custom_call_target="tpu_custom_call" | custom-call | tf_op jit(solution)/shard_map/pallas_call | solution.py:122
  69.3 1.5 convolution_convert_fusion.g_ref
  70.8 20.4 %shard_map.94 = (bf16[256,1024]{1,0:T(8,128)(2,1)}, f32[512,1024]{1,0:T(8,128)}, f32[512,1024]{1,0:T(8,128)}, f32[64,1024]{1,0:T(8,128)}, f32[64,1024]{1,0:T(8,128)}) custom-call(bf16[256,1024]{1,0:T(8,128)(2,1)} %bitcast.144, bf16[512,1024]{1,0:T(8,128)(2,1)} %get-tuple-element.35.k_ref, bf16[512,1024]{1,0:T(8,128)(2,1)} %get-tuple-element.34.v_ref, ...), custom_call_target="tpu_custom_call" | custom-call | tf_op jit(solution)/shard_map/pallas_call | solution.py:228
  91.2 1.1 pad_maximum_fusion.3
  92.9 1.4 collective-permute-done.9
  94.5 1.7 slice_bitcast_fusion.2
  96.2 3.8 %collective-permute-done.10 = f32[2,2,2,2,2048]{4,3,2,1,0:T(2,128)S(1)} collective-permute-done((f32[2,2,2,2,2048]{4,3,2,1,0:T(2,128)S(1)}, f32[2,2,2,2,2048]{4,3,2,1,0:T(2,128)S(1)}, u32[]{:S(2)}, u32[]{:S(2)}) %collective-permute-start.10) | collective-permute-done | bytes 131104 | tf_op jit(solution)/shard_map/ppermute | solution.py:63
  100.2 2.7 %collective-permute-start.11 = (f32[2,2,2,2048]{3,2,1,0:T(2,128)S(1)}, f32[2,2,2,2048]{3,2,1,0:T(2,128)S(1)}, u32[]{:S(2)}, u32[]{:S(2)}) collective-permute-start(f32[2,2,2,2048]{3,2,1,0:T(2,128)S(1)} %dynamic-slice_bitcast_fusion.3), channel_id=1, source_target_pairs={{0,4},{1,5},{2,6},{3,7},{4,0},{5,1},{6,2},{7,3},{8,12},{9,13},{10,... | collective-permute-start | bytes 196616 | tf_op jit(solution)/shard_map/ppermute | solution.py:63
  103.0 1.9 collective-permute-start.7
  104.9 1.3 collective-permute-done.11
  106.3 1.3 collective-permute-start.12
  107.6 1.1 pad_maximum_fusion.2
  108.6 4.9 %collective-permute-start.8 = (f32[2,128,1024]{2,1,0:T(8,128)}, f32[2,128,1024]{2,1,0:T(8,128)}, u32[]{:S(2)}, u32[]{:S(2)}) collective-permute-start(f32[2,128,1024]{2,1,0:T(8,128)} %pad_maximum_fusion.2), channel_id=1, source_target_pairs={{1,0},{2,1},{3,2},{4,3},{5,4},{6,5},{7,6},{8,7},{9,8},{10,9},{11,1... | collective-permute-start | bytes 3145736 | tf_op jit(solution)/shard_map/ppermute | solution.py:32
  113.6 8.1 %collective-permute-done.12 = f32[2,2,2048]{2,1,0:T(2,128)S(1)} collective-permute-done((f32[2,2,2048]{2,1,0:T(2,128)S(1)}, f32[2,2,2048]{2,1,0:T(2,128)S(1)}, u32[]{:S(2)}, u32[]{:S(2)}) %collective-permute-start.12) | collective-permute-done | bytes 32800 | tf_op jit(solution)/shard_map/ppermute | solution.py:63
  121.7 1.3 collective-permute-start.13
  123.0 4.2 %collective-permute-done.13 = f32[2,2048]{1,0:T(2,128)S(1)} collective-permute-done((f32[2,2048]{1,0:T(2,128)S(1)}, f32[2,2048]{1,0:T(2,128)S(1)}, u32[]{:S(2)}, u32[]{:S(2)}) %collective-permute-start.13) | collective-permute-done | bytes 16416 | tf_op jit(solution)/shard_map/ppermute | solution.py:63
  127.3 2.1 %collective-permute-done.8 = f32[2,128,1024]{2,1,0:T(8,128)} collective-permute-done((f32[2,128,1024]{2,1,0:T(8,128)}, f32[2,128,1024]{2,1,0:T(8,128)}, u32[]{:S(2)}, u32[]{:S(2)}) %collective-permute-start.8) | collective-permute-done | bytes 1048608 | tf_op jit(solution)/shard_map/ppermute | solution.py:32
  129.4 1.9 pad_add_fusion
  132.4 1.3 fusion.2
  133.6 29.3 %reduce-scatter.2.cloned.1.call-done = f32[32,1024]{1,0:T(8,128)} async-done(((f32[1024,1024]{1,0:T(8,128)}), f32[32,1024]{1,0:T(8,128)}) %reduce-scatter.2.cloned.1.call-update) | async-done | bytes 131088 | tf_op jit(solution)/shard_map/reduce_scatter | solution.py:336
  163.9 1.6 collective-permute-start.14
  165.5 2.7 %collective-permute-done.14 = f32[2,2,4,1024]{3,2,1,0:T(4,128)S(1)} collective-permute-done((f32[2,2,4,1024]{3,2,1,0:T(4,128)S(1)}, f32[2,2,4,1024]{3,2,1,0:T(4,128)S(1)}, u32[]{:S(2)}, u32[]{:S(2)}) %collective-permute-start.14) | collective-permute-done | bytes 65568 | tf_op jit(solution)/shard_map/ppermute | solution.py:63
  168.3 2.9 %collective-permute-start.15 = (f32[2,4,1024]{2,1,0:T(4,128)S(1)}, f32[2,4,1024]{2,1,0:T(4,128)S(1)}, u32[]{:S(2)}, u32[]{:S(2)}) collective-permute-start(f32[2,4,1024]{2,1,0:T(4,128)S(1)} %dynamic-slice_bitcast_fusion.4), channel_id=1, source_target_pairs={{0,64},{32,96},{64,0},{96,32},{128,192},{160,224},{192,128},{224,1... | collective-permute-start | bytes 98312 | tf_op jit(solution)/shard_map/ppermute | solution.py:63
  171.2 2.0 collective-permute-done.15
  173.2 5.8 %collective-permute-start.16 = (f32[4,1024]{1,0:T(4,128)S(1)}, f32[4,1024]{1,0:T(4,128)S(1)}, u32[]{:S(2)}, u32[]{:S(2)}) collective-permute-start(f32[4,1024]{1,0:T(4,128)S(1)} %dynamic-slice_bitcast_fusion.6), channel_id=1, source_target_pairs={{0,128},{32,160},{64,192},{96,224},{128,0},{160,32},{192,64},{224,... | collective-permute-start | bytes 49160 | tf_op jit(solution)/shard_map/ppermute | solution.py:63
  179.0 1.9 collective-permute-done.16
  181.0 5.7 %collective-permute-start.17 = (f32[4,1024]{1,0:T(4,128)S(1)}, f32[4,1024]{1,0:T(4,128)S(1)}, u32[]{:S(2)}, u32[]{:S(2)}) collective-permute-start(f32[4,1024]{1,0:T(4,128)S(1)} %bitcast_add_fusion.8), channel_id=1, source_target_pairs={{0,128},{32,160},{64,192},{96,224},{128,0},{160,32},{192,64},{224,... | collective-permute-start | bytes 49160 | tf_op jit(solution)/shard_map/ppermute | solution.py:48
  186.7 2.0 collective-permute-done.17
  188.7 3.0 %collective-permute-start.18 = (f32[2,4,1024]{2,1,0:T(4,128)S(1)}, f32[2,4,1024]{2,1,0:T(4,128)S(1)}, u32[]{:S(2)}, u32[]{:S(2)}) collective-permute-start(f32[2,4,1024]{2,1,0:T(4,128)S(1)} %get-tuple-element.43), channel_id=1, source_target_pairs={{0,64},{32,96},{64,0},{96,32},{128,192},{160,224},{192,128},{224,1... | collective-permute-start | bytes 98312 | tf_op jit(solution)/shard_map/ppermute | solution.py:48
  191.9 1.7 collective-permute-done.18
  193.7 1.6 collective-permute-start.19
  195.3 2.7 %collective-permute-done.19 = f32[2,2,4,1024]{3,2,1,0:T(4,128)S(1)} collective-permute-done((f32[2,2,4,1024]{3,2,1,0:T(4,128)S(1)}, f32[2,2,4,1024]{3,2,1,0:T(4,128)S(1)}, u32[]{:S(2)}, u32[]{:S(2)}) %collective-permute-start.19) | collective-permute-done | bytes 65568 | tf_op jit(solution)/shard_map/ppermute | solution.py:48
  (83 shorter events, 12.7 us)
Async XLA Ops:
  7.2 61.2 %copy-start = (bf16[1024,1024]{1,0:T(8,128)(2,1)S(1)}, bf16[1024,1024]{1,0:T(8,128)(2,1)}, u32[]{:S(2)}) copy-start(bf16[1024,1024]{1,0:T(8,128)(2,1)} %param.9) | copy-start | bytes 6291460
  7.2 155.7 %reduce-scatter.2.cloned.1.call-start = ((), (), s32[]{:S(2)}) async-start(), calls=%async_computation.1 | async-start | bytes 4325376 | tf_op jit(solution)/shard_map/reduce_scatter | solution.py:336
  7.2 7.0 %copy-start.1 = (bf16[1,256,1024]{2,1,0:T(8,128)(2,1)S(1)}, bf16[1,256,1024]{2,1,0:T(8,128)(2,1)}, u32[]{:S(2)}) copy-start(bf16[1,256,1024]{2,1,0:T(8,128)(2,1)} %param.8) | copy-start | bytes 1572868
  10.8 15.9 %collective-permute-start.2 = (bf16[2,2176]{1,0:T(2,128)(2,1)S(1)}, bf16[2,2176]{1,0:T(2,128)(2,1)S(1)}, u32[]{:S(2)}, u32[]{:S(2)}) collective-permute-start(bf16[2,2176]{1,0:T(2,128)(2,1)S(1)} %pad_maximum_fusion.12), channel_id=1, source_target_pairs={{0,16},{1,17},{2,18},{3,19},{4,20},{5,21},{6,22},{7,23},{8,24},{9,... | collective-permute-start | bytes 26120 | tf_op jit(solution)/shard_map/ppermute | solution.py:48
  15.4 31.7 %collective-permute-start = (bf16[2,128,1024]{2,1,0:T(8,128)(2,1)}, bf16[2,128,1024]{2,1,0:T(8,128)(2,1)}, u32[]{:S(2)}, u32[]{:S(2)}) collective-permute-start(bf16[2,128,1024]{2,1,0:T(8,128)(2,1)} %get-tuple-element.36), channel_id=1, source_target_pairs={{0,1},{1,2},{2,3},{3,4},{4,5},{5,6},{6,7},{7,8},{8,9},{9,10},{10,1... | collective-permute-start | bytes 1572872 | tf_op jit(solution)/shard_map/ppermute | solution.py:21
  17.3 29.8 %collective-permute-start.1 = (bf16[2,128,1024]{2,1,0:T(8,128)(2,1)}, bf16[2,128,1024]{2,1,0:T(8,128)(2,1)}, u32[]{:S(2)}, u32[]{:S(2)}) collective-permute-start(bf16[2,128,1024]{2,1,0:T(8,128)(2,1)} %get-tuple-element.37), channel_id=1, source_target_pairs={{1,0},{2,1},{3,2},{4,3},{5,4},{6,5},{7,6},{8,7},{9,8},{10,9},{11,1... | collective-permute-start | bytes 1572872 | tf_op jit(solution)/shard_map/ppermute | solution.py:24
  26.8 3.8 %collective-permute-start.3 = (bf16[2,2,2176]{2,1,0:T(2,128)(2,1)S(1)}, bf16[2,2,2176]{2,1,0:T(2,128)(2,1)S(1)}, u32[]{:S(2)}, u32[]{:S(2)}) collective-permute-start(bf16[2,2,2176]{2,1,0:T(2,128)(2,1)S(1)} %pad_maximum_fusion.11), channel_id=1, source_target_pairs={{0,8},{1,9},{2,10},{3,11},{4,12},{5,13},{6,14},{7,15},{8,0},{9,1},... | collective-permute-start | bytes 52232 | tf_op jit(solution)/shard_map/ppermute | solution.py:48
  30.7 5.5 %collective-permute-start.4 = (bf16[2,2,2,2176]{3,2,1,0:T(2,128)(2,1)S(1)}, bf16[2,2,2,2176]{3,2,1,0:T(2,128)(2,1)S(1)}, u32[]{:S(2)}, u32[]{:S(2)}) collective-permute-start(bf16[2,2,2,2176]{3,2,1,0:T(2,128)(2,1)S(1)} %pad_maximum_fusion.9), channel_id=1, source_target_pairs={{0,4},{1,5},{2,6},{3,7},{4,0},{5,1},{6,2},{7,3},{8,12},{9,13},{10,... | collective-permute-start | bytes 104456 | tf_op jit(solution)/shard_map/ppermute | solution.py:48
  36.3 4.4 %collective-permute-start.5 = (bf16[2,2,2,2,2176]{4,3,2,1,0:T(2,128)(2,1)S(1)}, bf16[2,2,2,2,2176]{4,3,2,1,0:T(2,128)(2,1)S(1)}, u32[]{:S(2)}, u32[]{:S(2)}) collective-permute-start(bf16[2,2,2,2,2176]{4,3,2,1,0:T(2,128)(2,1)S(1)} %pad_maximum_fusion.7), channel_id=1, source_target_pairs={{0,2},{1,3},{2,0},{3,1},{4,6},{5,7},{6,4},{7,5},{8,10},{9,11},{10,... | collective-permute-start | bytes 208904 | tf_op jit(solution)/shard_map/ppermute | solution.py:48
  40.9 1.4 collective-permute-start.6
  68.3 1.0 copy-start.4
  92.6 1.6 collective-permute-start.9
  94.4 5.6 %collective-permute-start.10 = (f32[2,2,2,2,2048]{4,3,2,1,0:T(2,128)S(1)}, f32[2,2,2,2,2048]{4,3,2,1,0:T(2,128)S(1)}, u32[]{:S(2)}, u32[]{:S(2)}) collective-permute-start(f32[2,2,2,2,2048]{4,3,2,1,0:T(2,128)S(1)} %dynamic-slice_bitcast_fusion.1), channel_id=1, source_target_pairs={{0,2},{1,3},{2,0},{3,1},{4,6},{5,7},{6,4},{7,5},{8,10},{9,11},{10,... | collective-permute-start | bytes 393224 | tf_op jit(solution)/shard_map/ppermute | solution.py:63
  100.2 6.0 %collective-permute-start.11 = (f32[2,2,2,2048]{3,2,1,0:T(2,128)S(1)}, f32[2,2,2,2048]{3,2,1,0:T(2,128)S(1)}, u32[]{:S(2)}, u32[]{:S(2)}) collective-permute-start(f32[2,2,2,2048]{3,2,1,0:T(2,128)S(1)} %dynamic-slice_bitcast_fusion.3), channel_id=1, source_target_pairs={{0,4},{1,5},{2,6},{3,7},{4,0},{5,1},{6,2},{7,3},{8,12},{9,13},{10,... | collective-permute-start | bytes 196616 | tf_op jit(solution)/shard_map/ppermute | solution.py:63
  103.0 24.3 %collective-permute-start.7 = (f32[2,128,1024]{2,1,0:T(8,128)S(1)}, f32[2,128,1024]{2,1,0:T(8,128)}, u32[]{:S(2)}, u32[]{:S(2)}) collective-permute-start(f32[2,128,1024]{2,1,0:T(8,128)S(1)} %pad_maximum_fusion.1), channel_id=1, source_target_pairs={{0,1},{1,2},{2,3},{3,4},{4,5},{5,6},{6,7},{7,8},{8,9},{9,10},{10,1... | collective-permute-start | bytes 3145736 | tf_op jit(solution)/shard_map/ppermute | solution.py:32
  106.3 15.4 %collective-permute-start.12 = (f32[2,2,2048]{2,1,0:T(2,128)S(1)}, f32[2,2,2048]{2,1,0:T(2,128)S(1)}, u32[]{:S(2)}, u32[]{:S(2)}) collective-permute-start(f32[2,2,2048]{2,1,0:T(2,128)S(1)} %dynamic-slice_bitcast_fusion.5), channel_id=1, source_target_pairs={{0,8},{1,9},{2,10},{3,11},{4,12},{5,13},{6,14},{7,15},{8,0},{9,1},... | collective-permute-start | bytes 98312 | tf_op jit(solution)/shard_map/ppermute | solution.py:63
  108.6 20.7 %collective-permute-start.8 = (f32[2,128,1024]{2,1,0:T(8,128)}, f32[2,128,1024]{2,1,0:T(8,128)}, u32[]{:S(2)}, u32[]{:S(2)}) collective-permute-start(f32[2,128,1024]{2,1,0:T(8,128)} %pad_maximum_fusion.2), channel_id=1, source_target_pairs={{1,0},{2,1},{3,2},{4,3},{5,4},{6,5},{7,6},{8,7},{9,8},{10,9},{11,1... | collective-permute-start | bytes 3145736 | tf_op jit(solution)/shard_map/ppermute | solution.py:32
  121.7 5.5 %collective-permute-start.13 = (f32[2,2048]{1,0:T(2,128)S(1)}, f32[2,2048]{1,0:T(2,128)S(1)}, u32[]{:S(2)}, u32[]{:S(2)}) collective-permute-start(f32[2,2048]{1,0:T(2,128)S(1)} %dynamic-slice_bitcast_fusion.7), channel_id=1, source_target_pairs={{0,16},{1,17},{2,18},{3,19},{4,20},{5,21},{6,22},{7,23},{8,24},{9,... | collective-permute-start | bytes 49160 | tf_op jit(solution)/shard_map/ppermute | solution.py:63
  129.4 2.3 %copy-start.2 = (f32[512,1024]{1,0:T(8,128)S(1)}, f32[512,1024]{1,0:T(8,128)}, u32[]{:S(2)}) copy-start(f32[512,1024]{1,0:T(8,128)} %get-tuple-element.20) | copy-start | bytes 6291460
  129.4 3.0 %copy-start.3 = (f32[512,1024]{1,0:T(8,128)S(1)}, f32[512,1024]{1,0:T(8,128)}, u32[]{:S(2)}) copy-start(f32[512,1024]{1,0:T(8,128)} %get-tuple-element.21) | copy-start | bytes 6291460
  163.9 4.4 %collective-permute-start.14 = (f32[2,2,4,1024]{3,2,1,0:T(4,128)S(1)}, f32[2,2,4,1024]{3,2,1,0:T(4,128)S(1)}, u32[]{:S(2)}, u32[]{:S(2)}) collective-permute-start(f32[2,2,4,1024]{3,2,1,0:T(4,128)S(1)} %dynamic-slice_bitcast_fusion.2), channel_id=1, source_target_pairs={{0,32},{32,0},{64,96},{96,64},{128,160},{160,128},{192,224},{224,1... | collective-permute-start | bytes 196616 | tf_op jit(solution)/shard_map/ppermute | solution.py:63
  168.3 4.9 %collective-permute-start.15 = (f32[2,4,1024]{2,1,0:T(4,128)S(1)}, f32[2,4,1024]{2,1,0:T(4,128)S(1)}, u32[]{:S(2)}, u32[]{:S(2)}) collective-permute-start(f32[2,4,1024]{2,1,0:T(4,128)S(1)} %dynamic-slice_bitcast_fusion.4), channel_id=1, source_target_pairs={{0,64},{32,96},{64,0},{96,32},{128,192},{160,224},{192,128},{224,1... | collective-permute-start | bytes 98312 | tf_op jit(solution)/shard_map/ppermute | solution.py:63
  173.2 7.7 %collective-permute-start.16 = (f32[4,1024]{1,0:T(4,128)S(1)}, f32[4,1024]{1,0:T(4,128)S(1)}, u32[]{:S(2)}, u32[]{:S(2)}) collective-permute-start(f32[4,1024]{1,0:T(4,128)S(1)} %dynamic-slice_bitcast_fusion.6), channel_id=1, source_target_pairs={{0,128},{32,160},{64,192},{96,224},{128,0},{160,32},{192,64},{224,... | collective-permute-start | bytes 49160 | tf_op jit(solution)/shard_map/ppermute | solution.py:63
  181.0 7.7 %collective-permute-start.17 = (f32[4,1024]{1,0:T(4,128)S(1)}, f32[4,1024]{1,0:T(4,128)S(1)}, u32[]{:S(2)}, u32[]{:S(2)}) collective-permute-start(f32[4,1024]{1,0:T(4,128)S(1)} %bitcast_add_fusion.8), channel_id=1, source_target_pairs={{0,128},{32,160},{64,192},{96,224},{128,0},{160,32},{192,64},{224,... | collective-permute-start | bytes 49160 | tf_op jit(solution)/shard_map/ppermute | solution.py:48
  188.7 4.9 %collective-permute-start.18 = (f32[2,4,1024]{2,1,0:T(4,128)S(1)}, f32[2,4,1024]{2,1,0:T(4,128)S(1)}, u32[]{:S(2)}, u32[]{:S(2)}) collective-permute-start(f32[2,4,1024]{2,1,0:T(4,128)S(1)} %get-tuple-element.43), channel_id=1, source_target_pairs={{0,64},{32,96},{64,0},{96,32},{128,192},{160,224},{192,128},{224,1... | collective-permute-start | bytes 98312 | tf_op jit(solution)/shard_map/ppermute | solution.py:48
  193.7 4.4 %collective-permute-start.19 = (f32[2,2,4,1024]{3,2,1,0:T(4,128)S(1)}, f32[2,2,4,1024]{3,2,1,0:T(4,128)S(1)}, u32[]{:S(2)}, u32[]{:S(2)}) collective-permute-start(f32[2,2,4,1024]{3,2,1,0:T(4,128)S(1)} %get-tuple-element.41), channel_id=1, source_target_pairs={{0,32},{32,0},{64,96},{96,64},{128,160},{160,128},{192,224},{224,1... | collective-permute-start | bytes 196616 | tf_op jit(solution)/shard_map/ppermute | solution.py:48
Sparse Core Ops, SparseCore 0:
  68.4 94.4 reduce-scatter.1

commit v6 on v2

--- a/solution.py
+++ b/solution.py
@@ -77,7 +77,7 @@
                    grad_t_ref, att_ref, term_ref):
     score_scale = 1.0 / math.sqrt(HEAD_DIM)
     lanes = q_ref.shape[1]
-    low_lanes = lax.broadcasted_iota(jnp.int32, (BLOCK, lanes), 1) < HEAD_DIM
+    lane_head = lax.broadcasted_iota(jnp.int32, (BLOCK, lanes), 1) // HEAD_DIM
     coarse_k = ck_ref[...]
     coarse_v = cv_ref[...]
     counts = counts_ref[...]
@@ -88,9 +88,9 @@
         value_win = v_ref[pl.ds(block * BLOCK, 3 * BLOCK), :]
         fine_ok = fine_ref[pl.ds(block, 1), :] > 0
         far_ok = far_ref[pl.ds(block, 1), :] > 0
-        halves = []
-        for half in range(2):
-            own = low_lanes if half == 0 else jnp.logical_not(low_lanes)
+        att_all = None
+        for half in range(lanes // HEAD_DIM):
+            own = lane_head == half
             query_h = jnp.where(own, query, jnp.zeros_like(query))
             fine_s = lax.dot_general(query_h, key_win, contract_last,
                                      preferred_element_type=jnp.float32) * score_scale
@@ -108,9 +108,9 @@
             coarse_w = (coarse_e / total).astype(jnp.bfloat16)
             att = (jnp.dot(fine_w, value_win, preferred_element_type=jnp.float32)
                    + jnp.dot(coarse_w, coarse_v, preferred_element_type=jnp.float32))
-            halves.append((att, top, total))
+            att_all = att if att_all is None else jnp.where(own, att, att_all)
         rows = pl.ds(block * BLOCK, BLOCK)
-        att_ref[rows, :] = jnp.where(low_lanes, halves[0][0], halves[1][0]).astype(att_ref.dtype)
+        att_ref[rows, :] = att_all.astype(att_ref.dtype)
     term_ref[...] = jnp.dot(grad_t_ref[...], att_ref[...],
                             preferred_element_type=jnp.float32) * term_scale
 
@@ -118,7 +118,7 @@
 def attention_forward(query_rows, padded_k, padded_v, coarse_k, coarse_v, counts, fine_ok, far_ok,
                       grad_t, term_scale):
     tokens, width = query_rows.shape
-    lanes = 2 * HEAD_DIM
+    lanes = 4 * HEAD_DIM
     by_pair = lambda rows: pl.BlockSpec((rows, lanes), lambda pair: (0, pair))
     whole = lambda shape: pl.BlockSpec(shape, lambda pair: (0, 0))
     return pl.pallas_call(

time: 201 us -> 200 us (level)
  no operation moved by 1% of the time
where the time goes in v6:
time: 200 us; the launch traced here: 199 us
  waiting for transfers between devices  78.9 us (39%)
  Pallas kernels  37.9 us (19%)
  starting transfers between devices  37.7 us (19%)
  between operations  14.5 us (7%)
  local copies, waits for them, and re-layouts  13.6 us (7%)
  other arithmetic  12.2 us (6%)
  matrix products  3.95 us (2%)
    reduce_scatter x1, waiting for transfers between devices, per_device(): lax.psum_scatter(full_term, 'seq', scatter_dimension=0, tiled=True)  29.9 us
    ppermute x8, waiting for transfers between devices, halving_scatter(): held = keep + lax.ppermute(send, axis, xor_pairs(count, bit))  29.3 us
    pallas_call x1, Pallas kernels, attention_backward(): pl.pallas_call(backward_kernel, grid=(width // lanes,), in_specs=[by_pair...  20.4 us
    ppermute x8, waiting for transfers between devices, doubling_gather(): other = lax.ppermute(held, axis, xor_pairs(count, bit))  19.5 us
    pallas_call x1, Pallas kernels, attention_forward(): pl.pallas_call(functools.partial(forward_kernel, term_scale), grid=(width...  17.5 us
    ppermute x8, starting transfers between devices, doubling_gather(): other = lax.ppermute(held, axis, xor_pairs(count, bit))  13.2 us
    ppermute x8, starting transfers between devices, halving_scatter(): held = keep + lax.ppermute(send, axis, xor_pairs(count, bit))  12.8 us
    ppermute x1, starting transfers between devices, padded_2(): lax.ppermute(lax.slice_in_dim(block, 0, width, axis=dim), axis, backward)  5.75 us
  transfers between devices with their start and end apart: 21, of which 17 were waited for; matrix products, arithmetic and copies ran while one was open for 10% of the time, Pallas kernels for 10%

profile of v6, /device:TPU:8, one launch (start us, length us, event | category | flops | bytes accessed | tf_op | source)
XLA Modules:
  0.0 198.9 jit_solution(8840356924278258094)
XLA Ops:
  7.2 0.8 convert_element_type.71
  8.2 1.2 fusion.18
  9.4 1.2 fusion.20
  10.8 2.4 %collective-permute-start.2 = (bf16[2,2176]{1,0:T(2,128)(2,1)S(1)}, bf16[2,2176]{1,0:T(2,128)(2,1)S(1)}, u32[]{:S(2)}, u32[]{:S(2)}) collective-permute-start(bf16[2,2176]{1,0:T(2,128)(2,1)S(1)} %pad_maximum_fusion.12), channel_id=1, source_target_pairs={{0,16},{1,17},{2,18},{3,19},{4,20},{5,21},{6,22},{7,23},{8,24},{9,... | collective-permute-start | bytes 26120 | tf_op jit(solution)/shard_map/ppermute | solution.py:48
  13.2 1.1 constant_dynamic-update-slice_fusion.1
  14.3 1.0 fusion.22
  15.4 1.9 collective-permute-start
  17.3 5.8 %collective-permute-start.1 = (bf16[2,128,1024]{2,1,0:T(8,128)(2,1)}, bf16[2,128,1024]{2,1,0:T(8,128)(2,1)}, u32[]{:S(2)}, u32[]{:S(2)}) collective-permute-start(bf16[2,128,1024]{2,1,0:T(8,128)(2,1)} %get-tuple-element.37), channel_id=1, source_target_pairs={{1,0},{2,1},{3,2},{4,3},{5,4},{6,5},{7,6},{8,7},{9,8},{10,9},{11,1... | collective-permute-start | bytes 1572872 | tf_op jit(solution)/shard_map/ppermute | solution.py:24
  23.3 5.2 %collective-permute-done.3 = bf16[2,2,2176]{2,1,0:T(2,128)(2,1)S(1)} collective-permute-done((bf16[2,2,2176]{2,1,0:T(2,128)(2,1)S(1)}, bf16[2,2,2176]{2,1,0:T(2,128)(2,1)S(1)}, u32[]{:S(2)}, u32[]{:S(2)}) %collective-permute-start.3) | collective-permute-done | bytes 17440 | tf_op jit(solution)/shard_map/ppermute | solution.py:48
  28.8 5.4 %collective-permute-done.4 = bf16[2,2,2,2176]{3,2,1,0:T(2,128)(2,1)S(1)} collective-permute-done((bf16[2,2,2,2176]{3,2,1,0:T(2,128)(2,1)S(1)}, bf16[2,2,2,2176]{3,2,1,0:T(2,128)(2,1)S(1)}, u32[]{:S(2)}, u32[]{:S(2)}) %collective-permute-start.4) | collective-permute-done | bytes 34848 | tf_op jit(solution)/shard_map/ppermute | solution.py:48
  35.1 2.0 %copy.21 = bf16[1,256,1024]{1,2,0:T(8,128)(2,1)} copy(bf16[1,256,1024]{2,1,0:T(8,128)(2,1)} %param.10) | data formatting | bytes 1048576 | tf_op args[4]
  37.2 1.6 collective-permute-done.5
  39.8 0.7 collective-permute-done.6
  40.9 1.1 pad_maximum_fusion.4
  42.0 1.1 reshape_reshape.12
  44.4 1.4 pad_maximum_fusion
  45.8 1.5 slice_bitcast_fusion
  47.3 17.5 %shard_map.93 = (bf16[256,1024]{1,0:T(8,128)(2,1)}, f32[1024,1024]{1,0:T(8,128)}) custom-call(bf16[256,1024]{1,0:T(8,128)(2,1)} %bitcast.143, bf16[512,1024]{1,0:T(8,128)(2,1)} %get-tuple-element.35.k_ref, bf16[512,1024]{1,0:T(8,128)(2,1)} %get-tuple-element.34.v_ref, bf16[64,1024]{1,0:T(8,128)(2,1)} %get-tuple-element.41.ck_ref, ...), custom_call_target="tpu_custom_call" | custom-call | tf_op jit(solution)/shard_map/pallas_call | solution.py:124
  64.9 1.0 copy-done.4
  65.9 1.5 convolution_convert_fusion.g_ref
  67.4 20.4 %shard_map.94 = (bf16[256,1024]{1,0:T(8,128)(2,1)}, f32[512,1024]{1,0:T(8,128)}, f32[512,1024]{1,0:T(8,128)}, f32[64,1024]{1,0:T(8,128)}, f32[64,1024]{1,0:T(8,128)}) custom-call(bf16[256,1024]{1,0:T(8,128)(2,1)} %bitcast.144, bf16[512,1024]{1,0:T(8,128)(2,1)} %get-tuple-element.35.k_ref, bf16[512,1024]{1,0:T(8,128)(2,1)} %get-tuple-element.34.v_ref, ...), custom_call_target="tpu_custom_call" | custom-call | tf_op jit(solution)/shard_map/pallas_call | solution.py:230
  87.8 1.1 pad_maximum_fusion.3
  89.5 1.4 collective-permute-done.9
  91.8 1.7 slice_bitcast_fusion.2
  93.5 3.4 %collective-permute-done.10 = f32[2,2,2,2,2048]{4,3,2,1,0:T(2,128)S(1)} collective-permute-done((f32[2,2,2,2,2048]{4,3,2,1,0:T(2,128)S(1)}, f32[2,2,2,2,2048]{4,3,2,1,0:T(2,128)S(1)}, u32[]{:S(2)}, u32[]{:S(2)}) %collective-permute-start.10) | collective-permute-done | bytes 131104 | tf_op jit(solution)/shard_map/ppermute | solution.py:65
  97.2 1.9 collective-permute-start.7
  99.1 3.7 %collective-permute-done.11 = f32[2,2,2,2048]{3,2,1,0:T(2,128)S(1)} collective-permute-done((f32[2,2,2,2048]{3,2,1,0:T(2,128)S(1)}, f32[2,2,2,2048]{3,2,1,0:T(2,128)S(1)}, u32[]{:S(2)}, u32[]{:S(2)}) %collective-permute-start.11) | collective-permute-done | bytes 65568 | tf_op jit(solution)/shard_map/ppermute | solution.py:65
  103.0 1.1 pad_maximum_fusion.2
  104.1 2.0 %collective-permute-start.8 = (f32[2,128,1024]{2,1,0:T(8,128)}, f32[2,128,1024]{2,1,0:T(8,128)}, u32[]{:S(2)}, u32[]{:S(2)}) collective-permute-start(f32[2,128,1024]{2,1,0:T(8,128)} %pad_maximum_fusion.2), channel_id=1, source_target_pairs={{1,0},{2,1},{3,2},{4,3},{5,4},{6,5},{7,6},{8,7},{9,8},{10,9},{11,1... | collective-permute-start | bytes 3145736 | tf_op jit(solution)/shard_map/ppermute | solution.py:32
  106.1 9.8 %collective-permute-done.12 = f32[2,2,2048]{2,1,0:T(2,128)S(1)} collective-permute-done((f32[2,2,2048]{2,1,0:T(2,128)S(1)}, f32[2,2,2048]{2,1,0:T(2,128)S(1)}, u32[]{:S(2)}, u32[]{:S(2)}) %collective-permute-start.12) | collective-permute-done | bytes 32800 | tf_op jit(solution)/shard_map/ppermute | solution.py:65
  116.0 1.3 collective-permute-start.13
  117.3 4.3 %collective-permute-done.13 = f32[2,2048]{1,0:T(2,128)S(1)} collective-permute-done((f32[2,2048]{1,0:T(2,128)S(1)}, f32[2,2048]{1,0:T(2,128)S(1)}, u32[]{:S(2)}, u32[]{:S(2)}) %collective-permute-start.13) | collective-permute-done | bytes 16416 | tf_op jit(solution)/shard_map/ppermute | solution.py:65
  121.9 1.8 pad_add_fusion
  124.9 1.3 fusion.2
  126.2 29.9 %reduce-scatter.2.cloned.1.call-done = f32[32,1024]{1,0:T(8,128)} async-done(((f32[1024,1024]{1,0:T(8,128)}), f32[32,1024]{1,0:T(8,128)}) %reduce-scatter.2.cloned.1.call-update) | async-done | bytes 131088 | tf_op jit(solution)/shard_map/reduce_scatter | solution.py:338
  156.1 0.9 reshape_reshape.14
  157.0 1.6 collective-permute-start.14
  158.7 2.7 %collective-permute-done.14 = f32[2,2,4,1024]{3,2,1,0:T(4,128)S(1)} collective-permute-done((f32[2,2,4,1024]{3,2,1,0:T(4,128)S(1)}, f32[2,2,4,1024]{3,2,1,0:T(4,128)S(1)}, u32[]{:S(2)}, u32[]{:S(2)}) %collective-permute-start.14) | collective-permute-done | bytes 65568 | tf_op jit(solution)/shard_map/ppermute | solution.py:65
  161.4 2.9 %collective-permute-start.15 = (f32[2,4,1024]{2,1,0:T(4,128)S(1)}, f32[2,4,1024]{2,1,0:T(4,128)S(1)}, u32[]{:S(2)}, u32[]{:S(2)}) collective-permute-start(f32[2,4,1024]{2,1,0:T(4,128)S(1)} %dynamic-slice_bitcast_fusion.3), channel_id=1, source_target_pairs={{0,64},{32,96},{64,0},{96,32},{128,192},{160,224},{192,128},{224,1... | collective-permute-start | bytes 98312 | tf_op jit(solution)/shard_map/ppermute | solution.py:65
  164.4 2.0 collective-permute-done.15
  166.4 5.8 %collective-permute-start.16 = (f32[4,1024]{1,0:T(4,128)S(1)}, f32[4,1024]{1,0:T(4,128)S(1)}, u32[]{:S(2)}, u32[]{:S(2)}) collective-permute-start(f32[4,1024]{1,0:T(4,128)S(1)} %dynamic-slice_bitcast_fusion.5), channel_id=1, source_target_pairs={{0,128},{32,160},{64,192},{96,224},{128,0},{160,32},{192,64},{224,... | collective-permute-start | bytes 49160 | tf_op jit(solution)/shard_map/ppermute | solution.py:65
  172.2 1.9 collective-permute-done.16
  174.1 5.8 %collective-permute-start.17 = (f32[4,1024]{1,0:T(4,128)S(1)}, f32[4,1024]{1,0:T(4,128)S(1)}, u32[]{:S(2)}, u32[]{:S(2)}) collective-permute-start(f32[4,1024]{1,0:T(4,128)S(1)} %bitcast_add_fusion.8), channel_id=1, source_target_pairs={{0,128},{32,160},{64,192},{96,224},{128,0},{160,32},{192,64},{224,... | collective-permute-start | bytes 49160 | tf_op jit(solution)/shard_map/ppermute | solution.py:48
  179.9 2.0 %collective-permute-done.17 = f32[4,1024]{1,0:T(4,128)S(1)} collective-permute-done((f32[4,1024]{1,0:T(4,128)S(1)}, f32[4,1024]{1,0:T(4,128)S(1)}, u32[]{:S(2)}, u32[]{:S(2)}) %collective-permute-start.17) | collective-permute-done | bytes 16416 | tf_op jit(solution)/shard_map/ppermute | solution.py:48
  181.9 3.0 %collective-permute-start.18 = (f32[2,4,1024]{2,1,0:T(4,128)S(1)}, f32[2,4,1024]{2,1,0:T(4,128)S(1)}, u32[]{:S(2)}, u32[]{:S(2)}) collective-permute-start(f32[2,4,1024]{2,1,0:T(4,128)S(1)} %pad_maximum_fusion.10), channel_id=1, source_target_pairs={{0,64},{32,96},{64,0},{96,32},{128,192},{160,224},{192,128},{224,1... | collective-permute-start | bytes 98312 | tf_op jit(solution)/shard_map/ppermute | solution.py:48
  184.9 1.9 collective-permute-done.18
  186.9 1.7 collective-permute-start.19
  188.5 2.7 %collective-permute-done.19 = f32[2,2,4,1024]{3,2,1,0:T(4,128)S(1)} collective-permute-done((f32[2,2,4,1024]{3,2,1,0:T(4,128)S(1)}, f32[2,2,4,1024]{3,2,1,0:T(4,128)S(1)}, u32[]{:S(2)}, u32[]{:S(2)}) %collective-permute-start.19) | collective-permute-done | bytes 65568 | tf_op jit(solution)/shard_map/ppermute | solution.py:48
  (73 shorter events, 8.7 us)
Async XLA Ops:
  7.2 57.7 %copy-start = (bf16[1024,1024]{1,0:T(8,128)(2,1)S(1)}, bf16[1024,1024]{1,0:T(8,128)(2,1)}, u32[]{:S(2)}) copy-start(bf16[1024,1024]{1,0:T(8,128)(2,1)} %param.9) | copy-start | bytes 6291460
  7.2 148.9 %reduce-scatter.2.cloned.1.call-start = ((), (), s32[]{:S(2)}) async-start(), calls=%async_computation.1 | async-start | bytes 4325376 | tf_op jit(solution)/shard_map/reduce_scatter | solution.py:338
  7.2 7.0 %copy-start.1 = (bf16[1,256,1024]{2,1,0:T(8,128)(2,1)S(1)}, bf16[1,256,1024]{2,1,0:T(8,128)(2,1)}, u32[]{:S(2)}) copy-start(bf16[1,256,1024]{2,1,0:T(8,128)(2,1)} %param.8) | copy-start | bytes 1572868
  10.8 12.3 %collective-permute-start.2 = (bf16[2,2176]{1,0:T(2,128)(2,1)S(1)}, bf16[2,2176]{1,0:T(2,128)(2,1)S(1)}, u32[]{:S(2)}, u32[]{:S(2)}) collective-permute-start(bf16[2,2176]{1,0:T(2,128)(2,1)S(1)} %pad_maximum_fusion.12), channel_id=1, source_target_pairs={{0,16},{1,17},{2,18},{3,19},{4,20},{5,21},{6,22},{7,23},{8,24},{9,... | collective-permute-start | bytes 26120 | tf_op jit(solution)/shard_map/ppermute | solution.py:48
  15.4 29.0 %collective-permute-start = (bf16[2,128,1024]{2,1,0:T(8,128)(2,1)}, bf16[2,128,1024]{2,1,0:T(8,128)(2,1)}, u32[]{:S(2)}, u32[]{:S(2)}) collective-permute-start(bf16[2,128,1024]{2,1,0:T(8,128)(2,1)} %get-tuple-element.36), channel_id=1, source_target_pairs={{0,1},{1,2},{2,3},{3,4},{4,5},{5,6},{6,7},{7,8},{8,9},{9,10},{10,1... | collective-permute-start | bytes 1572872 | tf_op jit(solution)/shard_map/ppermute | solution.py:21
  17.3 27.1 %collective-permute-start.1 = (bf16[2,128,1024]{2,1,0:T(8,128)(2,1)}, bf16[2,128,1024]{2,1,0:T(8,128)(2,1)}, u32[]{:S(2)}, u32[]{:S(2)}) collective-permute-start(bf16[2,128,1024]{2,1,0:T(8,128)(2,1)} %get-tuple-element.37), channel_id=1, source_target_pairs={{1,0},{2,1},{3,2},{4,3},{5,4},{6,5},{7,6},{8,7},{9,8},{10,9},{11,1... | collective-permute-start | bytes 1572872 | tf_op jit(solution)/shard_map/ppermute | solution.py:24
  23.2 5.4 %collective-permute-start.3 = (bf16[2,2,2176]{2,1,0:T(2,128)(2,1)S(1)}, bf16[2,2,2176]{2,1,0:T(2,128)(2,1)S(1)}, u32[]{:S(2)}, u32[]{:S(2)}) collective-permute-start(bf16[2,2,2176]{2,1,0:T(2,128)(2,1)S(1)} %pad_maximum_fusion.11), channel_id=1, source_target_pairs={{0,8},{1,9},{2,10},{3,11},{4,12},{5,13},{6,14},{7,15},{8,0},{9,1},... | collective-permute-start | bytes 52232 | tf_op jit(solution)/shard_map/ppermute | solution.py:48
  28.7 5.5 %collective-permute-start.4 = (bf16[2,2,2,2176]{3,2,1,0:T(2,128)(2,1)S(1)}, bf16[2,2,2,2176]{3,2,1,0:T(2,128)(2,1)S(1)}, u32[]{:S(2)}, u32[]{:S(2)}) collective-permute-start(bf16[2,2,2,2176]{3,2,1,0:T(2,128)(2,1)S(1)} %pad_maximum_fusion.9), channel_id=1, source_target_pairs={{0,4},{1,5},{2,6},{3,7},{4,0},{5,1},{6,2},{7,3},{8,12},{9,13},{10,... | collective-permute-start | bytes 104456 | tf_op jit(solution)/shard_map/ppermute | solution.py:48
  34.4 4.4 %collective-permute-start.5 = (bf16[2,2,2,2,2176]{4,3,2,1,0:T(2,128)(2,1)S(1)}, bf16[2,2,2,2,2176]{4,3,2,1,0:T(2,128)(2,1)S(1)}, u32[]{:S(2)}, u32[]{:S(2)}) collective-permute-start(bf16[2,2,2,2,2176]{4,3,2,1,0:T(2,128)(2,1)S(1)} %pad_maximum_fusion.7), channel_id=1, source_target_pairs={{0,2},{1,3},{2,0},{3,1},{4,6},{5,7},{6,4},{7,5},{8,10},{9,11},{10,... | collective-permute-start | bytes 208904 | tf_op jit(solution)/shard_map/ppermute | solution.py:48
  39.1 1.4 collective-permute-start.6
  64.9 1.0 copy-start.4
  89.3 1.6 collective-permute-start.9
  91.1 5.8 %collective-permute-start.10 = (f32[2,2,2,2,2048]{4,3,2,1,0:T(2,128)S(1)}, f32[2,2,2,2,2048]{4,3,2,1,0:T(2,128)S(1)}, u32[]{:S(2)}, u32[]{:S(2)}) collective-permute-start(f32[2,2,2,2,2048]{4,3,2,1,0:T(2,128)S(1)} %dynamic-slice_bitcast_fusion), channel_id=1, source_target_pairs={{0,2},{1,3},{2,0},{3,1},{4,6},{5,7},{6,4},{7,5},{8,10},{9,11},{10,... | collective-permute-start | bytes 393224 | tf_op jit(solution)/shard_map/ppermute | solution.py:65
  97.0 5.9 %collective-permute-start.11 = (f32[2,2,2,2048]{3,2,1,0:T(2,128)S(1)}, f32[2,2,2,2048]{3,2,1,0:T(2,128)S(1)}, u32[]{:S(2)}, u32[]{:S(2)}) collective-permute-start(f32[2,2,2,2048]{3,2,1,0:T(2,128)S(1)} %dynamic-slice_bitcast_fusion.2), channel_id=1, source_target_pairs={{0,4},{1,5},{2,6},{3,7},{4,0},{5,1},{6,2},{7,3},{8,12},{9,13},{10,... | collective-permute-start | bytes 196616 | tf_op jit(solution)/shard_map/ppermute | solution.py:65
  97.2 24.5 %collective-permute-start.7 = (f32[2,128,1024]{2,1,0:T(8,128)S(1)}, f32[2,128,1024]{2,1,0:T(8,128)}, u32[]{:S(2)}, u32[]{:S(2)}) collective-permute-start(f32[2,128,1024]{2,1,0:T(8,128)S(1)} %pad_maximum_fusion.1), channel_id=1, source_target_pairs={{0,1},{1,2},{2,3},{3,4},{4,5},{5,6},{6,7},{7,8},{8,9},{9,10},{10,1... | collective-permute-start | bytes 3145736 | tf_op jit(solution)/shard_map/ppermute | solution.py:32
  102.9 13.0 %collective-permute-start.12 = (f32[2,2,2048]{2,1,0:T(2,128)S(1)}, f32[2,2,2048]{2,1,0:T(2,128)S(1)}, u32[]{:S(2)}, u32[]{:S(2)}) collective-permute-start(f32[2,2,2048]{2,1,0:T(2,128)S(1)} %dynamic-slice_bitcast_fusion.4), channel_id=1, source_target_pairs={{0,8},{1,9},{2,10},{3,11},{4,12},{5,13},{6,14},{7,15},{8,0},{9,1},... | collective-permute-start | bytes 98312 | tf_op jit(solution)/shard_map/ppermute | solution.py:65
  104.1 17.8 %collective-permute-start.8 = (f32[2,128,1024]{2,1,0:T(8,128)}, f32[2,128,1024]{2,1,0:T(8,128)}, u32[]{:S(2)}, u32[]{:S(2)}) collective-permute-start(f32[2,128,1024]{2,1,0:T(8,128)} %pad_maximum_fusion.2), channel_id=1, source_target_pairs={{1,0},{2,1},{3,2},{4,3},{5,4},{6,5},{7,6},{8,7},{9,8},{10,9},{11,1... | collective-permute-start | bytes 3145736 | tf_op jit(solution)/shard_map/ppermute | solution.py:32
  116.0 5.6 %collective-permute-start.13 = (f32[2,2048]{1,0:T(2,128)S(1)}, f32[2,2048]{1,0:T(2,128)S(1)}, u32[]{:S(2)}, u32[]{:S(2)}) collective-permute-start(f32[2,2048]{1,0:T(2,128)S(1)} %dynamic-slice_bitcast_fusion.6), channel_id=1, source_target_pairs={{0,16},{1,17},{2,18},{3,19},{4,20},{5,21},{6,22},{7,23},{8,24},{9,... | collective-permute-start | bytes 49160 | tf_op jit(solution)/shard_map/ppermute | solution.py:65
  121.9 2.3 %copy-start.2 = (f32[512,1024]{1,0:T(8,128)S(1)}, f32[512,1024]{1,0:T(8,128)}, u32[]{:S(2)}) copy-start(f32[512,1024]{1,0:T(8,128)} %get-tuple-element.20) | copy-start | bytes 6291460
  121.9 3.0 %copy-start.3 = (f32[512,1024]{1,0:T(8,128)S(1)}, f32[512,1024]{1,0:T(8,128)}, u32[]{:S(2)}) copy-start(f32[512,1024]{1,0:T(8,128)} %get-tuple-element.21) | copy-start | bytes 6291460
  157.0 4.4 %collective-permute-start.14 = (f32[2,2,4,1024]{3,2,1,0:T(4,128)S(1)}, f32[2,2,4,1024]{3,2,1,0:T(4,128)S(1)}, u32[]{:S(2)}, u32[]{:S(2)}) collective-permute-start(f32[2,2,4,1024]{3,2,1,0:T(4,128)S(1)} %dynamic-slice_bitcast_fusion.1), channel_id=1, source_target_pairs={{0,32},{32,0},{64,96},{96,64},{128,160},{160,128},{192,224},{224,1... | collective-permute-start | bytes 196616 | tf_op jit(solution)/shard_map/ppermute | solution.py:65
  161.4 4.9 %collective-permute-start.15 = (f32[2,4,1024]{2,1,0:T(4,128)S(1)}, f32[2,4,1024]{2,1,0:T(4,128)S(1)}, u32[]{:S(2)}, u32[]{:S(2)}) collective-permute-start(f32[2,4,1024]{2,1,0:T(4,128)S(1)} %dynamic-slice_bitcast_fusion.3), channel_id=1, source_target_pairs={{0,64},{32,96},{64,0},{96,32},{128,192},{160,224},{192,128},{224,1... | collective-permute-start | bytes 98312 | tf_op jit(solution)/shard_map/ppermute | solution.py:65
  166.4 7.7 %collective-permute-start.16 = (f32[4,1024]{1,0:T(4,128)S(1)}, f32[4,1024]{1,0:T(4,128)S(1)}, u32[]{:S(2)}, u32[]{:S(2)}) collective-permute-start(f32[4,1024]{1,0:T(4,128)S(1)} %dynamic-slice_bitcast_fusion.5), channel_id=1, source_target_pairs={{0,128},{32,160},{64,192},{96,224},{128,0},{160,32},{192,64},{224,... | collective-permute-start | bytes 49160 | tf_op jit(solution)/shard_map/ppermute | solution.py:65
  174.1 7.7 %collective-permute-start.17 = (f32[4,1024]{1,0:T(4,128)S(1)}, f32[4,1024]{1,0:T(4,128)S(1)}, u32[]{:S(2)}, u32[]{:S(2)}) collective-permute-start(f32[4,1024]{1,0:T(4,128)S(1)} %bitcast_add_fusion.8), channel_id=1, source_target_pairs={{0,128},{32,160},{64,192},{96,224},{128,0},{160,32},{192,64},{224,... | collective-permute-start | bytes 49160 | tf_op jit(solution)/shard_map/ppermute | solution.py:48
  181.9 4.9 %collective-permute-start.18 = (f32[2,4,1024]{2,1,0:T(4,128)S(1)}, f32[2,4,1024]{2,1,0:T(4,128)S(1)}, u32[]{:S(2)}, u32[]{:S(2)}) collective-permute-start(f32[2,4,1024]{2,1,0:T(4,128)S(1)} %pad_maximum_fusion.10), channel_id=1, source_target_pairs={{0,64},{32,96},{64,0},{96,32},{128,192},{160,224},{192,128},{224,1... | collective-permute-start | bytes 98312 | tf_op jit(solution)/shard_map/ppermute | solution.py:48
  186.9 4.4 %collective-permute-start.19 = (f32[2,2,4,1024]{3,2,1,0:T(4,128)S(1)}, f32[2,2,4,1024]{3,2,1,0:T(4,128)S(1)}, u32[]{:S(2)}, u32[]{:S(2)}) collective-permute-start(f32[2,2,4,1024]{3,2,1,0:T(4,128)S(1)} %pad_maximum_fusion.8), channel_id=1, source_target_pairs={{0,32},{32,0},{64,96},{96,64},{128,160},{160,128},{192,224},{224,1... | collective-permute-start | bytes 196616 | tf_op jit(solution)/shard_map/ppermute | solution.py:48
Sparse Core Ops, SparseCore 0:
  65.0 91.0 reduce-scatter.1

commit v7 on v6

--- a/solution.py
+++ b/solution.py
@@ -129,7 +129,7 @@
             by_pair(padded_k.shape[0]),
             by_pair(padded_v.shape[0]),
             by_pair(coarse_k.shape[0]),
-            by_pair(coarse_v.shape[0]),
+            pl.BlockSpec((coarse_v.shape[0], lanes), lambda pair: (0, pair + width // lanes)),
             whole(counts.shape),
             whole(fine_ok.shape),
             whole(far_ok.shape),
@@ -235,7 +235,7 @@
             by_pair(padded_k.shape[0]),
             by_pair(padded_v.shape[0]),
             by_pair(coarse_k.shape[0]),
-            by_pair(coarse_v.shape[0]),
+            pl.BlockSpec((coarse_v.shape[0], lanes), lambda pair: (0, pair + width // lanes)),
             whole(counts.shape),
             whole(fine_ok.shape),
             whole(far_ok.shape),
@@ -307,8 +307,6 @@
     count_cols = jnp.broadcast_to(counts.astype(jnp.bfloat16)[:, None], (local_blocks, 128))
     packed = jnp.concatenate([coarse_keys, coarse_values, count_cols], axis=1)
     gathered = doubling_gather(packed, "seq").reshape(all_blocks, packed.shape[1])
-    gathered_keys = gathered[:, :model_width]
-    gathered_values = gathered[:, model_width : 2 * model_width]
     gathered_counts = gathered[:, 2 * model_width].astype(jnp.float32)
     paired = jnp.stack([key_rows, value_rows])
     extended = padded_2(paired, (("seq", 1),), BLOCK)
@@ -324,8 +322,8 @@
         query_rows,
         padded_rows[0],
         padded_rows[1],
-        gathered_keys,
-        gathered_values,
+        gathered,
+        gathered,
         gathered_counts[None, :],
         fine_ok.astype(jnp.float32),
         far_ok.astype(jnp.float32),
@@ -341,8 +339,8 @@
         query_rows,
         padded_rows[0],
         padded_rows[1],
-        gathered_keys,
-        gathered_values,
+        gathered,
+        gathered,
         gathered_counts[None, :],
         fine_ok.astype(jnp.float32),
         far_ok.astype(jnp.float32),

time: 200 us -> 199 us (level)
    unnamed x12 -> x14, local copies, waits for them, and re-layouts: 5.27 us -> 5.22 us
  transfers between devices with their start and end apart: 21 -> 21, of which waited for: 17 -> 17; matrix products, arithmetic and copies ran while one was open for 10% -> 9% of each run, Pallas kernels for 10% -> 10%
where the time goes in v7:
time: 199 us; the launch traced here: 198 us
  waiting for transfers between devices  78.3 us (39%)
  Pallas kernels  38 us (19%)
  starting transfers between devices  37.9 us (19%)
  between operations  14.5 us (7%)
  local copies, waits for them, and re-layouts  12.8 us (6%)
  other arithmetic  12.4 us (6%)
  matrix products  3.95 us (2%)
    ppermute x8, waiting for transfers between devices, halving_scatter(): held = keep + lax.ppermute(send, axis, xor_pairs(count, bit))  29.2 us
    reduce_scatter x1, waiting for transfers between devices, per_device(): lax.psum_scatter(full_term, 'seq', scatter_dimension=0, tiled=True)  29 us
    pallas_call x1, Pallas kernels, attention_backward(): pl.pallas_call(backward_kernel, grid=(width // lanes,), in_specs=[by_pair...  20.5 us
    ppermute x8, waiting for transfers between devices, doubling_gather(): other = lax.ppermute(held, axis, xor_pairs(count, bit))  19.4 us
    pallas_call x1, Pallas kernels, attention_forward(): pl.pallas_call(functools.partial(forward_kernel, term_scale), grid=(width...  17.5 us
    ppermute x8, starting transfers between devices, doubling_gather(): other = lax.ppermute(held, axis, xor_pairs(count, bit))  13.3 us
    ppermute x8, starting transfers between devices, halving_scatter(): held = keep + lax.ppermute(send, axis, xor_pairs(count, bit))  12.9 us
    ppermute x1, starting transfers between devices, padded_2(): lax.ppermute(lax.slice_in_dim(block, 0, width, axis=dim), axis, backward)  5.75 us
  transfers between devices with their start and end apart: 21, of which 17 were waited for; matrix products, arithmetic and copies ran while one was open for 9% of the time, Pallas kernels for 10%

profile of v7, /device:TPU:8, one launch (start us, length us, event | category | flops | bytes accessed | tf_op | source)
XLA Modules:
  0.0 197.8 jit_solution(12614219060825299878)
XLA Ops:
  7.2 0.8 convert_element_type.71
  8.2 1.2 fusion.18
  9.4 1.2 fusion.20
  10.8 2.4 %collective-permute-start.2 = (bf16[2,2176]{1,0:T(2,128)(2,1)S(1)}, bf16[2,2176]{1,0:T(2,128)(2,1)S(1)}, u32[]{:S(2)}, u32[]{:S(2)}) collective-permute-start(bf16[2,2176]{1,0:T(2,128)(2,1)S(1)} %pad_maximum_fusion.12), channel_id=1, source_target_pairs={{0,16},{1,17},{2,18},{3,19},{4,20},{5,21},{6,22},{7,23},{8,24},{9,... | collective-permute-start | bytes 26120 | tf_op jit(solution)/shard_map/ppermute | solution.py:48
  13.2 1.1 constant_dynamic-update-slice_fusion.1
  14.3 1.0 fusion.22
  15.4 1.9 collective-permute-start
  17.3 5.8 %collective-permute-start.1 = (bf16[2,128,1024]{2,1,0:T(8,128)(2,1)}, bf16[2,128,1024]{2,1,0:T(8,128)(2,1)}, u32[]{:S(2)}, u32[]{:S(2)}) collective-permute-start(bf16[2,128,1024]{2,1,0:T(8,128)(2,1)} %get-tuple-element.37), channel_id=1, source_target_pairs={{1,0},{2,1},{3,2},{4,3},{5,4},{6,5},{7,6},{8,7},{9,8},{10,9},{11,1... | collective-permute-start | bytes 1572872 | tf_op jit(solution)/shard_map/ppermute | solution.py:24
  23.3 5.2 %collective-permute-done.3 = bf16[2,2,2176]{2,1,0:T(2,128)(2,1)S(1)} collective-permute-done((bf16[2,2,2176]{2,1,0:T(2,128)(2,1)S(1)}, bf16[2,2,2176]{2,1,0:T(2,128)(2,1)S(1)}, u32[]{:S(2)}, u32[]{:S(2)}) %collective-permute-start.3) | collective-permute-done | bytes 17440 | tf_op jit(solution)/shard_map/ppermute | solution.py:48
  28.8 5.4 %collective-permute-done.4 = bf16[2,2,2,2176]{3,2,1,0:T(2,128)(2,1)S(1)} collective-permute-done((bf16[2,2,2,2176]{3,2,1,0:T(2,128)(2,1)S(1)}, bf16[2,2,2,2176]{3,2,1,0:T(2,128)(2,1)S(1)}, u32[]{:S(2)}, u32[]{:S(2)}) %collective-permute-start.4) | collective-permute-done | bytes 34848 | tf_op jit(solution)/shard_map/ppermute | solution.py:48
  35.1 2.0 %copy.21 = bf16[1,256,1024]{1,2,0:T(8,128)(2,1)} copy(bf16[1,256,1024]{2,1,0:T(8,128)(2,1)} %param.10) | data formatting | bytes 1048576 | tf_op args[4]
  37.2 1.6 collective-permute-done.5
  40.9 1.1 pad_maximum_fusion.4
  42.0 1.1 reshape_reshape.12.ck_ref.cv_ref
  43.7 1.4 pad_maximum_fusion
  45.1 1.5 slice_bitcast_fusion
  46.7 17.5 %shard_map.93 = (bf16[256,1024]{1,0:T(8,128)(2,1)}, f32[1024,1024]{1,0:T(8,128)}) custom-call(bf16[256,1024]{1,0:T(8,128)(2,1)} %bitcast.141, bf16[512,1024]{1,0:T(8,128)(2,1)} %get-tuple-element.35.k_ref, bf16[512,1024]{1,0:T(8,128)(2,1)} %get-tuple-element.34.v_ref, bf16[64,2176]{1,0:T(8,128)(2,1)} %copy-done.1, bf16[64,2176]{1,0:T(8,128)(2,1)} %copy-done.1, ...), custom_call_target="tpu_custom_call" | custom-call | tf_op jit(solution)/shard_map/pallas_call | solution.py:124
  64.2 1.0 copy-done.5
  65.2 1.5 convolution_convert_fusion.g_ref
  66.7 20.5 %shard_map.94 = (bf16[256,1024]{1,0:T(8,128)(2,1)}, f32[512,1024]{1,0:T(8,128)}, f32[512,1024]{1,0:T(8,128)}, f32[64,1024]{1,0:T(8,128)}, f32[64,1024]{1,0:T(8,128)}) custom-call(bf16[256,1024]{1,0:T(8,128)(2,1)} %bitcast.142, bf16[512,1024]{1,0:T(8,128)(2,1)} %get-tuple-element.35.k_ref, bf16[512,1024]{1,0:T(8,128)(2,1)} %get-tuple-element.34.v_ref, ...), custom_call_target="tpu_custom_call" | custom-call | tf_op jit(solution)/shard_map/pallas_call | solution.py:230
  87.3 1.1 pad_maximum_fusion.3
  89.0 1.4 collective-permute-done.9
  91.2 1.7 slice_bitcast_fusion.2
  92.9 3.4 %collective-permute-done.10 = f32[2,2,2,2,2048]{4,3,2,1,0:T(2,128)S(1)} collective-permute-done((f32[2,2,2,2,2048]{4,3,2,1,0:T(2,128)S(1)}, f32[2,2,2,2,2048]{4,3,2,1,0:T(2,128)S(1)}, u32[]{:S(2)}, u32[]{:S(2)}) %collective-permute-start.10) | collective-permute-done | bytes 131104 | tf_op jit(solution)/shard_map/ppermute | solution.py:65
  96.7 1.9 collective-permute-start.7
  98.6 3.7 %collective-permute-done.11 = f32[2,2,2,2048]{3,2,1,0:T(2,128)S(1)} collective-permute-done((f32[2,2,2,2048]{3,2,1,0:T(2,128)S(1)}, f32[2,2,2,2048]{3,2,1,0:T(2,128)S(1)}, u32[]{:S(2)}, u32[]{:S(2)}) %collective-permute-start.11) | collective-permute-done | bytes 65568 | tf_op jit(solution)/shard_map/ppermute | solution.py:65
  102.5 1.1 pad_maximum_fusion.2
  103.5 2.1 %collective-permute-start.8 = (f32[2,128,1024]{2,1,0:T(8,128)}, f32[2,128,1024]{2,1,0:T(8,128)}, u32[]{:S(2)}, u32[]{:S(2)}) collective-permute-start(f32[2,128,1024]{2,1,0:T(8,128)} %pad_maximum_fusion.2), channel_id=1, source_target_pairs={{1,0},{2,1},{3,2},{4,3},{5,4},{6,5},{7,6},{8,7},{9,8},{10,9},{11,1... | collective-permute-start | bytes 3145736 | tf_op jit(solution)/shard_map/ppermute | solution.py:32
  105.6 9.8 %collective-permute-done.12 = f32[2,2,2048]{2,1,0:T(2,128)S(1)} collective-permute-done((f32[2,2,2048]{2,1,0:T(2,128)S(1)}, f32[2,2,2048]{2,1,0:T(2,128)S(1)}, u32[]{:S(2)}, u32[]{:S(2)}) %collective-permute-start.12) | collective-permute-done | bytes 32800 | tf_op jit(solution)/shard_map/ppermute | solution.py:65
  115.5 1.3 collective-permute-start.13
  116.8 4.4 %collective-permute-done.13 = f32[2,2048]{1,0:T(2,128)S(1)} collective-permute-done((f32[2,2048]{1,0:T(2,128)S(1)}, f32[2,2048]{1,0:T(2,128)S(1)}, u32[]{:S(2)}, u32[]{:S(2)}) %collective-permute-start.13) | collective-permute-done | bytes 16416 | tf_op jit(solution)/shard_map/ppermute | solution.py:65
  121.8 1.9 pad_add_fusion
  124.8 1.3 fusion.2
  126.0 29.0 %reduce-scatter.2.cloned.1.call-done = f32[32,1024]{1,0:T(8,128)} async-done(((f32[1024,1024]{1,0:T(8,128)}), f32[32,1024]{1,0:T(8,128)}) %reduce-scatter.2.cloned.1.call-update) | async-done | bytes 131088 | tf_op jit(solution)/shard_map/reduce_scatter | solution.py:336
  155.0 0.9 reshape_reshape.14
  156.0 1.7 collective-permute-start.14
  157.7 2.7 %collective-permute-done.14 = f32[2,2,4,1024]{3,2,1,0:T(4,128)S(1)} collective-permute-done((f32[2,2,4,1024]{3,2,1,0:T(4,128)S(1)}, f32[2,2,4,1024]{3,2,1,0:T(4,128)S(1)}, u32[]{:S(2)}, u32[]{:S(2)}) %collective-permute-start.14) | collective-permute-done | bytes 65568 | tf_op jit(solution)/shard_map/ppermute | solution.py:65
  160.4 3.0 %collective-permute-start.15 = (f32[2,4,1024]{2,1,0:T(4,128)S(1)}, f32[2,4,1024]{2,1,0:T(4,128)S(1)}, u32[]{:S(2)}, u32[]{:S(2)}) collective-permute-start(f32[2,4,1024]{2,1,0:T(4,128)S(1)} %dynamic-slice_bitcast_fusion.3), channel_id=1, source_target_pairs={{0,64},{32,96},{64,0},{96,32},{128,192},{160,224},{192,128},{224,1... | collective-permute-start | bytes 98312 | tf_op jit(solution)/shard_map/ppermute | solution.py:65
  163.4 1.9 collective-permute-done.15
  165.3 5.9 %collective-permute-start.16 = (f32[4,1024]{1,0:T(4,128)S(1)}, f32[4,1024]{1,0:T(4,128)S(1)}, u32[]{:S(2)}, u32[]{:S(2)}) collective-permute-start(f32[4,1024]{1,0:T(4,128)S(1)} %dynamic-slice_bitcast_fusion.5), channel_id=1, source_target_pairs={{0,128},{32,160},{64,192},{96,224},{128,0},{160,32},{192,64},{224,... | collective-permute-start | bytes 49160 | tf_op jit(solution)/shard_map/ppermute | solution.py:65
  171.2 1.9 collective-permute-done.16
  173.1 5.8 %collective-permute-start.17 = (f32[4,1024]{1,0:T(4,128)S(1)}, f32[4,1024]{1,0:T(4,128)S(1)}, u32[]{:S(2)}, u32[]{:S(2)}) collective-permute-start(f32[4,1024]{1,0:T(4,128)S(1)} %bitcast_add_fusion.8), channel_id=1, source_target_pairs={{0,128},{32,160},{64,192},{96,224},{128,0},{160,32},{192,64},{224,... | collective-permute-start | bytes 49160 | tf_op jit(solution)/shard_map/ppermute | solution.py:48
  178.8 2.0 %collective-permute-done.17 = f32[4,1024]{1,0:T(4,128)S(1)} collective-permute-done((f32[4,1024]{1,0:T(4,128)S(1)}, f32[4,1024]{1,0:T(4,128)S(1)}, u32[]{:S(2)}, u32[]{:S(2)}) %collective-permute-start.17) | collective-permute-done | bytes 16416 | tf_op jit(solution)/shard_map/ppermute | solution.py:48
  180.8 3.1 %collective-permute-start.18 = (f32[2,4,1024]{2,1,0:T(4,128)S(1)}, f32[2,4,1024]{2,1,0:T(4,128)S(1)}, u32[]{:S(2)}, u32[]{:S(2)}) collective-permute-start(f32[2,4,1024]{2,1,0:T(4,128)S(1)} %pad_maximum_fusion.10), channel_id=1, source_target_pairs={{0,64},{32,96},{64,0},{96,32},{128,192},{160,224},{192,128},{224,1... | collective-permute-start | bytes 98312 | tf_op jit(solution)/shard_map/ppermute | solution.py:48
  183.9 1.9 collective-permute-done.18
  185.9 1.7 collective-permute-start.19
  187.5 2.7 %collective-permute-done.19 = f32[2,2,4,1024]{3,2,1,0:T(4,128)S(1)} collective-permute-done((f32[2,2,4,1024]{3,2,1,0:T(4,128)S(1)}, f32[2,2,4,1024]{3,2,1,0:T(4,128)S(1)}, u32[]{:S(2)}, u32[]{:S(2)}) %collective-permute-start.19) | collective-permute-done | bytes 65568 | tf_op jit(solution)/shard_map/ppermute | solution.py:48
  190.3 0.7 reshape_reshape.15
  (74 shorter events, 8.4 us)
Async XLA Ops:
  7.2 57.1 %copy-start = (bf16[1024,1024]{1,0:T(8,128)(2,1)S(1)}, bf16[1024,1024]{1,0:T(8,128)(2,1)}, u32[]{:S(2)}) copy-start(bf16[1024,1024]{1,0:T(8,128)(2,1)} %param.9) | copy-start | bytes 6291460
  7.2 147.8 %reduce-scatter.2.cloned.1.call-start = ((), (), s32[]{:S(2)}) async-start(), calls=%async_computation.1 | async-start | bytes 4325376 | tf_op jit(solution)/shard_map/reduce_scatter | solution.py:336
  7.2 7.0 %copy-start.2 = (bf16[1,256,1024]{2,1,0:T(8,128)(2,1)S(1)}, bf16[1,256,1024]{2,1,0:T(8,128)(2,1)}, u32[]{:S(2)}) copy-start(bf16[1,256,1024]{2,1,0:T(8,128)(2,1)} %param.8) | copy-start | bytes 1572868
  10.8 12.3 %collective-permute-start.2 = (bf16[2,2176]{1,0:T(2,128)(2,1)S(1)}, bf16[2,2176]{1,0:T(2,128)(2,1)S(1)}, u32[]{:S(2)}, u32[]{:S(2)}) collective-permute-start(bf16[2,2176]{1,0:T(2,128)(2,1)S(1)} %pad_maximum_fusion.12), channel_id=1, source_target_pairs={{0,16},{1,17},{2,18},{3,19},{4,20},{5,21},{6,22},{7,23},{8,24},{9,... | collective-permute-start | bytes 26120 | tf_op jit(solution)/shard_map/ppermute | solution.py:48
  15.4 28.4 %collective-permute-start = (bf16[2,128,1024]{2,1,0:T(8,128)(2,1)}, bf16[2,128,1024]{2,1,0:T(8,128)(2,1)}, u32[]{:S(2)}, u32[]{:S(2)}) collective-permute-start(bf16[2,128,1024]{2,1,0:T(8,128)(2,1)} %get-tuple-element.36), channel_id=1, source_target_pairs={{0,1},{1,2},{2,3},{3,4},{4,5},{5,6},{6,7},{7,8},{8,9},{9,10},{10,1... | collective-permute-start | bytes 1572872 | tf_op jit(solution)/shard_map/ppermute | solution.py:21
  17.3 26.5 %collective-permute-start.1 = (bf16[2,128,1024]{2,1,0:T(8,128)(2,1)}, bf16[2,128,1024]{2,1,0:T(8,128)(2,1)}, u32[]{:S(2)}, u32[]{:S(2)}) collective-permute-start(bf16[2,128,1024]{2,1,0:T(8,128)(2,1)} %get-tuple-element.37), channel_id=1, source_target_pairs={{1,0},{2,1},{3,2},{4,3},{5,4},{6,5},{7,6},{8,7},{9,8},{10,9},{11,1... | collective-permute-start | bytes 1572872 | tf_op jit(solution)/shard_map/ppermute | solution.py:24
  23.2 5.4 %collective-permute-start.3 = (bf16[2,2,2176]{2,1,0:T(2,128)(2,1)S(1)}, bf16[2,2,2176]{2,1,0:T(2,128)(2,1)S(1)}, u32[]{:S(2)}, u32[]{:S(2)}) collective-permute-start(bf16[2,2,2176]{2,1,0:T(2,128)(2,1)S(1)} %pad_maximum_fusion.11), channel_id=1, source_target_pairs={{0,8},{1,9},{2,10},{3,11},{4,12},{5,13},{6,14},{7,15},{8,0},{9,1},... | collective-permute-start | bytes 52232 | tf_op jit(solution)/shard_map/ppermute | solution.py:48
  28.7 5.5 %collective-permute-start.4 = (bf16[2,2,2,2176]{3,2,1,0:T(2,128)(2,1)S(1)}, bf16[2,2,2,2176]{3,2,1,0:T(2,128)(2,1)S(1)}, u32[]{:S(2)}, u32[]{:S(2)}) collective-permute-start(bf16[2,2,2,2176]{3,2,1,0:T(2,128)(2,1)S(1)} %pad_maximum_fusion.9), channel_id=1, source_target_pairs={{0,4},{1,5},{2,6},{3,7},{4,0},{5,1},{6,2},{7,3},{8,12},{9,13},{10,... | collective-permute-start | bytes 104456 | tf_op jit(solution)/shard_map/ppermute | solution.py:48
  34.4 4.4 %collective-permute-start.5 = (bf16[2,2,2,2,2176]{4,3,2,1,0:T(2,128)(2,1)S(1)}, bf16[2,2,2,2,2176]{4,3,2,1,0:T(2,128)(2,1)S(1)}, u32[]{:S(2)}, u32[]{:S(2)}) collective-permute-start(bf16[2,2,2,2,2176]{4,3,2,1,0:T(2,128)(2,1)S(1)} %pad_maximum_fusion.7), channel_id=1, source_target_pairs={{0,2},{1,3},{2,0},{3,1},{4,6},{5,7},{6,4},{7,5},{8,10},{9,11},{10,... | collective-permute-start | bytes 208904 | tf_op jit(solution)/shard_map/ppermute | solution.py:48
  39.1 1.4 collective-permute-start.6
  43.0 2.1 %copy-start.1 = (bf16[64,2176]{1,0:T(8,128)(2,1)}, bf16[64,2176]{1,0:T(8,128)(2,1)S(1)}, u32[]{:S(2)}) copy-start(bf16[64,2176]{1,0:T(8,128)(2,1)S(1)} %reshape_reshape.12.ck_ref.cv_ref) | copy-start | bytes 835588
  64.2 1.0 copy-start.5
  88.7 1.6 collective-permute-start.9
  90.5 5.8 %collective-permute-start.10 = (f32[2,2,2,2,2048]{4,3,2,1,0:T(2,128)S(1)}, f32[2,2,2,2,2048]{4,3,2,1,0:T(2,128)S(1)}, u32[]{:S(2)}, u32[]{:S(2)}) collective-permute-start(f32[2,2,2,2,2048]{4,3,2,1,0:T(2,128)S(1)} %dynamic-slice_bitcast_fusion), channel_id=1, source_target_pairs={{0,2},{1,3},{2,0},{3,1},{4,6},{5,7},{6,4},{7,5},{8,10},{9,11},{10,... | collective-permute-start | bytes 393224 | tf_op jit(solution)/shard_map/ppermute | solution.py:65
  96.4 5.9 %collective-permute-start.11 = (f32[2,2,2,2048]{3,2,1,0:T(2,128)S(1)}, f32[2,2,2,2048]{3,2,1,0:T(2,128)S(1)}, u32[]{:S(2)}, u32[]{:S(2)}) collective-permute-start(f32[2,2,2,2048]{3,2,1,0:T(2,128)S(1)} %dynamic-slice_bitcast_fusion.2), channel_id=1, source_target_pairs={{0,4},{1,5},{2,6},{3,7},{4,0},{5,1},{6,2},{7,3},{8,12},{9,13},{10,... | collective-permute-start | bytes 196616 | tf_op jit(solution)/shard_map/ppermute | solution.py:65
  96.7 24.5 %collective-permute-start.7 = (f32[2,128,1024]{2,1,0:T(8,128)S(1)}, f32[2,128,1024]{2,1,0:T(8,128)}, u32[]{:S(2)}, u32[]{:S(2)}) collective-permute-start(f32[2,128,1024]{2,1,0:T(8,128)S(1)} %pad_maximum_fusion.1), channel_id=1, source_target_pairs={{0,1},{1,2},{2,3},{3,4},{4,5},{5,6},{6,7},{7,8},{8,9},{9,10},{10,1... | collective-permute-start | bytes 3145736 | tf_op jit(solution)/shard_map/ppermute | solution.py:32
  102.4 13.1 %collective-permute-start.12 = (f32[2,2,2048]{2,1,0:T(2,128)S(1)}, f32[2,2,2048]{2,1,0:T(2,128)S(1)}, u32[]{:S(2)}, u32[]{:S(2)}) collective-permute-start(f32[2,2,2048]{2,1,0:T(2,128)S(1)} %dynamic-slice_bitcast_fusion.4), channel_id=1, source_target_pairs={{0,8},{1,9},{2,10},{3,11},{4,12},{5,13},{6,14},{7,15},{8,0},{9,1},... | collective-permute-start | bytes 98312 | tf_op jit(solution)/shard_map/ppermute | solution.py:65
  103.5 18.3 %collective-permute-start.8 = (f32[2,128,1024]{2,1,0:T(8,128)}, f32[2,128,1024]{2,1,0:T(8,128)}, u32[]{:S(2)}, u32[]{:S(2)}) collective-permute-start(f32[2,128,1024]{2,1,0:T(8,128)} %pad_maximum_fusion.2), channel_id=1, source_target_pairs={{1,0},{2,1},{3,2},{4,3},{5,4},{6,5},{7,6},{8,7},{9,8},{10,9},{11,1... | collective-permute-start | bytes 3145736 | tf_op jit(solution)/shard_map/ppermute | solution.py:32
  115.5 5.7 %collective-permute-start.13 = (f32[2,2048]{1,0:T(2,128)S(1)}, f32[2,2048]{1,0:T(2,128)S(1)}, u32[]{:S(2)}, u32[]{:S(2)}) collective-permute-start(f32[2,2048]{1,0:T(2,128)S(1)} %dynamic-slice_bitcast_fusion.6), channel_id=1, source_target_pairs={{0,16},{1,17},{2,18},{3,19},{4,20},{5,21},{6,22},{7,23},{8,24},{9,... | collective-permute-start | bytes 49160 | tf_op jit(solution)/shard_map/ppermute | solution.py:65
  121.8 2.3 %copy-start.3 = (f32[512,1024]{1,0:T(8,128)S(1)}, f32[512,1024]{1,0:T(8,128)}, u32[]{:S(2)}) copy-start(f32[512,1024]{1,0:T(8,128)} %get-tuple-element.20) | copy-start | bytes 6291460
  121.8 3.0 %copy-start.4 = (f32[512,1024]{1,0:T(8,128)S(1)}, f32[512,1024]{1,0:T(8,128)}, u32[]{:S(2)}) copy-start(f32[512,1024]{1,0:T(8,128)} %get-tuple-element.21) | copy-start | bytes 6291460
  156.0 4.4 %collective-permute-start.14 = (f32[2,2,4,1024]{3,2,1,0:T(4,128)S(1)}, f32[2,2,4,1024]{3,2,1,0:T(4,128)S(1)}, u32[]{:S(2)}, u32[]{:S(2)}) collective-permute-start(f32[2,2,4,1024]{3,2,1,0:T(4,128)S(1)} %dynamic-slice_bitcast_fusion.1), channel_id=1, source_target_pairs={{0,32},{32,0},{64,96},{96,64},{128,160},{160,128},{192,224},{224,1... | collective-permute-start | bytes 196616 | tf_op jit(solution)/shard_map/ppermute | solution.py:65
  160.4 4.9 %collective-permute-start.15 = (f32[2,4,1024]{2,1,0:T(4,128)S(1)}, f32[2,4,1024]{2,1,0:T(4,128)S(1)}, u32[]{:S(2)}, u32[]{:S(2)}) collective-permute-start(f32[2,4,1024]{2,1,0:T(4,128)S(1)} %dynamic-slice_bitcast_fusion.3), channel_id=1, source_target_pairs={{0,64},{32,96},{64,0},{96,32},{128,192},{160,224},{192,128},{224,1... | collective-permute-start | bytes 98312 | tf_op jit(solution)/shard_map/ppermute | solution.py:65
  165.3 7.7 %collective-permute-start.16 = (f32[4,1024]{1,0:T(4,128)S(1)}, f32[4,1024]{1,0:T(4,128)S(1)}, u32[]{:S(2)}, u32[]{:S(2)}) collective-permute-start(f32[4,1024]{1,0:T(4,128)S(1)} %dynamic-slice_bitcast_fusion.5), channel_id=1, source_target_pairs={{0,128},{32,160},{64,192},{96,224},{128,0},{160,32},{192,64},{224,... | collective-permute-start | bytes 49160 | tf_op jit(solution)/shard_map/ppermute | solution.py:65
  173.1 7.7 %collective-permute-start.17 = (f32[4,1024]{1,0:T(4,128)S(1)}, f32[4,1024]{1,0:T(4,128)S(1)}, u32[]{:S(2)}, u32[]{:S(2)}) collective-permute-start(f32[4,1024]{1,0:T(4,128)S(1)} %bitcast_add_fusion.8), channel_id=1, source_target_pairs={{0,128},{32,160},{64,192},{96,224},{128,0},{160,32},{192,64},{224,... | collective-permute-start | bytes 49160 | tf_op jit(solution)/shard_map/ppermute | solution.py:48
  180.8 5.0 %collective-permute-start.18 = (f32[2,4,1024]{2,1,0:T(4,128)S(1)}, f32[2,4,1024]{2,1,0:T(4,128)S(1)}, u32[]{:S(2)}, u32[]{:S(2)}) collective-permute-start(f32[2,4,1024]{2,1,0:T(4,128)S(1)} %pad_maximum_fusion.10), channel_id=1, source_target_pairs={{0,64},{32,96},{64,0},{96,32},{128,192},{160,224},{192,128},{224,1... | collective-permute-start | bytes 98312 | tf_op jit(solution)/shard_map/ppermute | solution.py:48
  185.9 4.4 %collective-permute-start.19 = (f32[2,2,4,1024]{3,2,1,0:T(4,128)S(1)}, f32[2,2,4,1024]{3,2,1,0:T(4,128)S(1)}, u32[]{:S(2)}, u32[]{:S(2)}) collective-permute-start(f32[2,2,4,1024]{3,2,1,0:T(4,128)S(1)} %pad_maximum_fusion.8), channel_id=1, source_target_pairs={{0,32},{32,0},{64,96},{96,64},{128,160},{160,128},{192,224},{224,1... | collective-permute-start | bytes 196616 | tf_op jit(solution)/shard_map/ppermute | solution.py:48
Sparse Core Ops, SparseCore 0:
  64.3 90.6 reduce-scatter.1

commit v8 on v7

--- a/solution.py
+++ b/solution.py
@@ -118,7 +118,7 @@
 def attention_forward(query_rows, padded_k, padded_v, coarse_k, coarse_v, counts, fine_ok, far_ok,
                       grad_t, term_scale):
     tokens, width = query_rows.shape
-    lanes = 4 * HEAD_DIM
+    lanes = 8 * HEAD_DIM
     by_pair = lambda rows: pl.BlockSpec((rows, lanes), lambda pair: (0, pair))
     whole = lambda shape: pl.BlockSpec(shape, lambda pair: (0, 0))
     return pl.pallas_call(

time: 199 us -> 203 us (1.020)
  Pallas kernels: 38 us -> 41.3 us
    pallas_call x1, Pallas kernels: 17.5 us -> 20.8 us  [attention_forward(): pl.pallas_call(functools.partial(forward_kernel, term_scale), grid=(width...]
where the time goes in v8:
time: 203 us; the launch traced here: 202 us
  waiting for transfers between devices  78.6 us (39%)
  Pallas kernels  41.3 us (20%)
  starting transfers between devices  37.8 us (19%)
  between operations  14.5 us (7%)
  local copies, waits for them, and re-layouts  12.9 us (6%)
  other arithmetic  12.3 us (6%)
  matrix products  3.95 us (2%)
    reduce_scatter x1, waiting for transfers between devices, per_device(): lax.psum_scatter(full_term, 'seq', scatter_dimension=0, tiled=True)  29.7 us
    ppermute x8, waiting for transfers between devices, halving_scatter(): held = keep + lax.ppermute(send, axis, xor_pairs(count, bit))  29.1 us
    pallas_call x1, Pallas kernels, attention_forward(): pl.pallas_call(functools.partial(forward_kernel, term_scale), grid=(width...  20.8 us
    pallas_call x1, Pallas kernels, attention_backward(): pl.pallas_call(backward_kernel, grid=(width // lanes,), in_specs=[by_pair...  20.5 us
    ppermute x8, waiting for transfers between devices, doubling_gather(): other = lax.ppermute(held, axis, xor_pairs(count, bit))  19.6 us
    ppermute x8, starting transfers between devices, doubling_gather(): other = lax.ppermute(held, axis, xor_pairs(count, bit))  13.3 us
    ppermute x8, starting transfers between devices, halving_scatter(): held = keep + lax.ppermute(send, axis, xor_pairs(count, bit))  12.9 us
    ppermute x1, starting transfers between devices, padded_2(): lax.ppermute(lax.slice_in_dim(block, 0, width, axis=dim), axis, backward)  5.75 us
  transfers between devices with their start and end apart: 21, of which 17 were waited for; matrix products, arithmetic and copies ran while one was open for 9% of the time, Pallas kernels for 10%

profile of v8, /device:TPU:8, one launch (start us, length us, event | category | flops | bytes accessed | tf_op | source)
XLA Modules:
  0.0 201.5 jit_solution(15803359112249260359)
XLA Ops:
  7.2 0.8 convert_element_type.71
  8.2 1.2 fusion.18
  9.4 1.2 fusion.20
  10.8 2.4 %collective-permute-start.2 = (bf16[2,2176]{1,0:T(2,128)(2,1)S(1)}, bf16[2,2176]{1,0:T(2,128)(2,1)S(1)}, u32[]{:S(2)}, u32[]{:S(2)}) collective-permute-start(bf16[2,2176]{1,0:T(2,128)(2,1)S(1)} %pad_maximum_fusion.12), channel_id=1, source_target_pairs={{0,16},{1,17},{2,18},{3,19},{4,20},{5,21},{6,22},{7,23},{8,24},{9,... | collective-permute-start | bytes 26120 | tf_op jit(solution)/shard_map/ppermute | solution.py:48
  13.2 1.1 constant_dynamic-update-slice_fusion.1
  14.3 1.0 fusion.22
  15.4 1.9 collective-permute-start
  17.3 5.8 %collective-permute-start.1 = (bf16[2,128,1024]{2,1,0:T(8,128)(2,1)}, bf16[2,128,1024]{2,1,0:T(8,128)(2,1)}, u32[]{:S(2)}, u32[]{:S(2)}) collective-permute-start(bf16[2,128,1024]{2,1,0:T(8,128)(2,1)} %get-tuple-element.37), channel_id=1, source_target_pairs={{1,0},{2,1},{3,2},{4,3},{5,4},{6,5},{7,6},{8,7},{9,8},{10,9},{11,1... | collective-permute-start | bytes 1572872 | tf_op jit(solution)/shard_map/ppermute | solution.py:24
  23.3 5.2 %collective-permute-done.3 = bf16[2,2,2176]{2,1,0:T(2,128)(2,1)S(1)} collective-permute-done((bf16[2,2,2176]{2,1,0:T(2,128)(2,1)S(1)}, bf16[2,2,2176]{2,1,0:T(2,128)(2,1)S(1)}, u32[]{:S(2)}, u32[]{:S(2)}) %collective-permute-start.3) | collective-permute-done | bytes 17440 | tf_op jit(solution)/shard_map/ppermute | solution.py:48
  28.8 5.4 %collective-permute-done.4 = bf16[2,2,2,2176]{3,2,1,0:T(2,128)(2,1)S(1)} collective-permute-done((bf16[2,2,2,2176]{3,2,1,0:T(2,128)(2,1)S(1)}, bf16[2,2,2,2176]{3,2,1,0:T(2,128)(2,1)S(1)}, u32[]{:S(2)}, u32[]{:S(2)}) %collective-permute-start.4) | collective-permute-done | bytes 34848 | tf_op jit(solution)/shard_map/ppermute | solution.py:48
  35.1 2.0 %copy.21 = bf16[1,256,1024]{1,2,0:T(8,128)(2,1)} copy(bf16[1,256,1024]{2,1,0:T(8,128)(2,1)} %param.10) | data formatting | bytes 1048576 | tf_op args[4]
  37.2 1.6 collective-permute-done.5
  41.1 1.1 pad_maximum_fusion.4
  42.2 1.1 reshape_reshape.12.ck_ref.cv_ref
  43.9 1.4 pad_maximum_fusion
  45.3 1.5 slice_bitcast_fusion
  46.9 20.8 %shard_map.93 = (bf16[256,1024]{1,0:T(8,128)(2,1)}, f32[1024,1024]{1,0:T(8,128)}) custom-call(bf16[256,1024]{1,0:T(8,128)(2,1)} %bitcast.141, bf16[512,1024]{1,0:T(8,128)(2,1)} %get-tuple-element.35.k_ref, bf16[512,1024]{1,0:T(8,128)(2,1)} %get-tuple-element.34.v_ref, bf16[64,2176]{1,0:T(8,128)(2,1)} %copy-done.1, bf16[64,2176]{1,0:T(8,128)(2,1)} %copy-done.1, ...), custom_call_target="tpu_custom_call" | custom-call | tf_op jit(solution)/shard_map/pallas_call | solution.py:124
  67.7 1.0 copy-done.5
  68.7 1.5 convolution_convert_fusion.g_ref
  70.2 20.5 %shard_map.94 = (bf16[256,1024]{1,0:T(8,128)(2,1)}, f32[512,1024]{1,0:T(8,128)}, f32[512,1024]{1,0:T(8,128)}, f32[64,1024]{1,0:T(8,128)}, f32[64,1024]{1,0:T(8,128)}) custom-call(bf16[256,1024]{1,0:T(8,128)(2,1)} %bitcast.142, bf16[512,1024]{1,0:T(8,128)(2,1)} %get-tuple-element.35.k_ref, bf16[512,1024]{1,0:T(8,128)(2,1)} %get-tuple-element.34.v_ref, ...), custom_call_target="tpu_custom_call" | custom-call | tf_op jit(solution)/shard_map/pallas_call | solution.py:230
  90.7 1.1 pad_maximum_fusion.3
  92.5 1.4 collective-permute-done.9
  94.5 1.7 slice_bitcast_fusion.2
  96.2 3.4 %collective-permute-done.10 = f32[2,2,2,2,2048]{4,3,2,1,0:T(2,128)S(1)} collective-permute-done((f32[2,2,2,2,2048]{4,3,2,1,0:T(2,128)S(1)}, f32[2,2,2,2,2048]{4,3,2,1,0:T(2,128)S(1)}, u32[]{:S(2)}, u32[]{:S(2)}) %collective-permute-start.10) | collective-permute-done | bytes 131104 | tf_op jit(solution)/shard_map/ppermute | solution.py:65
  100.0 1.9 collective-permute-start.7
  101.9 3.7 %collective-permute-done.11 = f32[2,2,2,2048]{3,2,1,0:T(2,128)S(1)} collective-permute-done((f32[2,2,2,2048]{3,2,1,0:T(2,128)S(1)}, f32[2,2,2,2048]{3,2,1,0:T(2,128)S(1)}, u32[]{:S(2)}, u32[]{:S(2)}) %collective-permute-start.11) | collective-permute-done | bytes 65568 | tf_op jit(solution)/shard_map/ppermute | solution.py:65
  106.0 1.1 pad_maximum_fusion.2
  107.1 2.0 %collective-permute-start.8 = (f32[2,128,1024]{2,1,0:T(8,128)}, f32[2,128,1024]{2,1,0:T(8,128)}, u32[]{:S(2)}, u32[]{:S(2)}) collective-permute-start(f32[2,128,1024]{2,1,0:T(8,128)} %pad_maximum_fusion.2), channel_id=1, source_target_pairs={{1,0},{2,1},{3,2},{4,3},{5,4},{6,5},{7,6},{8,7},{9,8},{10,9},{11,1... | collective-permute-start | bytes 3145736 | tf_op jit(solution)/shard_map/ppermute | solution.py:32
  109.1 9.7 %collective-permute-done.12 = f32[2,2,2048]{2,1,0:T(2,128)S(1)} collective-permute-done((f32[2,2,2048]{2,1,0:T(2,128)S(1)}, f32[2,2,2048]{2,1,0:T(2,128)S(1)}, u32[]{:S(2)}, u32[]{:S(2)}) %collective-permute-start.12) | collective-permute-done | bytes 32800 | tf_op jit(solution)/shard_map/ppermute | solution.py:65
  118.9 1.4 collective-permute-start.13
  120.2 4.2 %collective-permute-done.13 = f32[2,2048]{1,0:T(2,128)S(1)} collective-permute-done((f32[2,2048]{1,0:T(2,128)S(1)}, f32[2,2048]{1,0:T(2,128)S(1)}, u32[]{:S(2)}, u32[]{:S(2)}) %collective-permute-start.13) | collective-permute-done | bytes 16416 | tf_op jit(solution)/shard_map/ppermute | solution.py:65
  124.9 1.8 pad_add_fusion
  127.9 1.3 fusion.2
  129.1 29.7 %reduce-scatter.2.cloned.1.call-done = f32[32,1024]{1,0:T(8,128)} async-done(((f32[1024,1024]{1,0:T(8,128)}), f32[32,1024]{1,0:T(8,128)}) %reduce-scatter.2.cloned.1.call-update) | async-done | bytes 131088 | tf_op jit(solution)/shard_map/reduce_scatter | solution.py:336
  158.8 0.9 reshape_reshape.14
  159.7 1.6 collective-permute-start.14
  161.4 2.7 %collective-permute-done.14 = f32[2,2,4,1024]{3,2,1,0:T(4,128)S(1)} collective-permute-done((f32[2,2,4,1024]{3,2,1,0:T(4,128)S(1)}, f32[2,2,4,1024]{3,2,1,0:T(4,128)S(1)}, u32[]{:S(2)}, u32[]{:S(2)}) %collective-permute-start.14) | collective-permute-done | bytes 65568 | tf_op jit(solution)/shard_map/ppermute | solution.py:65
  164.1 2.9 %collective-permute-start.15 = (f32[2,4,1024]{2,1,0:T(4,128)S(1)}, f32[2,4,1024]{2,1,0:T(4,128)S(1)}, u32[]{:S(2)}, u32[]{:S(2)}) collective-permute-start(f32[2,4,1024]{2,1,0:T(4,128)S(1)} %dynamic-slice_bitcast_fusion.3), channel_id=1, source_target_pairs={{0,64},{32,96},{64,0},{96,32},{128,192},{160,224},{192,128},{224,1... | collective-permute-start | bytes 98312 | tf_op jit(solution)/shard_map/ppermute | solution.py:65
  167.1 2.0 collective-permute-done.15
  169.1 5.8 %collective-permute-start.16 = (f32[4,1024]{1,0:T(4,128)S(1)}, f32[4,1024]{1,0:T(4,128)S(1)}, u32[]{:S(2)}, u32[]{:S(2)}) collective-permute-start(f32[4,1024]{1,0:T(4,128)S(1)} %dynamic-slice_bitcast_fusion.5), channel_id=1, source_target_pairs={{0,128},{32,160},{64,192},{96,224},{128,0},{160,32},{192,64},{224,... | collective-permute-start | bytes 49160 | tf_op jit(solution)/shard_map/ppermute | solution.py:65
  174.9 1.9 collective-permute-done.16
  176.8 5.7 %collective-permute-start.17 = (f32[4,1024]{1,0:T(4,128)S(1)}, f32[4,1024]{1,0:T(4,128)S(1)}, u32[]{:S(2)}, u32[]{:S(2)}) collective-permute-start(f32[4,1024]{1,0:T(4,128)S(1)} %bitcast_add_fusion.8), channel_id=1, source_target_pairs={{0,128},{32,160},{64,192},{96,224},{128,0},{160,32},{192,64},{224,... | collective-permute-start | bytes 49160 | tf_op jit(solution)/shard_map/ppermute | solution.py:48
  182.6 2.0 collective-permute-done.17
  184.6 3.0 %collective-permute-start.18 = (f32[2,4,1024]{2,1,0:T(4,128)S(1)}, f32[2,4,1024]{2,1,0:T(4,128)S(1)}, u32[]{:S(2)}, u32[]{:S(2)}) collective-permute-start(f32[2,4,1024]{2,1,0:T(4,128)S(1)} %pad_maximum_fusion.10), channel_id=1, source_target_pairs={{0,64},{32,96},{64,0},{96,32},{128,192},{160,224},{192,128},{224,1... | collective-permute-start | bytes 98312 | tf_op jit(solution)/shard_map/ppermute | solution.py:48
  187.6 1.9 collective-permute-done.18
  189.6 1.6 collective-permute-start.19
  191.2 2.8 %collective-permute-done.19 = f32[2,2,4,1024]{3,2,1,0:T(4,128)S(1)} collective-permute-done((f32[2,2,4,1024]{3,2,1,0:T(4,128)S(1)}, f32[2,2,4,1024]{3,2,1,0:T(4,128)S(1)}, u32[]{:S(2)}, u32[]{:S(2)}) %collective-permute-start.19) | collective-permute-done | bytes 65568 | tf_op jit(solution)/shard_map/ppermute | solution.py:48
  194.0 0.7 reshape_reshape.15
  (74 shorter events, 8.3 us)
Async XLA Ops:
  7.2 60.5 %copy-start = (bf16[1024,1024]{1,0:T(8,128)(2,1)S(1)}, bf16[1024,1024]{1,0:T(8,128)(2,1)}, u32[]{:S(2)}) copy-start(bf16[1024,1024]{1,0:T(8,128)(2,1)} %param.9) | copy-start | bytes 6291460
  7.2 151.6 %reduce-scatter.2.cloned.1.call-start = ((), (), s32[]{:S(2)}) async-start(), calls=%async_computation.1 | async-start | bytes 4325376 | tf_op jit(solution)/shard_map/reduce_scatter | solution.py:336
  7.2 7.0 %copy-start.2 = (bf16[1,256,1024]{2,1,0:T(8,128)(2,1)S(1)}, bf16[1,256,1024]{2,1,0:T(8,128)(2,1)}, u32[]{:S(2)}) copy-start(bf16[1,256,1024]{2,1,0:T(8,128)(2,1)} %param.8) | copy-start | bytes 1572868
  10.8 12.3 %collective-permute-start.2 = (bf16[2,2176]{1,0:T(2,128)(2,1)S(1)}, bf16[2,2176]{1,0:T(2,128)(2,1)S(1)}, u32[]{:S(2)}, u32[]{:S(2)}) collective-permute-start(bf16[2,2176]{1,0:T(2,128)(2,1)S(1)} %pad_maximum_fusion.12), channel_id=1, source_target_pairs={{0,16},{1,17},{2,18},{3,19},{4,20},{5,21},{6,22},{7,23},{8,24},{9,... | collective-permute-start | bytes 26120 | tf_op jit(solution)/shard_map/ppermute | solution.py:48
  15.4 28.6 %collective-permute-start = (bf16[2,128,1024]{2,1,0:T(8,128)(2,1)}, bf16[2,128,1024]{2,1,0:T(8,128)(2,1)}, u32[]{:S(2)}, u32[]{:S(2)}) collective-permute-start(bf16[2,128,1024]{2,1,0:T(8,128)(2,1)} %get-tuple-element.36), channel_id=1, source_target_pairs={{0,1},{1,2},{2,3},{3,4},{4,5},{5,6},{6,7},{7,8},{8,9},{9,10},{10,1... | collective-permute-start | bytes 1572872 | tf_op jit(solution)/shard_map/ppermute | solution.py:21
  17.3 26.6 %collective-permute-start.1 = (bf16[2,128,1024]{2,1,0:T(8,128)(2,1)}, bf16[2,128,1024]{2,1,0:T(8,128)(2,1)}, u32[]{:S(2)}, u32[]{:S(2)}) collective-permute-start(bf16[2,128,1024]{2,1,0:T(8,128)(2,1)} %get-tuple-element.37), channel_id=1, source_target_pairs={{1,0},{2,1},{3,2},{4,3},{5,4},{6,5},{7,6},{8,7},{9,8},{10,9},{11,1... | collective-permute-start | bytes 1572872 | tf_op jit(solution)/shard_map/ppermute | solution.py:24
  23.2 5.4 %collective-permute-start.3 = (bf16[2,2,2176]{2,1,0:T(2,128)(2,1)S(1)}, bf16[2,2,2176]{2,1,0:T(2,128)(2,1)S(1)}, u32[]{:S(2)}, u32[]{:S(2)}) collective-permute-start(bf16[2,2,2176]{2,1,0:T(2,128)(2,1)S(1)} %pad_maximum_fusion.11), channel_id=1, source_target_pairs={{0,8},{1,9},{2,10},{3,11},{4,12},{5,13},{6,14},{7,15},{8,0},{9,1},... | collective-permute-start | bytes 52232 | tf_op jit(solution)/shard_map/ppermute | solution.py:48
  28.7 5.5 %collective-permute-start.4 = (bf16[2,2,2,2176]{3,2,1,0:T(2,128)(2,1)S(1)}, bf16[2,2,2,2176]{3,2,1,0:T(2,128)(2,1)S(1)}, u32[]{:S(2)}, u32[]{:S(2)}) collective-permute-start(bf16[2,2,2,2176]{3,2,1,0:T(2,128)(2,1)S(1)} %pad_maximum_fusion.9), channel_id=1, source_target_pairs={{0,4},{1,5},{2,6},{3,7},{4,0},{5,1},{6,2},{7,3},{8,12},{9,13},{10,... | collective-permute-start | bytes 104456 | tf_op jit(solution)/shard_map/ppermute | solution.py:48
  34.4 4.4 %collective-permute-start.5 = (bf16[2,2,2,2,2176]{4,3,2,1,0:T(2,128)(2,1)S(1)}, bf16[2,2,2,2,2176]{4,3,2,1,0:T(2,128)(2,1)S(1)}, u32[]{:S(2)}, u32[]{:S(2)}) collective-permute-start(bf16[2,2,2,2,2176]{4,3,2,1,0:T(2,128)(2,1)S(1)} %pad_maximum_fusion.7), channel_id=1, source_target_pairs={{0,2},{1,3},{2,0},{3,1},{4,6},{5,7},{6,4},{7,5},{8,10},{9,11},{10,... | collective-permute-start | bytes 208904 | tf_op jit(solution)/shard_map/ppermute | solution.py:48
  39.1 1.6 collective-permute-start.6
  43.2 2.1 %copy-start.1 = (bf16[64,2176]{1,0:T(8,128)(2,1)}, bf16[64,2176]{1,0:T(8,128)(2,1)S(1)}, u32[]{:S(2)}) copy-start(bf16[64,2176]{1,0:T(8,128)(2,1)S(1)} %reshape_reshape.12.ck_ref.cv_ref) | copy-start | bytes 835588
  67.7 1.0 copy-start.5
  92.2 1.6 collective-permute-start.9
  94.0 5.6 %collective-permute-start.10 = (f32[2,2,2,2,2048]{4,3,2,1,0:T(2,128)S(1)}, f32[2,2,2,2,2048]{4,3,2,1,0:T(2,128)S(1)}, u32[]{:S(2)}, u32[]{:S(2)}) collective-permute-start(f32[2,2,2,2,2048]{4,3,2,1,0:T(2,128)S(1)} %dynamic-slice_bitcast_fusion), channel_id=1, source_target_pairs={{0,2},{1,3},{2,0},{3,1},{4,6},{5,7},{6,4},{7,5},{8,10},{9,11},{10,... | collective-permute-start | bytes 393224 | tf_op jit(solution)/shard_map/ppermute | solution.py:65
  99.7 5.9 %collective-permute-start.11 = (f32[2,2,2,2048]{3,2,1,0:T(2,128)S(1)}, f32[2,2,2,2048]{3,2,1,0:T(2,128)S(1)}, u32[]{:S(2)}, u32[]{:S(2)}) collective-permute-start(f32[2,2,2,2048]{3,2,1,0:T(2,128)S(1)} %dynamic-slice_bitcast_fusion.2), channel_id=1, source_target_pairs={{0,4},{1,5},{2,6},{3,7},{4,0},{5,1},{6,2},{7,3},{8,12},{9,13},{10,... | collective-permute-start | bytes 196616 | tf_op jit(solution)/shard_map/ppermute | solution.py:65
  100.0 24.6 %collective-permute-start.7 = (f32[2,128,1024]{2,1,0:T(8,128)S(1)}, f32[2,128,1024]{2,1,0:T(8,128)}, u32[]{:S(2)}, u32[]{:S(2)}) collective-permute-start(f32[2,128,1024]{2,1,0:T(8,128)S(1)} %pad_maximum_fusion.1), channel_id=1, source_target_pairs={{0,1},{1,2},{2,3},{3,4},{4,5},{5,6},{6,7},{7,8},{8,9},{9,10},{10,1... | collective-permute-start | bytes 3145736 | tf_op jit(solution)/shard_map/ppermute | solution.py:32
  105.7 13.2 %collective-permute-start.12 = (f32[2,2,2048]{2,1,0:T(2,128)S(1)}, f32[2,2,2048]{2,1,0:T(2,128)S(1)}, u32[]{:S(2)}, u32[]{:S(2)}) collective-permute-start(f32[2,2,2048]{2,1,0:T(2,128)S(1)} %dynamic-slice_bitcast_fusion.4), channel_id=1, source_target_pairs={{0,8},{1,9},{2,10},{3,11},{4,12},{5,13},{6,14},{7,15},{8,0},{9,1},... | collective-permute-start | bytes 98312 | tf_op jit(solution)/shard_map/ppermute | solution.py:65
  107.1 17.8 %collective-permute-start.8 = (f32[2,128,1024]{2,1,0:T(8,128)}, f32[2,128,1024]{2,1,0:T(8,128)}, u32[]{:S(2)}, u32[]{:S(2)}) collective-permute-start(f32[2,128,1024]{2,1,0:T(8,128)} %pad_maximum_fusion.2), channel_id=1, source_target_pairs={{1,0},{2,1},{3,2},{4,3},{5,4},{6,5},{7,6},{8,7},{9,8},{10,9},{11,1... | collective-permute-start | bytes 3145736 | tf_op jit(solution)/shard_map/ppermute | solution.py:32
  118.9 5.6 %collective-permute-start.13 = (f32[2,2048]{1,0:T(2,128)S(1)}, f32[2,2048]{1,0:T(2,128)S(1)}, u32[]{:S(2)}, u32[]{:S(2)}) collective-permute-start(f32[2,2048]{1,0:T(2,128)S(1)} %dynamic-slice_bitcast_fusion.6), channel_id=1, source_target_pairs={{0,16},{1,17},{2,18},{3,19},{4,20},{5,21},{6,22},{7,23},{8,24},{9,... | collective-permute-start | bytes 49160 | tf_op jit(solution)/shard_map/ppermute | solution.py:65
  124.9 2.3 %copy-start.3 = (f32[512,1024]{1,0:T(8,128)S(1)}, f32[512,1024]{1,0:T(8,128)}, u32[]{:S(2)}) copy-start(f32[512,1024]{1,0:T(8,128)} %get-tuple-element.20) | copy-start | bytes 6291460
  124.9 3.0 %copy-start.4 = (f32[512,1024]{1,0:T(8,128)S(1)}, f32[512,1024]{1,0:T(8,128)}, u32[]{:S(2)}) copy-start(f32[512,1024]{1,0:T(8,128)} %get-tuple-element.21) | copy-start | bytes 6291460
  159.7 4.4 %collective-permute-start.14 = (f32[2,2,4,1024]{3,2,1,0:T(4,128)S(1)}, f32[2,2,4,1024]{3,2,1,0:T(4,128)S(1)}, u32[]{:S(2)}, u32[]{:S(2)}) collective-permute-start(f32[2,2,4,1024]{3,2,1,0:T(4,128)S(1)} %dynamic-slice_bitcast_fusion.1), channel_id=1, source_target_pairs={{0,32},{32,0},{64,96},{96,64},{128,160},{160,128},{192,224},{224,1... | collective-permute-start | bytes 196616 | tf_op jit(solution)/shard_map/ppermute | solution.py:65
  164.1 4.9 %collective-permute-start.15 = (f32[2,4,1024]{2,1,0:T(4,128)S(1)}, f32[2,4,1024]{2,1,0:T(4,128)S(1)}, u32[]{:S(2)}, u32[]{:S(2)}) collective-permute-start(f32[2,4,1024]{2,1,0:T(4,128)S(1)} %dynamic-slice_bitcast_fusion.3), channel_id=1, source_target_pairs={{0,64},{32,96},{64,0},{96,32},{128,192},{160,224},{192,128},{224,1... | collective-permute-start | bytes 98312 | tf_op jit(solution)/shard_map/ppermute | solution.py:65
  169.1 7.7 %collective-permute-start.16 = (f32[4,1024]{1,0:T(4,128)S(1)}, f32[4,1024]{1,0:T(4,128)S(1)}, u32[]{:S(2)}, u32[]{:S(2)}) collective-permute-start(f32[4,1024]{1,0:T(4,128)S(1)} %dynamic-slice_bitcast_fusion.5), channel_id=1, source_target_pairs={{0,128},{32,160},{64,192},{96,224},{128,0},{160,32},{192,64},{224,... | collective-permute-start | bytes 49160 | tf_op jit(solution)/shard_map/ppermute | solution.py:65
  176.8 7.7 %collective-permute-start.17 = (f32[4,1024]{1,0:T(4,128)S(1)}, f32[4,1024]{1,0:T(4,128)S(1)}, u32[]{:S(2)}, u32[]{:S(2)}) collective-permute-start(f32[4,1024]{1,0:T(4,128)S(1)} %bitcast_add_fusion.8), channel_id=1, source_target_pairs={{0,128},{32,160},{64,192},{96,224},{128,0},{160,32},{192,64},{224,... | collective-permute-start | bytes 49160 | tf_op jit(solution)/shard_map/ppermute | solution.py:48
  184.6 4.9 %collective-permute-start.18 = (f32[2,4,1024]{2,1,0:T(4,128)S(1)}, f32[2,4,1024]{2,1,0:T(4,128)S(1)}, u32[]{:S(2)}, u32[]{:S(2)}) collective-permute-start(f32[2,4,1024]{2,1,0:T(4,128)S(1)} %pad_maximum_fusion.10), channel_id=1, source_target_pairs={{0,64},{32,96},{64,0},{96,32},{128,192},{160,224},{192,128},{224,1... | collective-permute-start | bytes 98312 | tf_op jit(solution)/shard_map/ppermute | solution.py:48
  189.6 4.4 %collective-permute-start.19 = (f32[2,2,4,1024]{3,2,1,0:T(4,128)S(1)}, f32[2,2,4,1024]{3,2,1,0:T(4,128)S(1)}, u32[]{:S(2)}, u32[]{:S(2)}) collective-permute-start(f32[2,2,4,1024]{3,2,1,0:T(4,128)S(1)} %pad_maximum_fusion.8), channel_id=1, source_target_pairs={{0,32},{32,0},{64,96},{96,64},{128,160},{160,128},{192,224},{224,1... | collective-permute-start | bytes 196616 | tf_op jit(solution)/shard_map/ppermute | solution.py:48
Sparse Core Ops, SparseCore 0:
  67.8 90.9 reduce-scatter.1
